TPU v7x, 512 devices: a whole 4x8x8 slice. The times are simulated.
512 devices in a mesh: ply: 8 (over y_lo, x), tile: 64 (over z, y_hi, core).
Axes of the slice: x: 4, y: 8 (y_hi: 4, y_lo: 2; y = y_hi * 2 + y_lo), z: 8, core: 2. Of those that a mesh axis runs over, the one named last changes fastest.
Arguments:
- strain: float32 [4, 3, 16, 16384], P(None, None, None, 'tile'), may hold values from -6 to 6
- case_ids: int32 [4], replicated, may hold values from 0 to 3, each once
- angle_ids: int32 [192], P('ply'), may hold values from 0 to 3
- stiffening: float32 [192, 16, 16384], P('ply', None, 'tile'), may hold values from 0.5 to 8
- interface: float32 [192, 16, 16384], P('ply', None, 'tile'), may hold values from 0.5 to 4
Outputs:
- adjoint: float32 [4, 192, 16, 16384], P(None, 'ply', None, 'tile')
- through: float32 [192, 16, 16384], P('ply', None, 'tile')
Inputs may be any that keep to these rules, and one draw needn't show every extreme that they name: `case_ids`: each of the 4 load states is taken by exactly one load case.
All inputs are finite; a program needn't handle non-finite values.
Results may differ from a plain program's by a relative error of at most 0.0085.
Values sent between devices are 32-bit elements; how exact they have to be, the bound alone decides.
No kernel may reach another device: no remote copies, remote signals or barrier semaphores. Data moves between devices by JAX's collectives and lax.ppermute only.
A program may use at most 64 MiB of HBM per device.

v0:
```python
import jax
import jax.numpy as jnp
from jax import lax
from jax.sharding import PartitionSpec as P

ITERS = 4


relaxation = 2.0 / 3.0
half_root = 0.7071067811865476
fibre_modulus = 1.0
trans_modulus = 0.5
shear_modulus = 0.3
linear_fibre = 0.3
linear_trans = 0.8
square_fibre = 0.5
square_trans = 1.0
square_shear = 0.8
cross_term = -0.35


def passed_along(array, axis, by):
    count = lax.axis_size(axis)
    pairs = [(i, i + by) for i in range(count) if 0 <= i + by < count]
    return lax.ppermute(array, axis, pairs)


def extended(block, sides, width):
    for axis, dim in sides:
        count = lax.axis_size(axis)
        forward = [(i, i + 1) for i in range(count - 1)]
        backward = [(target, source) for source, target in forward]
        low = lax.ppermute(
            lax.slice_in_dim(block, block.shape[dim] - width, None, axis=dim), axis, forward
        )
        high = lax.ppermute(lax.slice_in_dim(block, 0, width, axis=dim), axis, backward)
        block = jnp.concatenate([low, block, high], axis=dim)
    return block


def prefix_2(value, axis, join, neutral):
    count, mine = (lax.axis_size(axis), lax.axis_index(axis))
    pieces = lax.all_gather(value, axis)
    so_far = jnp.full_like(value, 0) + jnp.asarray(neutral, value.dtype)

    def hop(position, so_far):
        longer = join(so_far, pieces[position])
        return jnp.where(position < mine, longer, so_far)

    return lax.fori_loop(0, count - 1, hop, so_far)


def ply_tables(angles):
    one_hot = (angles[:, None] == jnp.arange(4, dtype=jnp.int32)[None, :]).astype(jnp.float32)
    ply_cosine = jnp.sum(
        one_hot * jnp.array([1.0, half_root, half_root, 0.0], jnp.float32)[None, :], axis=1
    )
    ply_sine = jnp.sum(
        one_hot * jnp.array([0.0, half_root, -half_root, 1.0], jnp.float32)[None, :], axis=1
    )
    ply_cosine = ply_cosine.reshape(-1, 1, 1)
    ply_sine = ply_sine.reshape(-1, 1, 1)
    cond_rows = 4.0 * ply_cosine * ply_cosine + ply_sine * ply_sine
    cond_cols = 4.0 * ply_sine * ply_sine + ply_cosine * ply_cosine
    cond_cross = 3.0 * ply_cosine * ply_sine
    return (cond_rows, cond_cols, cond_cross, ply_cosine, ply_sine)


def tsai_wu(strain_x, strain_y, strain_xy, ply_cosine, ply_sine):
    cos_sq = ply_cosine * ply_cosine
    sin_sq = ply_sine * ply_sine
    mixed = ply_cosine * ply_sine
    fibre_strain = cos_sq * strain_x + sin_sq * strain_y + mixed * strain_xy
    trans_strain = sin_sq * strain_x + cos_sq * strain_y - mixed * strain_xy
    shear_strain = 2.0 * mixed * (strain_y - strain_x) + (cos_sq - sin_sq) * strain_xy
    fibre_stress = fibre_modulus * fibre_strain
    trans_stress = trans_modulus * trans_strain
    shear_stress = shear_modulus * shear_strain
    first = linear_fibre + 2.0 * square_fibre * fibre_stress + 2.0 * cross_term * trans_stress
    second = linear_trans + 2.0 * square_trans * trans_stress + 2.0 * cross_term * fibre_stress
    return first + second + 2.0 * square_shear * shear_stress


def sweep(padded, source, stiffening, coupling_up, coupling_down, cond_rows, cond_cols, cond_cross):
    widths = [(0, 0)] * (padded.ndim - 2) + [(1, 1), (0, 0)]
    framed = jnp.pad(padded, widths)
    centre = framed[..., 1:-1, 1:-1, 1:-1]
    along_rows = framed[..., 1:-1, 2:, 1:-1] + framed[..., 1:-1, :-2, 1:-1]
    along_cols = framed[..., 1:-1, 1:-1, 2:] + framed[..., 1:-1, 1:-1, :-2]
    diagonal_pairs = (
        framed[..., 1:-1, 2:, 2:]
        + framed[..., 1:-1, :-2, :-2]
        - framed[..., 1:-1, 2:, :-2]
        - framed[..., 1:-1, :-2, 2:]
    )
    overhead = framed[..., 2:, 1:-1, 1:-1]
    beneath = framed[..., :-2, 1:-1, 1:-1]
    image = (
        cond_rows * (2.0 * centre - along_rows)
        + cond_cols * (2.0 * centre - along_cols)
        - 0.5 * cond_cross * diagonal_pairs
    )
    image = (
        image
        + coupling_up * (centre - overhead)
        + coupling_down * (centre - beneath)
        + stiffening * centre
    )
    diagonal_sum = 2.0 * cond_rows + 2.0 * cond_cols + coupling_up + coupling_down + stiffening
    return centre + relaxation * (source - image) / diagonal_sum


def combine_sum(earlier, later):
    return earlier + later


def body(strain, case_ids, angle_ids, stiffening, interface):
    ply_count = angle_ids.shape[0]
    chosen = jnp.take(strain, case_ids, axis=0)
    cond_rows, cond_cols, cond_cross, ply_cosine, ply_sine = ply_tables(angle_ids)
    source = tsai_wu(
        chosen[:, 0][:, None], chosen[:, 1][:, None], chosen[:, 2][:, None], ply_cosine, ply_sine
    )
    adjoint = jnp.zeros(source.shape, jnp.float32)
    lower_plane = passed_along(interface[-1:], "ply", 1)
    coupling_down = jnp.concatenate([lower_plane, interface[:-1]], axis=0)
    for iteration in range(ITERS):
        padded = extended(adjoint, (("ply", 1), ("tile", 3)), 1)
        adjoint = sweep(
            padded, source, stiffening, interface, coupling_down, cond_rows, cond_cols, cond_cross
        )
    summed = jnp.sum(adjoint * source, axis=0)
    running = jnp.cumsum(summed, axis=0)
    plane_total = running[-1]
    prefix = prefix_2(plane_total, "ply", combine_sum, jnp.zeros_like(plane_total))
    through = (running + prefix[None]) / (ply_count * lax.axis_size("ply"))
    return (adjoint, through)


def solution(mesh):
    return jax.shard_map(
        body,
        mesh=mesh,
        in_specs=(
            P(None, None, None, "tile"),
            P(),
            P("ply"),
            P("ply", None, "tile"),
            P("ply", None, "tile"),
        ),
        out_specs=(P(None, "ply", None, "tile"), P("ply", None, "tile")),
        check_vma=False,
    )
```

profile of v0, /device:TPU:262, one launch (start us, length us, event | category | flops | bytes accessed | tf_op | source)
XLA Modules:
  0.0 188.7 jit_solution(13346259651190175369)
XLA Ops:
  0.7 3.5 %collective-permute-start = (f32[4,1,16,256]{3,2,1,0:T(8,128)S(1)}, f32[4,1,16,256]{3,2,1,0:T(8,128)S(1)}, u32[]{:S(2)}, u32[]{:S(2)}) collective-permute-start(f32[4,1,16,256]{3,2,1,0:T(8,128)S(1)} %broadcast.118), channel_id=1, source_target_pairs={{0,64},{64,128},{128,192},{192,256},{256,320},{320,384},{384,448},... | collective-permute-start | bytes 196616 | tf_op jit(solution)/shard_map/ppermute | solution.py:33
  4.2 2.4 %collective-permute-start.1 = (f32[4,1,16,256]{3,2,1,0:T(8,128)S(1)}, f32[4,1,16,256]{3,2,1,0:T(8,128)S(1)}, u32[]{:S(2)}, u32[]{:S(2)}) collective-permute-start(f32[4,1,16,256]{3,2,1,0:T(8,128)S(1)} %broadcast.118), channel_id=1, source_target_pairs={{64,0},{128,64},{192,128},{256,192},{320,256},{384,320},{448,384},... | collective-permute-start | bytes 196616 | tf_op jit(solution)/shard_map/ppermute | solution.py:36
  7.4 5.5 %collective-permute-start.4 = (f32[1,16,256]{2,1,0:T(8,128)S(1)}, f32[1,16,256]{2,1,0:T(8,128)S(1)}, u32[]{:S(2)}, u32[]{:S(2)}) collective-permute-start(f32[1,16,256]{2,1,0:T(8,128)S(1)} %slice.246), channel_id=1, source_target_pairs={{0,64},{64,128},{128,192},{192,256},{256,320},{320,384},{384,448},... | collective-permute-start | bytes 49160 | tf_op jit(solution)/shard_map/ppermute | solution.py:25
  15.5 0.8 select_reduce_fusion
  17.3 1.5 fusion.84
  18.8 1.7 copy.72
  20.5 1.9 %collective-permute-start.2 = (f32[4,26,16,1]{1,2,3,0:T(8,128)S(1)}, f32[4,26,16,1]{1,2,3,0:T(8,128)S(1)}, u32[]{:S(2)}, u32[]{:S(2)}) collective-permute-start(f32[4,26,16,1]{1,2,3,0:T(8,128)S(1)} %copy.72), channel_id=1, source_target_pairs={{0,1},{1,2},{2,3},{3,4},{4,5},{5,6},{6,7},{7,8},{8,9},{9,10},{10,1... | collective-permute-start | bytes 19976 | tf_op jit(solution)/shard_map/ppermute | solution.py:33
  22.5 1.7 copy.73
  24.1 7.9 %collective-permute-start.3 = (f32[4,26,16,1]{1,2,3,0:T(8,128)S(1)}, f32[4,26,16,1]{1,2,3,0:T(8,128)S(1)}, u32[]{:S(2)}, u32[]{:S(2)}) collective-permute-start(f32[4,26,16,1]{1,2,3,0:T(8,128)S(1)} %copy.73), channel_id=1, source_target_pairs={{1,0},{2,1},{3,2},{4,3},{5,4},{6,5},{7,6},{8,7},{9,8},{10,9},{11,1... | collective-permute-start | bytes 19976 | tf_op jit(solution)/shard_map/ppermute | solution.py:36
  32.0 1.1 pad_maximum_fusion.34
  33.7 1.4 copy.48
  35.2 3.6 %select_maximum_fusion.12 = f32[4,26,18,258]{3,2,1,0:T(8,128)S(1)} fusion(f32[4,26,16,1]{3,2,1,0:T(8,128)} %copy.48, f32[4,26,16,1]{3,2,1,0:T(8,128)S(1)} %copy.47, f32[4,1,16,256]{3,2,1,0:T(8,128)S(1)} %collective-permute-done.1, f32[4,24,16,256]{3,2,1,0:T(8,128)S(1)} %broadcast_in_dim.21, f32[4,1,16,256]{3,2,1,0:T(8,128)S(1)} %collective-permute-done), kind=kLoop, calls=%fused_computation.16 | loop fusion | flops 5795712 | bytes 3649152 | tf_op jit(solution)/shard_map/concatenate | solution.py:37
  38.9 5.9 %fusion.8 = f32[4,24,16,256]{3,2,1,0:T(8,128)S(1)} fusion(f32[4,24,16,256]{3,2,1,0:T(8,128)S(1)} %broadcast_in_dim.21, f32[4,1,16,256]{3,2,1,0:T(8,128)} %copy-done.38, f32[4,1,16,256]{3,2,1,0:T(8,128)} %copy-done.37, f32[4,26,18,258]{3,2,1,0:T(8,128)S(1)} %select_maximum_fusion.12, f32[4,26,16,1]{3,2,1,0:T(8,128)} %copy-done.14, ...), kind=kLoop, calls=%fused_computation.36 | loop fusion | flops 19267584 | bytes 14563072 | tf_op jit(solution)/shard_map/div | solution.py:110
  44.9 1.9 %collective-permute-start.5 = (f32[4,1,16,256]{3,2,1,0:T(8,128)S(1)}, f32[4,1,16,256]{3,2,1,0:T(8,128)S(1)}, u32[]{:S(2)}, u32[]{:S(2)}) collective-permute-start(f32[4,1,16,256]{3,2,1,0:T(8,128)S(1)} %get-tuple-element.129), channel_id=1, source_target_pairs={{0,64},{64,128},{128,192},{192,256},{256,320},{320,384},{384,448},... | collective-permute-start | bytes 196616 | tf_op jit(solution)/shard_map/ppermute | solution.py:33
  46.8 3.9 %collective-permute-start.6 = (f32[4,1,16,256]{3,2,1,0:T(8,128)S(1)}, f32[4,1,16,256]{3,2,1,0:T(8,128)S(1)}, u32[]{:S(2)}, u32[]{:S(2)}) collective-permute-start(f32[4,1,16,256]{3,2,1,0:T(8,128)S(1)} %get-tuple-element.128), channel_id=1, source_target_pairs={{64,0},{128,64},{192,128},{256,192},{320,256},{384,320},{448,384},... | collective-permute-start | bytes 196616 | tf_op jit(solution)/shard_map/ppermute | solution.py:36
  51.0 4.0 %collective-permute-done.6 = f32[4,1,16,256]{3,2,1,0:T(8,128)S(1)} collective-permute-done((f32[4,1,16,256]{3,2,1,0:T(8,128)S(1)}, f32[4,1,16,256]{3,2,1,0:T(8,128)S(1)}, u32[]{:S(2)}, u32[]{:S(2)}) %collective-permute-start.6) | collective-permute-done | bytes 65568 | tf_op jit(solution)/shard_map/ppermute | solution.py:36
  56.1 1.1 copy.74
  57.3 1.9 %collective-permute-start.7 = (f32[4,26,16,1]{1,2,3,0:T(8,128)}, f32[4,26,16,1]{1,2,3,0:T(8,128)S(1)}, u32[]{:S(2)}, u32[]{:S(2)}) collective-permute-start(f32[4,26,16,1]{1,2,3,0:T(8,128)} %copy.74), channel_id=1, source_target_pairs={{0,1},{1,2},{2,3},{3,4},{4,5},{5,6},{6,7},{7,8},{8,9},{9,10},{10,1... | collective-permute-start | bytes 19976 | tf_op jit(solution)/shard_map/ppermute | solution.py:33
  59.7 7.9 %collective-permute-start.8 = (f32[4,26,16,1]{1,2,3,0:T(8,128)S(1)}, f32[4,26,16,1]{1,2,3,0:T(8,128)}, u32[]{:S(2)}, u32[]{:S(2)}) collective-permute-start(f32[4,26,16,1]{1,2,3,0:T(8,128)S(1)} %copy.75), channel_id=1, source_target_pairs={{1,0},{2,1},{3,2},{4,3},{5,4},{6,5},{7,6},{8,7},{9,8},{10,9},{11,1... | collective-permute-start | bytes 19976 | tf_op jit(solution)/shard_map/ppermute | solution.py:36
  68.1 1.0 collective-permute-done.8
  69.1 1.3 copy.54
  70.4 0.9 copy-done.18
  71.4 3.3 %select_maximum_fusion.8 = f32[4,26,18,258]{3,2,1,0:T(8,128)S(1)} fusion(f32[4,26,16,1]{3,2,1,0:T(8,128)S(1)} %copy.54, f32[4,26,16,1]{3,2,1,0:T(8,128)S(1)} %copy.53, f32[4,1,16,256]{3,2,1,0:T(8,128)} %copy-done.46, f32[4,24,16,256]{3,2,1,0:T(8,128)S(1)} %fusion.8, f32[4,1,16,256]{3,2,1,0:T(8,128)} %copy-done.43), kind=kLoop, calls=%fused_computation.12 | loop fusion | flops 5795712 | bytes 3649152 | tf_op jit(solution)/shard_map/concatenate | solution.py:37
  74.9 6.3 %fusion.56 = f32[4,24,16,256]{3,2,1,0:T(8,128)S(1)} fusion(f32[4,24,16,256]{3,2,1,0:T(8,128)S(1)} %fusion.8, f32[4,1,16,256]{3,2,1,0:T(8,128)S(1)} %copy-done.44, f32[4,1,16,256]{3,2,1,0:T(8,128)S(1)} %copy-done.47, f32[4,26,18,258]{3,2,1,0:T(8,128)S(1)} %select_maximum_fusion.8, f32[4,26,16,1]{3,2,1,0:T(8,128)} %copy-done.15, ...), kind=kLoop, calls=%fused_computation.109 | loop fusion | flops 21233664 | bytes 14563072 | tf_op jit(solution)/shard_map/add | solution.py:110
  81.2 1.9 %collective-permute-start.10 = (f32[4,1,16,256]{3,2,1,0:T(8,128)S(1)}, f32[4,1,16,256]{3,2,1,0:T(8,128)S(1)}, u32[]{:S(2)}, u32[]{:S(2)}) collective-permute-start(f32[4,1,16,256]{3,2,1,0:T(8,128)S(1)} %get-tuple-element.126), channel_id=1, source_target_pairs={{64,0},{128,64},{192,128},{256,192},{320,256},{384,320},{448,384},... | collective-permute-start | bytes 196616 | tf_op jit(solution)/shard_map/ppermute | solution.py:36
  83.1 6.0 %collective-permute-start.9 = (f32[4,1,16,256]{3,2,1,0:T(8,128)S(1)}, f32[4,1,16,256]{3,2,1,0:T(8,128)S(1)}, u32[]{:S(2)}, u32[]{:S(2)}) collective-permute-start(f32[4,1,16,256]{3,2,1,0:T(8,128)S(1)} %get-tuple-element.127), channel_id=1, source_target_pairs={{0,64},{64,128},{128,192},{192,256},{256,320},{320,384},{384,448},... | collective-permute-start | bytes 196616 | tf_op jit(solution)/shard_map/ppermute | solution.py:33
  89.4 1.6 collective-permute-done.9
  91.2 1.2 fusion.82
  92.4 1.7 copy.76
  94.0 2.1 %collective-permute-start.11 = (f32[4,26,16,1]{1,2,3,0:T(8,128)S(1)}, f32[4,26,16,1]{1,2,3,0:T(8,128)S(1)}, u32[]{:S(2)}, u32[]{:S(2)}) collective-permute-start(f32[4,26,16,1]{1,2,3,0:T(8,128)S(1)} %copy.76), channel_id=1, source_target_pairs={{0,1},{1,2},{2,3},{3,4},{4,5},{5,6},{6,7},{7,8},{8,9},{9,10},{10,1... | collective-permute-start | bytes 19976 | tf_op jit(solution)/shard_map/ppermute | solution.py:33
  96.6 7.9 %collective-permute-start.12 = (f32[4,26,16,1]{1,2,3,0:T(8,128)S(1)}, f32[4,26,16,1]{1,2,3,0:T(8,128)S(1)}, u32[]{:S(2)}, u32[]{:S(2)}) collective-permute-start(f32[4,26,16,1]{1,2,3,0:T(8,128)S(1)} %copy.77), channel_id=1, source_target_pairs={{1,0},{2,1},{3,2},{4,3},{5,4},{6,5},{7,6},{8,7},{9,8},{10,9},{11,1... | collective-permute-start | bytes 19976 | tf_op jit(solution)/shard_map/ppermute | solution.py:36
  105.0 1.0 collective-permute-done.12
  106.1 1.4 copy.60
  107.6 3.6 %select_maximum_fusion.4 = f32[4,26,18,258]{3,2,1,0:T(8,128)S(1)} fusion(f32[4,26,16,1]{3,2,1,0:T(8,128)} %copy.60, f32[4,26,16,1]{3,2,1,0:T(8,128)S(1)} %copy.59, f32[4,1,16,256]{3,2,1,0:T(8,128)S(1)} %collective-permute-done.10, f32[4,24,16,256]{3,2,1,0:T(8,128)S(1)} %fusion.56, f32[4,1,16,256]{3,2,1,0:T(8,128)S(1)} %collective-permute-done.9), kind=kLoop, calls=%fused_computation.8 | loop fusion | flops 5795712 | bytes 3649152 | tf_op jit(solution)/shard_map/concatenate | solution.py:37
  111.4 6.1 %fusion.37 = f32[4,24,16,256]{3,2,1,0:T(8,128)S(1)} fusion(f32[4,24,16,256]{3,2,1,0:T(8,128)S(1)} %fusion.56, f32[4,1,16,256]{3,2,1,0:T(8,128)} %copy-done.48, f32[4,1,16,256]{3,2,1,0:T(8,128)} %copy-done.45, f32[4,26,18,258]{3,2,1,0:T(8,128)S(1)} %select_maximum_fusion.4, f32[4,26,16,1]{3,2,1,0:T(8,128)} %copy-done.16, f32[4,26,16,1]{3,2,1,0:T(8,128)S(1)} %copy-done.19, ...), kind=kLoop, calls=%fused_computation.78 | loop fusion | flops 21233664 | bytes 14563072 | tf_op jit(solution)/shard_map/add | solution.py:110
  117.5 6.4 %collective-permute-start.13 = (f32[4,1,16,256]{3,2,1,0:T(8,128)S(1)}, f32[4,1,16,256]{3,2,1,0:T(8,128)S(1)}, u32[]{:S(2)}, u32[]{:S(2)}) collective-permute-start(f32[4,1,16,256]{3,2,1,0:T(8,128)S(1)} %get-tuple-element.125), channel_id=1, source_target_pairs={{0,64},{64,128},{128,192},{192,256},{256,320},{320,384},{384,448},... | collective-permute-start | bytes 196616 | tf_op jit(solution)/shard_map/ppermute | solution.py:33
  123.9 1.9 %collective-permute-start.14 = (f32[4,1,16,256]{3,2,1,0:T(8,128)S(1)}, f32[4,1,16,256]{3,2,1,0:T(8,128)S(1)}, u32[]{:S(2)}, u32[]{:S(2)}) collective-permute-start(f32[4,1,16,256]{3,2,1,0:T(8,128)S(1)} %get-tuple-element.124), channel_id=1, source_target_pairs={{64,0},{128,64},{192,128},{256,192},{320,256},{384,320},{448,384},... | collective-permute-start | bytes 196616 | tf_op jit(solution)/shard_map/ppermute | solution.py:36
  125.9 6.3 %collective-permute-done.14 = f32[4,1,16,256]{3,2,1,0:T(8,128)S(1)} collective-permute-done((f32[4,1,16,256]{3,2,1,0:T(8,128)S(1)}, f32[4,1,16,256]{3,2,1,0:T(8,128)S(1)}, u32[]{:S(2)}, u32[]{:S(2)}) %collective-permute-start.14) | collective-permute-done | bytes 65568 | tf_op jit(solution)/shard_map/ppermute | solution.py:36
  133.3 1.1 copy.78
  134.4 1.9 %collective-permute-start.15 = (f32[4,26,16,1]{1,2,3,0:T(8,128)}, f32[4,26,16,1]{1,2,3,0:T(8,128)S(1)}, u32[]{:S(2)}, u32[]{:S(2)}) collective-permute-start(f32[4,26,16,1]{1,2,3,0:T(8,128)} %copy.78), channel_id=1, source_target_pairs={{0,1},{1,2},{2,3},{3,4},{4,5},{5,6},{6,7},{7,8},{8,9},{9,10},{10,1... | collective-permute-start | bytes 19976 | tf_op jit(solution)/shard_map/ppermute | solution.py:33
  136.8 7.9 %collective-permute-start.16 = (f32[4,26,16,1]{1,2,3,0:T(8,128)S(1)}, f32[4,26,16,1]{1,2,3,0:T(8,128)}, u32[]{:S(2)}, u32[]{:S(2)}) collective-permute-start(f32[4,26,16,1]{1,2,3,0:T(8,128)S(1)} %copy.79), channel_id=1, source_target_pairs={{1,0},{2,1},{3,2},{4,3},{5,4},{6,5},{7,6},{8,7},{9,8},{10,9},{11,1... | collective-permute-start | bytes 19976 | tf_op jit(solution)/shard_map/ppermute | solution.py:36
  145.2 1.0 collective-permute-done.16
  146.2 1.3 copy.66
  147.7 3.3 %select_maximum_fusion = f32[4,26,18,258]{3,2,1,0:T(8,128)S(1)} fusion(f32[4,26,16,1]{3,2,1,0:T(8,128)S(1)} %copy.66, f32[4,26,16,1]{3,2,1,0:T(8,128)S(1)} %copy.65, f32[4,1,16,256]{3,2,1,0:T(8,128)} %copy-done.41, f32[4,24,16,256]{3,2,1,0:T(8,128)S(1)} %fusion.37, f32[4,1,16,256]{3,2,1,0:T(8,128)} %copy-done.39), kind=kLoop, calls=%fused_computation.4 | loop fusion | flops 5795712 | bytes 3649152 | tf_op jit(solution)/shard_map/concatenate | solution.py:37
  151.1 5.9 %multiply_reduce_fusion = (f32[24,16,256]{2,1,0:T(8,128)S(1)}, f32[4,24,16,256]{3,2,1,0:T(8,128)}) fusion(f32[24]{0:T(128)S(1)} %copy-done.54, f32[4,16,256]{2,1,0:T(8,128)S(1)} %copy-done.27, f32[24]{0:T(128)S(1)} %copy-done.64, f32[4,16,256]{2,1,0:T(8,128)S(1)} %copy-done.31, f32[24]{0:T(128)S(1)} %copy-done.68, f32[4,16,256]{2,1,0:T(8,128)S(1)} %copy-done.35, ...), kind=kLoop, calls=%fused_computation.150 | loop fusion | flops 21921792 | bytes 14956288 | tf_op jit(solution)/shard_map/reduce_sum | solution.py:132
  157.0 2.4 %fusion.88 = f32[24,16,256]{2,1,0:T(8,128)S(1)} fusion(f32[24,16,256]{2,1,0:T(8,128)S(1)} %get-tuple-element.109), kind=kOutput, calls=%fused_computation.182 | output fusion | flops 2260992 | bytes 786432 | tf_op jit(solution)/shard_map/jit(cumsum)/reduce_window_sum | solution.py:133
  159.5 28.2 %all_gather.3 = f32[8,16,256]{2,1,0:T(8,128)S(1)} all-gather(f32[1,16,256]{2,1,0:T(8,128)S(1)} %slice.335), channel_id=1, replica_groups=mesh['ply'=8,'tile'=64] {'ply'}, dimensions={0}, use_global_device_ids=true | all-gather | bytes 147456 | tf_op jit(solution)/shard_map/all_gather | solution.py:43
  187.9 0.8 add_multiply_fusion
  (194 shorter events, 11.5 us)
Async XLA Ops:
  0.6 13.6 %copy-start = (f32[4,3,16,256]{3,2,1,0:T(8,128)S(1)}, f32[4,3,16,256]{3,2,1,0:T(8,128)}, u32[]{:S(2)}) copy-start(f32[4,3,16,256]{3,2,1,0:T(8,128)} %param.9) | copy-start | bytes 589828
  0.7 16.3 %collective-permute-start = (f32[4,1,16,256]{3,2,1,0:T(8,128)S(1)}, f32[4,1,16,256]{3,2,1,0:T(8,128)S(1)}, u32[]{:S(2)}, u32[]{:S(2)}) collective-permute-start(f32[4,1,16,256]{3,2,1,0:T(8,128)S(1)} %broadcast.118), channel_id=1, source_target_pairs={{0,64},{64,128},{128,192},{192,256},{256,320},{320,384},{384,448},... | collective-permute-start | bytes 196616 | tf_op jit(solution)/shard_map/ppermute | solution.py:33
  4.2 12.8 %collective-permute-start.1 = (f32[4,1,16,256]{3,2,1,0:T(8,128)S(1)}, f32[4,1,16,256]{3,2,1,0:T(8,128)S(1)}, u32[]{:S(2)}, u32[]{:S(2)}) collective-permute-start(f32[4,1,16,256]{3,2,1,0:T(8,128)S(1)} %broadcast.118), channel_id=1, source_target_pairs={{64,0},{128,64},{192,128},{256,192},{320,256},{384,320},{448,384},... | collective-permute-start | bytes 196616 | tf_op jit(solution)/shard_map/ppermute | solution.py:36
  7.4 24.6 %collective-permute-start.4 = (f32[1,16,256]{2,1,0:T(8,128)S(1)}, f32[1,16,256]{2,1,0:T(8,128)S(1)}, u32[]{:S(2)}, u32[]{:S(2)}) collective-permute-start(f32[1,16,256]{2,1,0:T(8,128)S(1)} %slice.246), channel_id=1, source_target_pairs={{0,64},{64,128},{128,192},{192,256},{256,320},{320,384},{384,448},... | collective-permute-start | bytes 49160 | tf_op jit(solution)/shard_map/ppermute | solution.py:25
  15.5 23.3 %copy-start.24 = (f32[4,16,256]{2,1,0:T(8,128)}, f32[4,16,256]{2,1,0:T(8,128)S(1)}, u32[]{:S(2)}) copy-start(f32[4,16,256]{2,1,0:T(8,128)S(1)} %get-tuple-element.134) | copy-start | bytes 196612
  15.5 23.3 %copy-start.28 = (f32[4,16,256]{2,1,0:T(8,128)}, f32[4,16,256]{2,1,0:T(8,128)S(1)}, u32[]{:S(2)}) copy-start(f32[4,16,256]{2,1,0:T(8,128)S(1)} %get-tuple-element.135) | copy-start | bytes 196612
  16.9 94.3 %copy-start.49 = (f32[24]{0:T(128)}, f32[24]{0:T(128)S(1)}, u32[]{:S(2)}) copy-start(f32[24]{0:T(128)S(1)} %get-tuple-element.137) | copy-start | bytes 292
  16.9 94.3 %copy-start.51 = (f32[24]{0:T(128)}, f32[24]{0:T(128)S(1)}, u32[]{:S(2)}) copy-start(f32[24]{0:T(128)S(1)} %get-tuple-element.138) | copy-start | bytes 292
  16.9 94.3 %copy-start.53 = (f32[24]{0:T(128)}, f32[24]{0:T(128)S(1)}, u32[]{:S(2)}) copy-start(f32[24]{0:T(128)S(1)} %get-tuple-element.139) | copy-start | bytes 292
  16.9 94.3 %copy-start.55 = (f32[24]{0:T(128)}, f32[24]{0:T(128)S(1)}, u32[]{:S(2)}) copy-start(f32[24]{0:T(128)S(1)} %get-tuple-element.141) | copy-start | bytes 292
  17.0 18.1 %copy-start.37 = (f32[4,1,16,256]{3,2,1,0:T(8,128)}, f32[4,1,16,256]{3,2,1,0:T(8,128)S(1)}, u32[]{:S(2)}) copy-start(f32[4,1,16,256]{3,2,1,0:T(8,128)S(1)} %collective-permute-done) | copy-start | bytes 196612
  17.0 18.1 %copy-start.38 = (f32[4,1,16,256]{3,2,1,0:T(8,128)}, f32[4,1,16,256]{3,2,1,0:T(8,128)S(1)}, u32[]{:S(2)}) copy-start(f32[4,1,16,256]{3,2,1,0:T(8,128)S(1)} %collective-permute-done.1) | copy-start | bytes 196612
  18.8 13.2 %copy-start.1 = (f32[24,16,256]{2,1,0:T(8,128)S(1)}, f32[24,16,256]{2,1,0:T(8,128)}, u32[]{:S(2)}) copy-start(f32[24,16,256]{2,1,0:T(8,128)} %param.13) | copy-start | bytes 1179652
  18.8 13.2 %slice-start = ((f32[24,16,256]{2,1,0:T(8,128)}), f32[23,16,256]{2,1,0:T(8,128)S(1)}, s32[]{:S(2)}) async-start(f32[24,16,256]{2,1,0:T(8,128)} %param.13), calls=%async_computation | async-start | bytes 753664 | tf_op jit(solution)/shard_map/slice | solution.py:126
  18.8 13.2 %copy-start.20 = (f32[24,16,256]{2,1,0:T(8,128)S(1)}, f32[24,16,256]{2,1,0:T(8,128)}, u32[]{:S(2)}) copy-start(f32[24,16,256]{2,1,0:T(8,128)} %param.12) | copy-start | bytes 1179652
  20.5 12.6 %collective-permute-start.2 = (f32[4,26,16,1]{1,2,3,0:T(8,128)S(1)}, f32[4,26,16,1]{1,2,3,0:T(8,128)S(1)}, u32[]{:S(2)}, u32[]{:S(2)}) collective-permute-start(f32[4,26,16,1]{1,2,3,0:T(8,128)S(1)} %copy.72), channel_id=1, source_target_pairs={{0,1},{1,2},{2,3},{3,4},{4,5},{5,6},{6,7},{7,8},{8,9},{9,10},{10,1... | collective-permute-start | bytes 19976 | tf_op jit(solution)/shard_map/ppermute | solution.py:33
  24.1 9.5 %collective-permute-start.3 = (f32[4,26,16,1]{1,2,3,0:T(8,128)S(1)}, f32[4,26,16,1]{1,2,3,0:T(8,128)S(1)}, u32[]{:S(2)}, u32[]{:S(2)}) collective-permute-start(f32[4,26,16,1]{1,2,3,0:T(8,128)S(1)} %copy.73), channel_id=1, source_target_pairs={{1,0},{2,1},{3,2},{4,3},{5,4},{6,5},{7,6},{8,7},{9,8},{10,9},{11,1... | collective-permute-start | bytes 19976 | tf_op jit(solution)/shard_map/ppermute | solution.py:36
  33.6 5.1 %copy-start.14 = (f32[4,26,16,1]{3,2,1,0:T(8,128)}, f32[4,26,16,1]{3,2,1,0:T(8,128)S(1)}, u32[]{:S(2)}) copy-start(f32[4,26,16,1]{3,2,1,0:T(8,128)S(1)} %copy.47) | copy-start | bytes 19972
  35.1 3.8 %copy-start.10 = (f32[24,16,256]{2,1,0:T(8,128)S(1)}, f32[24,16,256]{2,1,0:T(8,128)}, u32[]{:S(2)}) copy-start(f32[24,16,256]{2,1,0:T(8,128)} %get-tuple-element.131) | copy-start | bytes 1179652
  35.1 3.8 %copy-start.17 = (f32[4,26,16,1]{3,2,1,0:T(8,128)S(1)}, f32[4,26,16,1]{3,2,1,0:T(8,128)}, u32[]{:S(2)}) copy-start(f32[4,26,16,1]{3,2,1,0:T(8,128)} %copy.48) | copy-start | bytes 19972
  44.9 6.2 %collective-permute-start.5 = (f32[4,1,16,256]{3,2,1,0:T(8,128)S(1)}, f32[4,1,16,256]{3,2,1,0:T(8,128)S(1)}, u32[]{:S(2)}, u32[]{:S(2)}) collective-permute-start(f32[4,1,16,256]{3,2,1,0:T(8,128)S(1)} %get-tuple-element.129), channel_id=1, source_target_pairs={{0,64},{64,128},{128,192},{192,256},{256,320},{320,384},{384,448},... | collective-permute-start | bytes 196616 | tf_op jit(solution)/shard_map/ppermute | solution.py:33
  46.8 8.3 %collective-permute-start.6 = (f32[4,1,16,256]{3,2,1,0:T(8,128)S(1)}, f32[4,1,16,256]{3,2,1,0:T(8,128)S(1)}, u32[]{:S(2)}, u32[]{:S(2)}) collective-permute-start(f32[4,1,16,256]{3,2,1,0:T(8,128)S(1)} %get-tuple-element.128), channel_id=1, source_target_pairs={{64,0},{128,64},{192,128},{256,192},{320,256},{384,320},{448,384},... | collective-permute-start | bytes 196616 | tf_op jit(solution)/shard_map/ppermute | solution.py:36
  51.0 4.0 %copy-start.43 = (f32[4,1,16,256]{3,2,1,0:T(8,128)}, f32[4,1,16,256]{3,2,1,0:T(8,128)S(1)}, u32[]{:S(2)}) copy-start(f32[4,1,16,256]{3,2,1,0:T(8,128)S(1)} %collective-permute-done.5) | copy-start | bytes 196612
  57.3 10.3 %collective-permute-start.7 = (f32[4,26,16,1]{1,2,3,0:T(8,128)}, f32[4,26,16,1]{1,2,3,0:T(8,128)S(1)}, u32[]{:S(2)}, u32[]{:S(2)}) collective-permute-start(f32[4,26,16,1]{1,2,3,0:T(8,128)} %copy.74), channel_id=1, source_target_pairs={{0,1},{1,2},{2,3},{3,4},{4,5},{5,6},{6,7},{7,8},{8,9},{9,10},{10,1... | collective-permute-start | bytes 19976 | tf_op jit(solution)/shard_map/ppermute | solution.py:33
  59.7 9.4 %collective-permute-start.8 = (f32[4,26,16,1]{1,2,3,0:T(8,128)S(1)}, f32[4,26,16,1]{1,2,3,0:T(8,128)}, u32[]{:S(2)}, u32[]{:S(2)}) collective-permute-start(f32[4,26,16,1]{1,2,3,0:T(8,128)S(1)} %copy.75), channel_id=1, source_target_pairs={{1,0},{2,1},{3,2},{4,3},{5,4},{6,5},{7,6},{8,7},{9,8},{10,9},{11,1... | collective-permute-start | bytes 19976 | tf_op jit(solution)/shard_map/ppermute | solution.py:36
  81.2 8.3 %collective-permute-start.10 = (f32[4,1,16,256]{3,2,1,0:T(8,128)S(1)}, f32[4,1,16,256]{3,2,1,0:T(8,128)S(1)}, u32[]{:S(2)}, u32[]{:S(2)}) collective-permute-start(f32[4,1,16,256]{3,2,1,0:T(8,128)S(1)} %get-tuple-element.126), channel_id=1, source_target_pairs={{64,0},{128,64},{192,128},{256,192},{320,256},{384,320},{448,384},... | collective-permute-start | bytes 196616 | tf_op jit(solution)/shard_map/ppermute | solution.py:36
  83.1 7.9 %collective-permute-start.9 = (f32[4,1,16,256]{3,2,1,0:T(8,128)S(1)}, f32[4,1,16,256]{3,2,1,0:T(8,128)S(1)}, u32[]{:S(2)}, u32[]{:S(2)}) collective-permute-start(f32[4,1,16,256]{3,2,1,0:T(8,128)S(1)} %get-tuple-element.127), channel_id=1, source_target_pairs={{0,64},{64,128},{128,192},{192,256},{256,320},{320,384},{384,448},... | collective-permute-start | bytes 196616 | tf_op jit(solution)/shard_map/ppermute | solution.py:33
  89.4 18.0 %copy-start.45 = (f32[4,1,16,256]{3,2,1,0:T(8,128)}, f32[4,1,16,256]{3,2,1,0:T(8,128)S(1)}, u32[]{:S(2)}) copy-start(f32[4,1,16,256]{3,2,1,0:T(8,128)S(1)} %collective-permute-done.10) | copy-start | bytes 196612
  91.0 16.4 %copy-start.48 = (f32[4,1,16,256]{3,2,1,0:T(8,128)}, f32[4,1,16,256]{3,2,1,0:T(8,128)S(1)}, u32[]{:S(2)}) copy-start(f32[4,1,16,256]{3,2,1,0:T(8,128)S(1)} %collective-permute-done.9) | copy-start | bytes 196612
  94.0 10.5 %collective-permute-start.11 = (f32[4,26,16,1]{1,2,3,0:T(8,128)S(1)}, f32[4,26,16,1]{1,2,3,0:T(8,128)S(1)}, u32[]{:S(2)}, u32[]{:S(2)}) collective-permute-start(f32[4,26,16,1]{1,2,3,0:T(8,128)S(1)} %copy.76), channel_id=1, source_target_pairs={{0,1},{1,2},{2,3},{3,4},{4,5},{5,6},{6,7},{7,8},{8,9},{9,10},{10,1... | collective-permute-start | bytes 19976 | tf_op jit(solution)/shard_map/ppermute | solution.py:33
  96.6 9.4 %collective-permute-start.12 = (f32[4,26,16,1]{1,2,3,0:T(8,128)S(1)}, f32[4,26,16,1]{1,2,3,0:T(8,128)S(1)}, u32[]{:S(2)}, u32[]{:S(2)}) collective-permute-start(f32[4,26,16,1]{1,2,3,0:T(8,128)S(1)} %copy.77), channel_id=1, source_target_pairs={{1,0},{2,1},{3,2},{4,3},{5,4},{6,5},{7,6},{8,7},{9,8},{10,9},{11,1... | collective-permute-start | bytes 19976 | tf_op jit(solution)/shard_map/ppermute | solution.py:36
  107.5 3.8 %copy-start.4 = (f32[24,16,256]{2,1,0:T(8,128)S(1)}, f32[24,16,256]{2,1,0:T(8,128)}, u32[]{:S(2)}) copy-start(f32[24,16,256]{2,1,0:T(8,128)} %param.13) | copy-start | bytes 1179652
  107.5 3.8 %copy-start.8 = (f32[24,16,256]{2,1,0:T(8,128)S(1)}, f32[24,16,256]{2,1,0:T(8,128)}, u32[]{:S(2)}) copy-start(f32[24,16,256]{2,1,0:T(8,128)} %get-tuple-element.130) | copy-start | bytes 1179652
  107.5 3.8 %copy-start.12 = (f32[24,16,256]{2,1,0:T(8,128)S(1)}, f32[24,16,256]{2,1,0:T(8,128)}, u32[]{:S(2)}) copy-start(f32[24,16,256]{2,1,0:T(8,128)} %get-tuple-element.131) | copy-start | bytes 1179652
  107.5 3.8 %copy-start.19 = (f32[4,26,16,1]{3,2,1,0:T(8,128)S(1)}, f32[4,26,16,1]{3,2,1,0:T(8,128)}, u32[]{:S(2)}) copy-start(f32[4,26,16,1]{3,2,1,0:T(8,128)} %copy.60) | copy-start | bytes 19972
  107.5 3.8 %copy-start.22 = (f32[24,16,256]{2,1,0:T(8,128)S(1)}, f32[24,16,256]{2,1,0:T(8,128)}, u32[]{:S(2)}) copy-start(f32[24,16,256]{2,1,0:T(8,128)} %param.12) | copy-start | bytes 1179652
  107.5 3.8 %copy-start.26 = (f32[4,16,256]{2,1,0:T(8,128)S(1)}, f32[4,16,256]{2,1,0:T(8,128)}, u32[]{:S(2)}) copy-start(f32[4,16,256]{2,1,0:T(8,128)} %copy-done.24) | copy-start | bytes 196612
  107.5 3.8 %copy-start.30 = (f32[4,16,256]{2,1,0:T(8,128)S(1)}, f32[4,16,256]{2,1,0:T(8,128)}, u32[]{:S(2)}) copy-start(f32[4,16,256]{2,1,0:T(8,128)} %copy-done.28) | copy-start | bytes 196612
  107.5 3.8 %copy-start.34 = (f32[4,16,256]{2,1,0:T(8,128)S(1)}, f32[4,16,256]{2,1,0:T(8,128)}, u32[]{:S(2)}) copy-start(f32[4,16,256]{2,1,0:T(8,128)} %get-tuple-element.136) | copy-start | bytes 196612
  107.5 3.8 %copy-start.59 = (f32[24]{0:T(128)S(1)}, f32[24]{0:T(128)}, u32[]{:S(2)}) copy-start(f32[24]{0:T(128)} %get-tuple-element.142) | copy-start | bytes 292
  107.6 3.8 %copy-start.63 = (f32[24]{0:T(128)S(1)}, f32[24]{0:T(128)}, u32[]{:S(2)}) copy-start(f32[24]{0:T(128)} %get-tuple-element.143) | copy-start | bytes 292
  107.6 3.8 %copy-start.67 = (f32[24]{0:T(128)S(1)}, f32[24]{0:T(128)}, u32[]{:S(2)}) copy-start(f32[24]{0:T(128)} %get-tuple-element.144) | copy-start | bytes 292
  107.6 3.8 %copy-start.71 = (f32[24]{0:T(128)S(1)}, f32[24]{0:T(128)}, u32[]{:S(2)}) copy-start(f32[24]{0:T(128)} %get-tuple-element.145) | copy-start | bytes 292
  117.5 8.3 %collective-permute-start.13 = (f32[4,1,16,256]{3,2,1,0:T(8,128)S(1)}, f32[4,1,16,256]{3,2,1,0:T(8,128)S(1)}, u32[]{:S(2)}, u32[]{:S(2)}) collective-permute-start(f32[4,1,16,256]{3,2,1,0:T(8,128)S(1)} %get-tuple-element.125), channel_id=1, source_target_pairs={{0,64},{64,128},{128,192},{192,256},{256,320},{320,384},{384,448},... | collective-permute-start | bytes 196616 | tf_op jit(solution)/shard_map/ppermute | solution.py:33
  123.9 8.3 %collective-permute-start.14 = (f32[4,1,16,256]{3,2,1,0:T(8,128)S(1)}, f32[4,1,16,256]{3,2,1,0:T(8,128)S(1)}, u32[]{:S(2)}, u32[]{:S(2)}) collective-permute-start(f32[4,1,16,256]{3,2,1,0:T(8,128)S(1)} %get-tuple-element.124), channel_id=1, source_target_pairs={{64,0},{128,64},{192,128},{256,192},{320,256},{384,320},{448,384},... | collective-permute-start | bytes 196616 | tf_op jit(solution)/shard_map/ppermute | solution.py:36
  125.9 6.3 %copy-start.39 = (f32[4,1,16,256]{3,2,1,0:T(8,128)}, f32[4,1,16,256]{3,2,1,0:T(8,128)S(1)}, u32[]{:S(2)}) copy-start(f32[4,1,16,256]{3,2,1,0:T(8,128)S(1)} %collective-permute-done.13) | copy-start | bytes 196612
  134.4 10.3 %collective-permute-start.15 = (f32[4,26,16,1]{1,2,3,0:T(8,128)}, f32[4,26,16,1]{1,2,3,0:T(8,128)S(1)}, u32[]{:S(2)}, u32[]{:S(2)}) collective-permute-start(f32[4,26,16,1]{1,2,3,0:T(8,128)} %copy.78), channel_id=1, source_target_pairs={{0,1},{1,2},{2,3},{3,4},{4,5},{5,6},{6,7},{7,8},{8,9},{9,10},{10,1... | collective-permute-start | bytes 19976 | tf_op jit(solution)/shard_map/ppermute | solution.py:33
  136.8 9.4 %collective-permute-start.16 = (f32[4,26,16,1]{1,2,3,0:T(8,128)S(1)}, f32[4,26,16,1]{1,2,3,0:T(8,128)}, u32[]{:S(2)}, u32[]{:S(2)}) collective-permute-start(f32[4,26,16,1]{1,2,3,0:T(8,128)S(1)} %copy.79), channel_id=1, source_target_pairs={{1,0},{2,1},{3,2},{4,3},{5,4},{6,5},{7,6},{8,7},{9,8},{10,9},{11,1... | collective-permute-start | bytes 19976 | tf_op jit(solution)/shard_map/ppermute | solution.py:36
  (43 other events, 140.2 us)
where the time goes:
time: 190 us; the launch traced here: 189 us
  starting transfers between devices  72.8 us (38%)
  other arithmetic  46.4 us (24%)
  blocking collectives  28.2 us (15%)
  local copies, waits for them, and re-layouts  23.5 us (12%)
  waiting for transfers between devices  15.6 us (8%)
  between operations  1.98 us (1%)
    ppermute x8, starting transfers between devices, extended(): lax.ppermute(lax.slice_in_dim(block, 0, width, axis=dim), axis, backward)  41.6 us
    all_gather x1, blocking collectives, prefix_2(): pieces = lax.all_gather(value, axis)  28.2 us
    ppermute x8, starting transfers between devices, extended(): lax.ppermute(lax.slice_in_dim(block, block.shape[dim] - width, None, axis...  25.7 us
    concatenate x8, other arithmetic, extended(): block = jnp.concatenate([low, block, high], axis=dim)  14.3 us
    ppermute x8, waiting for transfers between devices, extended(): lax.ppermute(lax.slice_in_dim(block, 0, width, axis=dim), axis, backward)  13.7 us
    add x2, other arithmetic, sweep(): return centre + relaxation * (source - image) / diagonal_sum  12.4 us
    unnamed x154, local copies, waits for them, and re-layouts  11.3 us
    div x1, other arithmetic, sweep(): return centre + relaxation * (source - image) / diagonal_sum  5.93 us
  transfers between devices with their start and end apart: 17, of which 8 were waited for; matrix products, arithmetic and copies ran while one was open for 8% of the time, Pallas kernels for 0%

commit v1 on v0

--- a/solution.py
+++ b/solution.py
@@ -25,29 +25,11 @@
     return lax.ppermute(array, axis, pairs)
 
 
-def extended(block, sides, width):
-    for axis, dim in sides:
-        count = lax.axis_size(axis)
-        forward = [(i, i + 1) for i in range(count - 1)]
-        backward = [(target, source) for source, target in forward]
-        low = lax.ppermute(
-            lax.slice_in_dim(block, block.shape[dim] - width, None, axis=dim), axis, forward
-        )
-        high = lax.ppermute(lax.slice_in_dim(block, 0, width, axis=dim), axis, backward)
-        block = jnp.concatenate([low, block, high], axis=dim)
-    return block
-
-
-def prefix_2(value, axis, join, neutral):
-    count, mine = (lax.axis_size(axis), lax.axis_index(axis))
-    pieces = lax.all_gather(value, axis)
-    so_far = jnp.full_like(value, 0) + jnp.asarray(neutral, value.dtype)
-
-    def hop(position, so_far):
-        longer = join(so_far, pieces[position])
-        return jnp.where(position < mine, longer, so_far)
-
-    return lax.fori_loop(0, count - 1, hop, so_far)
+def with_halos(block, axis, dim, below, above):
+    size = block.shape[dim]
+    low = passed_along(lax.slice_in_dim(block, size - below, size, axis=dim), axis, 1)
+    high = passed_along(lax.slice_in_dim(block, 0, above, axis=dim), axis, -1)
+    return jnp.concatenate([low, block, high], axis=dim)
 
 
 def ply_tables(angles):
@@ -110,30 +92,86 @@
     return centre + relaxation * (source - image) / diagonal_sum
 
 
-def combine_sum(earlier, later):
-    return earlier + later
+def trim(array, by, ply_dim, col_dim):
+    if by == 0:
+        return array
+    array = lax.slice_in_dim(array, by, array.shape[ply_dim] - by, axis=ply_dim)
+    return lax.slice_in_dim(array, by, array.shape[col_dim] - by, axis=col_dim)
 
 
 def body(strain, case_ids, angle_ids, stiffening, interface):
-    ply_count = angle_ids.shape[0]
+    halo = ITERS - 1
+    ply_local = angle_ids.shape[0]
+    col_local = stiffening.shape[2]
+    ply_count = lax.axis_size("ply")
+    tile_count = lax.axis_size("tile")
+    cases = case_ids.shape[0]
     chosen = jnp.take(strain, case_ids, axis=0)
-    cond_rows, cond_cols, cond_cross, ply_cosine, ply_sine = ply_tables(angle_ids)
-    source = tsai_wu(
-        chosen[:, 0][:, None], chosen[:, 1][:, None], chosen[:, 2][:, None], ply_cosine, ply_sine
+    rows = chosen.shape[2]
+
+    packed = jnp.concatenate(
+        [chosen.reshape(cases * 3, rows, col_local), stiffening, interface], axis=0
     )
-    adjoint = jnp.zeros(source.shape, jnp.float32)
-    lower_plane = passed_along(interface[-1:], "ply", 1)
-    coupling_down = jnp.concatenate([lower_plane, interface[:-1]], axis=0)
-    for iteration in range(ITERS):
-        padded = extended(adjoint, (("ply", 1), ("tile", 3)), 1)
+    packed = with_halos(packed, "tile", 2, halo, halo)
+    width = col_local + 2 * halo
+    strain_e = packed[: cases * 3].reshape(cases, 3, rows, width)
+    stiff_c = packed[cases * 3 : cases * 3 + ply_local]
+    inter_c = packed[cases * 3 + ply_local :]
+    below = passed_along(
+        jnp.concatenate([stiff_c[ply_local - halo :], inter_c[ply_local - halo - 1 :]], axis=0),
+        "ply",
+        1,
+    )
+    above = passed_along(jnp.concatenate([stiff_c[:halo], inter_c[:halo]], axis=0), "ply", -1)
+    angles = with_halos(angle_ids, "ply", 0, halo, halo)
+    stiff_e = jnp.concatenate([below[:halo], stiff_c, above[:halo]], axis=0)
+    inter_all = jnp.concatenate([below[halo:], inter_c, above[halo:]], axis=0)
+    up_e = inter_all[1:]
+    down_e = inter_all[:-1]
+
+    cond_rows, cond_cols, cond_cross, ply_cosine, ply_sine = ply_tables(angles)
+    source_e = tsai_wu(
+        strain_e[:, 0][:, None],
+        strain_e[:, 1][:, None],
+        strain_e[:, 2][:, None],
+        ply_cosine,
+        ply_sine,
+    )
+    ply_at = lax.axis_index("ply") * ply_local - halo + jnp.arange(ply_local + 2 * halo)
+    col_at = lax.axis_index("tile") * col_local - halo + jnp.arange(width)
+    inside = (
+        ((ply_at >= 0) & (ply_at < ply_local * ply_count))[:, None, None]
+        & ((col_at >= 0) & (col_at < col_local * tile_count))[None, None, :]
+    ).astype(jnp.float32)
+
+    diagonal_sum = 2.0 * cond_rows + 2.0 * cond_cols + up_e + down_e + stiff_e
+    adjoint = relaxation * source_e / diagonal_sum * inside
+    for iteration in range(1, ITERS):
+        by = iteration
         adjoint = sweep(
-            padded, source, stiffening, interface, coupling_down, cond_rows, cond_cols, cond_cross
+            adjoint,
+            trim(source_e, by, 1, 3),
+            trim(stiff_e, by, 0, 2),
+            trim(up_e, by, 0, 2),
+            trim(down_e, by, 0, 2),
+            cond_rows[by : cond_rows.shape[0] - by],
+            cond_cols[by : cond_cols.shape[0] - by],
+            cond_cross[by : cond_cross.shape[0] - by],
         )
+        if iteration < ITERS - 1:
+            adjoint = adjoint * trim(inside, by, 0, 2)
+    source = trim(source_e, halo, 1, 3)
     summed = jnp.sum(adjoint * source, axis=0)
     running = jnp.cumsum(summed, axis=0)
-    plane_total = running[-1]
-    prefix = prefix_2(plane_total, "ply", combine_sum, jnp.zeros_like(plane_total))
-    through = (running + prefix[None]) / (ply_count * lax.axis_size("ply"))
+    inclusive = running[-1]
+    prefix = jnp.zeros_like(inclusive)
+    shift = 1
+    while shift < ply_count:
+        arrived = passed_along(inclusive, "ply", shift)
+        prefix = prefix + arrived
+        inclusive = inclusive + arrived
+        shift *= 2
+    through = (running + prefix[None]) / (ply_local * ply_count)
     return (adjoint, through)
 
 

time: 190 us -> 98.5 us (0.52)
  the two profiles are of different devices: /device:TPU:262 before, /device:TPU:448 now
where the time goes in v1:
time: 98.5 us; the launch traced here: 97.2 us
  starting transfers between devices  40.8 us (41%)
  other arithmetic  38.1 us (39%)
  waiting for transfers between devices  16 us (16%)
  local copies, waits for them, and re-layouts  1.35 us (1%)
    ppermute x9, starting transfers between devices, passed_along(): return lax.ppermute(array, axis, pairs)  40.8 us
    mul x2, other arithmetic, body(): adjoint = adjoint * trim(inside, by, 0, 2)  16.9 us
    ppermute x9, waiting for transfers between devices, passed_along(): return lax.ppermute(array, axis, pairs)  16 us
    reduce_sum x1, other arithmetic, body(): summed = jnp.sum(adjoint * source, axis=0)  5.02 us
    mul x1, other arithmetic, body(): adjoint = relaxation * source_e / diagonal_sum * inside  3.67 us
    add x2, other arithmetic, sweep(): 2.0 * cond_rows + 2.0 * cond_cols + coupling_up + coupling_down + stiffening  3.15 us
    another operation x1, other arithmetic, body(): running = jnp.cumsum(summed, axis=0)  2.39 us
  transfers between devices with their start and end apart: 9, of which 8 were waited for; matrix products, arithmetic and copies ran while one was open for 1% of the time, Pallas kernels for 0%

profile of v1, /device:TPU:448, one launch (start us, length us, event | category | flops | bytes accessed | tf_op | source)
XLA Modules:
  0.0 97.2 jit_solution(17375024205578906720)
XLA Ops:
  0.7 0.8 compare_select_fusion
  1.5 0.7 compare_and_fusion.1
  2.1 0.1 broadcast_in_dim.16
  2.2 0.1 broadcast_in_dim.17
  2.3 0.6 gather_fusion
  2.9 0.1 bitcast_select_fusion
  3.0 1.2 %pad_maximum_fusion.1 = f32[60,16,256]{2,1,0:T(8,128)S(1)} fusion(f32[24,16,256]{2,1,0:T(8,128)} %param.11, f32[24,16,256]{2,1,0:T(8,128)} %param.10, f32[12,16,256]{2,1,0:T(8,128)S(1)} %bitcast_select_fusion), kind=kLoop, calls=%fused_computation.96 | loop fusion | flops 491520 | bytes 1966080 | tf_op jit(solution)/shard_map/concatenate | solution.py:112
  4.2 0.2 fusion.95
  4.4 5.6 %collective-permute-start.3 = (f32[60,16,3]{2,1,0:T(8,128)S(1)}, f32[60,16,3]{2,1,0:T(8,128)S(1)}, u32[]{:S(2)}, u32[]{:S(2)}) collective-permute-start(f32[60,16,3]{2,1,0:T(8,128)S(1)} %get-tuple-element.15), channel_id=1, source_target_pairs={{1,0},{2,1},{3,2},{4,3},{5,4},{6,5},{7,6},{8,7},{9,8},{10,9},{11,1... | collective-permute-start | bytes 34568 | tf_op jit(solution)/shard_map/ppermute | solution.py:25
  9.9 1.9 %collective-permute-start.2 = (f32[60,16,3]{2,1,0:T(8,128)S(1)}, f32[60,16,3]{2,1,0:T(8,128)S(1)}, u32[]{:S(2)}, u32[]{:S(2)}) collective-permute-start(f32[60,16,3]{2,1,0:T(8,128)S(1)} %get-tuple-element.14), channel_id=1, source_target_pairs={{0,1},{1,2},{2,3},{3,4},{4,5},{5,6},{6,7},{7,8},{8,9},{9,10},{10,1... | collective-permute-start | bytes 34568 | tf_op jit(solution)/shard_map/ppermute | solution.py:25
  12.0 1.3 %collective-permute-start.1 = (s32[3]{0:T(128)S(1)}, s32[3]{0:T(128)S(1)}, u32[]{:S(2)}, u32[]{:S(2)}) collective-permute-start(s32[3]{0:T(128)S(1)} %get-tuple-element.50), channel_id=1, source_target_pairs={{64,0},{128,64},{192,128},{256,192},{320,256},{384,320},{448,384},... | collective-permute-start | bytes 44 | tf_op jit(solution)/shard_map/ppermute | solution.py:25
  13.2 4.5 %collective-permute-start = (s32[3]{0:T(128)S(1)}, s32[3]{0:T(128)S(1)}, u32[]{:S(2)}, u32[]{:S(2)}) collective-permute-start(s32[3]{0:T(128)S(1)} %get-tuple-element.49), channel_id=1, source_target_pairs={{0,64},{64,128},{128,192},{192,256},{256,320},{320,384},{384,448},... | collective-permute-start | bytes 44 | tf_op jit(solution)/shard_map/ppermute | solution.py:25
  17.8 0.1 and_convert_fusion.1
  17.9 0.1 and_convert_fusion
  18.0 0.1 slice_bitcast_fusion.4
  18.1 0.1 slice_bitcast_fusion.3
  18.2 0.9 collective-permute-done
  19.1 0.1 pad_add_fusion
  19.2 0.1 select_reduce_fusion.1
  19.3 0.1 slice_bitcast_fusion.7
  19.4 0.1 slice_bitcast_fusion.11
  19.5 0.1 slice_bitcast_fusion.9
  19.7 1.9 %collective-permute-done.3 = f32[60,16,3]{2,1,0:T(8,128)S(1)} collective-permute-done((f32[60,16,3]{2,1,0:T(8,128)S(1)}, f32[60,16,3]{2,1,0:T(8,128)S(1)}, u32[]{:S(2)}, u32[]{:S(2)}) %collective-permute-start.3) | collective-permute-done | bytes 11552 | tf_op jit(solution)/shard_map/ppermute | solution.py:25
  21.6 6.0 %collective-permute-done.2 = f32[60,16,3]{2,1,0:T(8,128)S(1)} collective-permute-done((f32[60,16,3]{2,1,0:T(8,128)S(1)}, f32[60,16,3]{2,1,0:T(8,128)S(1)}, u32[]{:S(2)}, u32[]{:S(2)}) %collective-permute-start.2) | collective-permute-done | bytes 11552 | tf_op jit(solution)/shard_map/ppermute | solution.py:25
  27.6 0.6 pad_maximum_fusion
  28.2 0.1 fusion.94
  28.3 0.1 fusion.72
  28.5 1.3 %collective-permute-start.5 = (f32[6,16,262]{2,1,0:T(8,128)S(1)}, f32[6,16,262]{2,1,0:T(8,128)S(1)}, u32[]{:S(2)}, u32[]{:S(2)}) collective-permute-start(f32[6,16,262]{2,1,0:T(8,128)S(1)} %fusion.72), channel_id=1, source_target_pairs={{64,0},{128,64},{192,128},{256,192},{320,256},{384,320},{448,384},... | collective-permute-start | bytes 301832 | tf_op jit(solution)/shard_map/ppermute | solution.py:25
  29.8 0.1 fusion.64
  29.9 4.6 %collective-permute-start.4 = (f32[7,16,262]{2,1,0:T(8,128)S(1)}, f32[7,16,262]{2,1,0:T(8,128)S(1)}, u32[]{:S(2)}, u32[]{:S(2)}) collective-permute-start(f32[7,16,262]{2,1,0:T(8,128)S(1)} %fusion.64), channel_id=1, source_target_pairs={{0,64},{64,128},{128,192},{192,256},{256,320},{320,384},{384,448},... | collective-permute-start | bytes 352136 | tf_op jit(solution)/shard_map/ppermute | solution.py:25
  34.5 1.0 %collective-permute-done.5 = f32[6,16,262]{2,1,0:T(8,128)S(1)} collective-permute-done((f32[6,16,262]{2,1,0:T(8,128)S(1)}, f32[6,16,262]{2,1,0:T(8,128)S(1)}, u32[]{:S(2)}, u32[]{:S(2)}) %collective-permute-start.5) | collective-permute-done | bytes 100640 | tf_op jit(solution)/shard_map/ppermute | solution.py:25
  35.5 1.8 %collective-permute-done.4 = f32[7,16,262]{2,1,0:T(8,128)S(1)} collective-permute-done((f32[7,16,262]{2,1,0:T(8,128)S(1)}, f32[7,16,262]{2,1,0:T(8,128)S(1)}, u32[]{:S(2)}, u32[]{:S(2)}) %collective-permute-start.4) | collective-permute-done | bytes 117408 | tf_op jit(solution)/shard_map/ppermute | solution.py:25
  37.4 1.1 %add_add_fusion.2 = (f32[24,16,256]{2,1,0:T(8,128)}, f32[24,16,256]{2,1,0:T(8,128)}) fusion(f32[24,16,256]{2,1,0:T(8,128)S(1)} %copy-done.3, f32[24,16,256]{2,1,0:T(8,128)S(1)} %copy-done.2, f32[24]{0:T(128)S(1)} %get-tuple-element.41, f32[24,16,262]{2,1,0:T(8,128)S(1)} %get-tuple-element.13, f32[4,16,262]{2,1,0:T(8,128)S(1)} %slice.370), kind=kLoop, calls=%fused_computation.109 | loop fusion | flops 393216 | bytes 2042464 | tf_op jit(solution)/shard_map/add | solution.py:91
  38.5 0.2 pad_maximum_fusion.3
  38.7 1.7 %fusion.96 = (f32[28,16,260]{2,1,0:T(8,128)S(1)}, f32[28,16,260]{2,1,0:T(8,128)S(1)}, f32[28,16,260]{2,1,0:T(8,128)}, f32[28,16,260]{2,1,0:T(8,128)}) fusion(f32[31,16,262]{2,1,0:T(8,128)S(1)} %pad_maximum_fusion.2, f32[30,16,262]{2,1,0:T(8,128)S(1)} %get-tuple-element.22, f32[28]{0:T(128)S(1)} %get-tuple-element.47), kind=kLoop, calls=%fused_computation.195 | loop fusion | flops 349440 | bytes 3261552 | tf_op jit(solution)/shard_map/slice | solution.py:99
  40.4 2.1 %add_add_fusion.1 = (f32[26,16,258]{2,1,0:T(8,128)}, f32[26,16,258]{2,1,0:T(8,128)}, f32[26,16,258]{2,1,0:T(8,128)}, f32[26,16,258]{2,1,0:T(8,128)}) fusion(f32[26]{0:T(128)S(1)} %get-tuple-element.44, f32[30,16,262]{2,1,0:T(8,128)S(1)} %get-tuple-element.22, f32[31,16,262]{2,1,0:T(8,128)S(1)} %pad_maximum_fusion.2, ...), kind=kLoop, calls=%fused_computation.106 | loop fusion | flops 429312 | bytes 3045480 | tf_op jit(solution)/shard_map/add | solution.py:91
  42.4 3.7 %divide_multiply_fusion = (f32[4,30,16,262]{3,2,1,0:T(8,128)S(1)}, f32[4,30,16,262]{3,2,1,0:T(8,128)}) fusion(f32[30,262]{1,0:T(8,128)S(1)} %and_convert_fusion.1, f32[30,16,262]{2,1,0:T(8,128)S(1)} %get-tuple-element.23, f32[30]{0:T(128)S(1)} %get-tuple-element.36, f32[4,16,262]{2,1,0:T(8,128)S(1)} %fusion.81, f32[30]{0:T(128)S(1)} %get-tuple-element.37, ...), kind=kLoop, calls=%fused_computation.21 | loop fusion | flops 12072960 | bytes 4827688 | tf_op jit(solution)/shard_map/mul | solution.py:148
  46.1 8.4 %fusion.20 = f32[4,28,16,260]{3,2,1,0:T(8,128)S(1)} fusion(f32[4,30,16,262]{3,2,1,0:T(8,128)S(1)} %get-tuple-element.24, f32[4,30,16,262]{3,2,1,0:T(8,128)} %get-tuple-element.25, f32[28,260]{1,0:T(8,128)S(1)} %slice_bitcast_fusion.4, f32[28,16,260]{2,1,0:T(8,128)S(1)} %get-tuple-element.18, f32[28,16,260]{2,1,0:T(8,128)} %get-tuple-element.20, ...), kind=kLoop, calls=%fused_computation.46 | loop fusion | flops 12113920 | bytes 22797824 | tf_op jit(solution)/shard_map/mul | solution.py:162
  54.6 8.5 %fusion.41 = f32[4,26,16,258]{3,2,1,0:T(8,128)S(1)} fusion(f32[4,28,16,260]{3,2,1,0:T(8,128)S(1)} %fusion.20, f32[4,30,16,262]{3,2,1,0:T(8,128)} %get-tuple-element.25, f32[26,258]{1,0:T(8,128)S(1)} %slice_bitcast_fusion.3, f32[26,16,258]{2,1,0:T(8,128)} %get-tuple-element.8, f32[26,16,258]{2,1,0:T(8,128)} %get-tuple-element.21, ...), kind=kLoop, calls=%fused_computation.70 | loop fusion | flops 11162112 | bytes 20734464 | tf_op jit(solution)/shard_map/mul | solution.py:162
  63.1 5.0 %multiply_reduce_fusion = (f32[24,16,256]{2,1,0:T(8,128)S(1)}, f32[4,24,16,256]{3,2,1,0:T(8,128)}) fusion(f32[4,30,16,262]{3,2,1,0:T(8,128)S(1)} %copy-done.1, f32[24,16,256]{2,1,0:T(8,128)S(1)} %copy-done.4, f32[24,16,256]{2,1,0:T(8,128)S(1)} %copy-done.3, f32[4,26,16,258]{3,2,1,0:T(8,128)S(1)} %fusion.41, f32[24,16,256]{2,1,0:T(8,128)S(1)} %copy-done.5, ...), kind=kLoop, calls=%fused_computation.94 | loop fusion | flops 10518528 | bytes 15533568 | tf_op jit(solution)/shard_map/reduce_sum | solution.py:164
  68.1 2.4 %fusion.99 = f32[24,16,256]{2,1,0:T(8,128)S(1)} fusion(f32[24,16,256]{2,1,0:T(8,128)S(1)} %get-tuple-element.4), kind=kOutput, calls=%fused_computation.198 | output fusion | flops 2260992 | bytes 786432 | tf_op jit(solution)/shard_map/jit(cumsum)/reduce_window_sum | solution.py:165
  70.5 4.4 %collective-permute-start.6 = (f32[16,256]{1,0:T(8,128)S(1)}, f32[16,256]{1,0:T(8,128)S(1)}, u32[]{:S(2)}, u32[]{:S(2)}) collective-permute-start(f32[16,256]{1,0:T(8,128)S(1)} %slice_bitcast_fusion.5), channel_id=1, source_target_pairs={{0,64},{64,128},{128,192},{192,256},{256,320},{320,384},{384,448},... | collective-permute-start | bytes 49160 | tf_op jit(solution)/shard_map/ppermute | solution.py:25
  74.9 1.4 %collective-permute-done.6 = f32[16,256]{1,0:T(8,128)S(1)} collective-permute-done((f32[16,256]{1,0:T(8,128)S(1)}, f32[16,256]{1,0:T(8,128)S(1)}, u32[]{:S(2)}, u32[]{:S(2)}) %collective-permute-start.6) | collective-permute-done | bytes 16416 | tf_op jit(solution)/shard_map/ppermute | solution.py:25
  76.3 5.7 %collective-permute-start.7 = (f32[16,256]{1,0:T(8,128)S(1)}, f32[16,256]{1,0:T(8,128)S(1)}, u32[]{:S(2)}, u32[]{:S(2)}) collective-permute-start(f32[16,256]{1,0:T(8,128)S(1)} %fusion.91), channel_id=1, source_target_pairs={{0,128},{64,192},{128,256},{192,320},{256,384},{320,448},{1,129},{... | collective-permute-start | bytes 49160 | tf_op jit(solution)/shard_map/ppermute | solution.py:25
  82.1 1.4 %collective-permute-done.7 = f32[16,256]{1,0:T(8,128)S(1)} collective-permute-done((f32[16,256]{1,0:T(8,128)S(1)}, f32[16,256]{1,0:T(8,128)S(1)}, u32[]{:S(2)}, u32[]{:S(2)}) %collective-permute-start.7) | collective-permute-done | bytes 16416 | tf_op jit(solution)/shard_map/ppermute | solution.py:25
  83.5 11.5 %collective-permute-start.8 = (f32[16,256]{1,0:T(8,128)S(1)}, f32[16,256]{1,0:T(8,128)S(1)}, u32[]{:S(2)}, u32[]{:S(2)}) collective-permute-start(f32[16,256]{1,0:T(8,128)S(1)} %add.341), channel_id=1, source_target_pairs={{0,256},{64,320},{128,384},{192,448},{1,257},{65,321},{129,385},{1... | collective-permute-start | bytes 49160 | tf_op jit(solution)/shard_map/ppermute | solution.py:25
  95.0 1.4 %collective-permute-done.8 = f32[16,256]{1,0:T(8,128)S(1)} collective-permute-done((f32[16,256]{1,0:T(8,128)S(1)}, f32[16,256]{1,0:T(8,128)S(1)}, u32[]{:S(2)}, u32[]{:S(2)}) %collective-permute-start.8) | collective-permute-done | bytes 16416 | tf_op jit(solution)/shard_map/ppermute | solution.py:25
  96.4 0.8 add_multiply_fusion
  (38 shorter events, 0.5 us)
Async XLA Ops:
  0.6 1.7 %copy-start = (f32[4,3,16,256]{3,2,1,0:T(8,128)S(1)}, f32[4,3,16,256]{3,2,1,0:T(8,128)}, u32[]{:S(2)}) copy-start(f32[4,3,16,256]{3,2,1,0:T(8,128)} %param.7) | copy-start | bytes 589828
  0.6 18.5 %copy-start.7 = (f32[4]{0:T(128)S(1)}, f32[4]{0:T(128)}, u32[]{:S(2)}) copy-start(f32[4]{0:T(128)} %constant.90.clone) | copy-start | bytes 52
  0.7 18.5 %copy-start.8 = (f32[4]{0:T(128)S(1)}, f32[4]{0:T(128)}, u32[]{:S(2)}) copy-start(f32[4]{0:T(128)} %constant.91.clone) | copy-start | bytes 52
  0.7 26.9 %copy-start.2 = (f32[24,16,256]{2,1,0:T(8,128)S(1)}, f32[24,16,256]{2,1,0:T(8,128)}, u32[]{:S(2)}) copy-start(f32[24,16,256]{2,1,0:T(8,128)} %param.11) | copy-start | bytes 1179652
  0.7 26.9 %copy-start.3 = (f32[24,16,256]{2,1,0:T(8,128)S(1)}, f32[24,16,256]{2,1,0:T(8,128)}, u32[]{:S(2)}) copy-start(f32[24,16,256]{2,1,0:T(8,128)} %param.10) | copy-start | bytes 1179652
  0.7 11.2 %copy-start.6 = (s32[24]{0:T(128)S(1)}, s32[24]{0:T(128)}, u32[]{:S(2)}) copy-start(s32[24]{0:T(128)} %param.9) | copy-start | bytes 292
  4.4 17.2 %collective-permute-start.3 = (f32[60,16,3]{2,1,0:T(8,128)S(1)}, f32[60,16,3]{2,1,0:T(8,128)S(1)}, u32[]{:S(2)}, u32[]{:S(2)}) collective-permute-start(f32[60,16,3]{2,1,0:T(8,128)S(1)} %get-tuple-element.15), channel_id=1, source_target_pairs={{1,0},{2,1},{3,2},{4,3},{5,4},{6,5},{7,6},{8,7},{9,8},{10,9},{11,1... | collective-permute-start | bytes 34568 | tf_op jit(solution)/shard_map/ppermute | solution.py:25
  9.9 17.6 %collective-permute-start.2 = (f32[60,16,3]{2,1,0:T(8,128)S(1)}, f32[60,16,3]{2,1,0:T(8,128)S(1)}, u32[]{:S(2)}, u32[]{:S(2)}) collective-permute-start(f32[60,16,3]{2,1,0:T(8,128)S(1)} %get-tuple-element.14), channel_id=1, source_target_pairs={{0,1},{1,2},{2,3},{3,4},{4,5},{5,6},{6,7},{7,8},{8,9},{9,10},{10,1... | collective-permute-start | bytes 34568 | tf_op jit(solution)/shard_map/ppermute | solution.py:25
  12.0 6.2 %collective-permute-start.1 = (s32[3]{0:T(128)S(1)}, s32[3]{0:T(128)S(1)}, u32[]{:S(2)}, u32[]{:S(2)}) collective-permute-start(s32[3]{0:T(128)S(1)} %get-tuple-element.50), channel_id=1, source_target_pairs={{64,0},{128,64},{192,128},{256,192},{320,256},{384,320},{448,384},... | collective-permute-start | bytes 44 | tf_op jit(solution)/shard_map/ppermute | solution.py:25
  13.2 5.8 %collective-permute-start = (s32[3]{0:T(128)S(1)}, s32[3]{0:T(128)S(1)}, u32[]{:S(2)}, u32[]{:S(2)}) collective-permute-start(s32[3]{0:T(128)S(1)} %get-tuple-element.49), channel_id=1, source_target_pairs={{0,64},{64,128},{128,192},{192,256},{256,320},{320,384},{384,448},... | collective-permute-start | bytes 44 | tf_op jit(solution)/shard_map/ppermute | solution.py:25
  28.5 7.0 %collective-permute-start.5 = (f32[6,16,262]{2,1,0:T(8,128)S(1)}, f32[6,16,262]{2,1,0:T(8,128)S(1)}, u32[]{:S(2)}, u32[]{:S(2)}) collective-permute-start(f32[6,16,262]{2,1,0:T(8,128)S(1)} %fusion.72), channel_id=1, source_target_pairs={{64,0},{128,64},{192,128},{256,192},{320,256},{384,320},{448,384},... | collective-permute-start | bytes 301832 | tf_op jit(solution)/shard_map/ppermute | solution.py:25
  29.9 7.5 %collective-permute-start.4 = (f32[7,16,262]{2,1,0:T(8,128)S(1)}, f32[7,16,262]{2,1,0:T(8,128)S(1)}, u32[]{:S(2)}, u32[]{:S(2)}) collective-permute-start(f32[7,16,262]{2,1,0:T(8,128)S(1)} %fusion.64), channel_id=1, source_target_pairs={{0,64},{64,128},{128,192},{192,256},{256,320},{320,384},{384,448},... | collective-permute-start | bytes 352136 | tf_op jit(solution)/shard_map/ppermute | solution.py:25
  54.5 8.5 %copy-start.1 = (f32[4,30,16,262]{3,2,1,0:T(8,128)S(1)}, f32[4,30,16,262]{3,2,1,0:T(8,128)}, u32[]{:S(2)}) copy-start(f32[4,30,16,262]{3,2,1,0:T(8,128)} %get-tuple-element.25) | copy-start | bytes 6036484
  54.5 8.5 %copy-start.4 = (f32[24,16,256]{2,1,0:T(8,128)S(1)}, f32[24,16,256]{2,1,0:T(8,128)}, u32[]{:S(2)}) copy-start(f32[24,16,256]{2,1,0:T(8,128)} %get-tuple-element.6) | copy-start | bytes 1179652
  54.6 8.5 %copy-start.5 = (f32[24,16,256]{2,1,0:T(8,128)S(1)}, f32[24,16,256]{2,1,0:T(8,128)}, u32[]{:S(2)}) copy-start(f32[24,16,256]{2,1,0:T(8,128)} %get-tuple-element.7) | copy-start | bytes 1179652
  70.5 5.8 %collective-permute-start.6 = (f32[16,256]{1,0:T(8,128)S(1)}, f32[16,256]{1,0:T(8,128)S(1)}, u32[]{:S(2)}, u32[]{:S(2)}) collective-permute-start(f32[16,256]{1,0:T(8,128)S(1)} %slice_bitcast_fusion.5), channel_id=1, source_target_pairs={{0,64},{64,128},{128,192},{192,256},{256,320},{320,384},{384,448},... | collective-permute-start | bytes 49160 | tf_op jit(solution)/shard_map/ppermute | solution.py:25
  76.3 7.2 %collective-permute-start.7 = (f32[16,256]{1,0:T(8,128)S(1)}, f32[16,256]{1,0:T(8,128)S(1)}, u32[]{:S(2)}, u32[]{:S(2)}) collective-permute-start(f32[16,256]{1,0:T(8,128)S(1)} %fusion.91), channel_id=1, source_target_pairs={{0,128},{64,192},{128,256},{192,320},{256,384},{320,448},{1,129},{... | collective-permute-start | bytes 49160 | tf_op jit(solution)/shard_map/ppermute | solution.py:25
  83.5 12.9 %collective-permute-start.8 = (f32[16,256]{1,0:T(8,128)S(1)}, f32[16,256]{1,0:T(8,128)S(1)}, u32[]{:S(2)}, u32[]{:S(2)}) collective-permute-start(f32[16,256]{1,0:T(8,128)S(1)} %add.341), channel_id=1, source_target_pairs={{0,256},{64,320},{128,384},{192,448},{1,257},{65,321},{129,385},{1... | collective-permute-start | bytes 49160 | tf_op jit(solution)/shard_map/ppermute | solution.py:25

commit v2 on v1

--- a/solution.py
+++ b/solution.py
@@ -99,6 +99,17 @@
     return lax.slice_in_dim(array, by, array.shape[col_dim] - by, axis=col_dim)
 
 
+def passed_across(array, by_ply, by_tile):
+    plies, tiles = lax.axis_size("ply"), lax.axis_size("tile")
+    pairs = [
+        (p * tiles + t, (p + by_ply) * tiles + t + by_tile)
+        for p in range(plies)
+        for t in range(tiles)
+        if 0 <= p + by_ply < plies and 0 <= t + by_tile < tiles
+    ]
+    return lax.ppermute(array, ("ply", "tile"), pairs)
+
+
 def body(strain, case_ids, angle_ids, stiffening, interface):
     halo = ITERS - 1
     ply_local = angle_ids.shape[0]
@@ -108,26 +119,56 @@
     cases = case_ids.shape[0]
     chosen = jnp.take(strain, case_ids, axis=0)
     rows = chosen.shape[2]
-
-    packed = jnp.concatenate(
+    width = col_local + 2 * halo
+
+    flat = jnp.concatenate(
         [chosen.reshape(cases * 3, rows, col_local), stiffening, interface], axis=0
     )
-    packed = with_halos(packed, "tile", 2, halo, halo)
-    width = col_local + 2 * halo
+    left = passed_along(flat[..., col_local - halo :], "tile", 1)
+    right = passed_along(flat[..., :halo], "tile", -1)
+    angle_plane = jnp.zeros((1, rows, col_local), jnp.float32)
+    top_planes = jnp.concatenate(
+        [stiffening[ply_local - halo :], interface[ply_local - halo - 1 :]], axis=0
+    )
+    bottom_planes = jnp.concatenate([stiffening[:halo], interface[:halo]], axis=0)
+    below = passed_along(
+        jnp.concatenate(
+            [top_planes, angle_plane.at[0, 0, :halo].set(angle_ids[ply_local - halo :].astype(jnp.float32))],
+            axis=0,
+        ),
+        "ply",
+        1,
+    )
+    above = passed_along(
+        jnp.concatenate(
+            [bottom_planes, angle_plane.at[0, 0, :halo].set(angle_ids[:halo].astype(jnp.float32))],
+            axis=0,
+        ),
+        "ply",
+        -1,
+    )
+    below_left = passed_across(top_planes[..., col_local - halo :], 1, 1)
+    below_right = passed_across(top_planes[..., :halo], 1, -1)
+    above_left = passed_across(bottom_planes[..., col_local - halo :], -1, 1)
+    above_right = passed_across(bottom_planes[..., :halo], -1, -1)
+
+    packed = jnp.concatenate([left, flat, right], axis=2)
     strain_e = packed[: cases * 3].reshape(cases, 3, rows, width)
     stiff_c = packed[cases * 3 : cases * 3 + ply_local]
     inter_c = packed[cases * 3 + ply_local :]
-    below = passed_along(
-        jnp.concatenate([stiff_c[ply_local - halo :], inter_c[ply_local - halo - 1 :]], axis=0),
-        "ply",
-        1,
-    )
-    above = passed_along(jnp.concatenate([stiff_c[:halo], inter_c[:halo]], axis=0), "ply", -1)
-    angles = with_halos(angle_ids, "ply", 0, halo, halo)
-    stiff_e = jnp.concatenate([below[:halo], stiff_c, above[:halo]], axis=0)
-    inter_all = jnp.concatenate([below[halo:], inter_c, above[halo:]], axis=0)
+    below_e = jnp.concatenate([below_left, below[: 2 * halo + 1], below_right], axis=2)
+    above_e = jnp.concatenate([above_left, above[: 2 * halo], above_right], axis=2)
+    stiff_e = jnp.concatenate([below_e[:halo], stiff_c, above_e[:halo]], axis=0)
+    inter_all = jnp.concatenate([below_e[halo:], inter_c, above_e[halo:]], axis=0)
     up_e = inter_all[1:]
     down_e = inter_all[:-1]
+    angles = jnp.concatenate(
+        [
+            below[2 * halo + 1, 0, :halo].astype(jnp.int32),
+            angle_ids,
+            above[2 * halo, 0, :halo].astype(jnp.int32),
+        ]
+    )
 
     cond_rows, cond_cols, cond_cross, ply_cosine, ply_sine = ply_tables(angles)
     source_e = tsai_wu(
@@ -161,16 +202,13 @@
         if iteration < ITERS - 1:
             adjoint = adjoint * trim(inside, by, 0, 2)
     source = trim(source_e, halo, 1, 3)
-    summed = jnp.sum(adjoint * source, axis=0)
-    running = jnp.cumsum(summed, axis=0)
-    inclusive = running[-1]
-    prefix = jnp.zeros_like(inclusive)
-    shift = 1
-    while shift < ply_count:
-        arrived = passed_along(inclusive, "ply", shift)
+    product = adjoint * source
+    total = jnp.sum(product, axis=(0, 1))
+    arrivals = [passed_along(total, "ply", shift) for shift in range(1, ply_count)]
+    running = jnp.cumsum(jnp.sum(product, axis=0), axis=0)
+    prefix = arrivals[0]
+    for arrived in arrivals[1:]:
         prefix = prefix + arrived
-        inclusive = inclusive + arrived
-        shift *= 2
     through = (running + prefix[None]) / (ply_local * ply_count)
     return (adjoint, through)
 

time: 98.5 us -> 111 us (1.13)
  the two profiles are of different devices: /device:TPU:448 before, /device:TPU:260 now
where the time goes in v2:
time: 111 us; the launch traced here: 110 us
  starting transfers between devices  46.1 us (42%)
  other arithmetic  39.3 us (35%)
  waiting for transfers between devices  20.1 us (18%)
  local copies, waits for them, and re-layouts  3.78 us (3%)
    ppermute x11, starting transfers between devices, passed_along(): return lax.ppermute(array, axis, pairs)  28 us
    ppermute x4, starting transfers between devices, passed_across(): return lax.ppermute(array, ('ply', 'tile'), pairs)  18.1 us
    mul x2, other arithmetic, body(): adjoint = adjoint * trim(inside, by, 0, 2)  16.9 us
    ppermute x11, waiting for transfers between devices, passed_along(): return lax.ppermute(array, axis, pairs)  14.4 us
    ppermute x4, waiting for transfers between devices, passed_across(): return lax.ppermute(array, ('ply', 'tile'), pairs)  5.63 us
    reduce_sum x1, other arithmetic, body(): total = jnp.sum(product, axis=(0, 1))  5.02 us
    mul x1, other arithmetic, body(): adjoint = relaxation * source_e / diagonal_sum * inside  3.68 us
    add x2, other arithmetic, sweep(): 2.0 * cond_rows + 2.0 * cond_cols + coupling_up + coupling_down + stiffening  3.12 us
  transfers between devices with their start and end apart: 15, of which 4 were waited for; matrix products, arithmetic and copies ran while one was open for 8% of the time, Pallas kernels for 0%

profile of v2, /device:TPU:260, one launch (start us, length us, event | category | flops | bytes accessed | tf_op | source)
XLA Modules:
  0.0 110.3 jit_solution(6018557605134456311)
XLA Ops:
  0.7 0.9 fusion.88
  1.5 0.8 slice.351
  2.4 0.6 fusion.71
  3.0 4.7 %collective-permute-start.7 = (f32[6,16,3]{2,1,0:T(8,128)}, f32[6,16,3]{2,1,0:T(8,128)}, u32[]{:S(2)}, u32[]{:S(2)}) collective-permute-start(f32[6,16,3]{2,1,0:T(8,128)} %get-tuple-element.59), channel_id=1, source_target_pairs={{65,0},{66,1},{67,2},{68,3},{69,4},{70,5},{71,6},{72,7},{73,8},{74... | collective-permute-start | bytes 3464 | tf_op jit(solution)/shard_map/ppermute | solution.py:110
  7.6 0.8 convert_bitcast_fusion.1
  8.4 0.7 select_maximum_fusion.6
  9.1 2.4 %collective-permute-start.1 = (f32[7,16,256]{2,1,0:T(8,128)}, f32[7,16,256]{2,1,0:T(8,128)}, u32[]{:S(2)}, u32[]{:S(2)}) collective-permute-start(f32[7,16,256]{2,1,0:T(8,128)} %select_maximum_fusion.6), channel_id=1, source_target_pairs={{64,0},{128,64},{192,128},{256,192},{320,256},{384,320},{448,384},... | collective-permute-start | bytes 344072 | tf_op jit(solution)/shard_map/ppermute | solution.py:25
  11.5 1.9 %collective-permute-start.6 = (f32[6,16,3]{2,1,0:T(8,128)S(1)}, f32[6,16,3]{2,1,0:T(8,128)}, u32[]{:S(2)}, u32[]{:S(2)}) collective-permute-start(f32[6,16,3]{2,1,0:T(8,128)S(1)} %get-tuple-element.58), channel_id=1, source_target_pairs={{64,1},{65,2},{66,3},{67,4},{68,5},{69,6},{70,7},{71,8},{72,9},{73... | collective-permute-start | bytes 3464 | tf_op jit(solution)/shard_map/ppermute | solution.py:110
  13.5 0.7 compare_select_fusion
  14.1 0.7 compare_and_fusion.1
  14.9 0.1 broadcast_in_dim.17
  15.0 0.6 gather_fusion
  15.5 0.1 bitcast_select_fusion
  15.6 1.2 %pad_maximum_fusion = f32[60,16,256]{2,1,0:T(8,128)S(1)} fusion(f32[24,16,256]{2,1,0:T(8,128)} %param.15, f32[24,16,256]{2,1,0:T(8,128)} %param.14, f32[12,16,256]{2,1,0:T(8,128)S(1)} %bitcast_select_fusion), kind=kLoop, calls=%fused_computation.97 | loop fusion | flops 491520 | bytes 1966080 | tf_op jit(solution)/shard_map/concatenate | solution.py:124
  16.8 0.2 fusion.86
  17.0 7.3 %collective-permute-start.3 = (f32[60,16,3]{2,1,0:T(8,128)S(1)}, f32[60,16,3]{2,1,0:T(8,128)S(1)}, u32[]{:S(2)}, u32[]{:S(2)}) collective-permute-start(f32[60,16,3]{2,1,0:T(8,128)S(1)} %get-tuple-element.40), channel_id=1, source_target_pairs={{1,0},{2,1},{3,2},{4,3},{5,4},{6,5},{7,6},{8,7},{9,8},{10,9},{11,1... | collective-permute-start | bytes 34568 | tf_op jit(solution)/shard_map/ppermute | solution.py:25
  24.3 1.9 %collective-permute-start.2 = (f32[60,16,3]{2,1,0:T(8,128)S(1)}, f32[60,16,3]{2,1,0:T(8,128)S(1)}, u32[]{:S(2)}, u32[]{:S(2)}) collective-permute-start(f32[60,16,3]{2,1,0:T(8,128)S(1)} %get-tuple-element.39), channel_id=1, source_target_pairs={{0,1},{1,2},{2,3},{3,4},{4,5},{5,6},{6,7},{7,8},{8,9},{9,10},{10,1... | collective-permute-start | bytes 34568 | tf_op jit(solution)/shard_map/ppermute | solution.py:25
  26.6 0.1 slice_bitcast_fusion.3
  26.7 9.2 %collective-permute-done.3 = f32[60,16,3]{2,1,0:T(8,128)S(1)} collective-permute-done((f32[60,16,3]{2,1,0:T(8,128)S(1)}, f32[60,16,3]{2,1,0:T(8,128)S(1)}, u32[]{:S(2)}, u32[]{:S(2)}) %collective-permute-start.3) | collective-permute-done | bytes 11552 | tf_op jit(solution)/shard_map/ppermute | solution.py:25
  36.0 9.6 %collective-permute-start.5 = (f32[7,16,3]{2,1,0:T(8,128)S(1)}, f32[7,16,3]{2,1,0:T(8,128)S(1)}, u32[]{:S(2)}, u32[]{:S(2)}) collective-permute-start(f32[7,16,3]{2,1,0:T(8,128)S(1)} %get-tuple-element.57), channel_id=1, source_target_pairs={{1,64},{2,65},{3,66},{4,67},{5,68},{6,69},{7,70},{8,71},{9,72},{10... | collective-permute-start | bytes 4040 | tf_op jit(solution)/shard_map/ppermute | solution.py:110
  45.5 3.0 %collective-permute-start = (f32[8,16,256]{2,1,0:T(8,128)S(1)}, f32[8,16,256]{2,1,0:T(8,128)S(1)}, u32[]{:S(2)}, u32[]{:S(2)}) collective-permute-start(f32[8,16,256]{2,1,0:T(8,128)S(1)} %select_maximum_fusion.5), channel_id=1, source_target_pairs={{0,64},{64,128},{128,192},{192,256},{256,320},{320,384},{384,448},... | collective-permute-start | bytes 393224 | tf_op jit(solution)/shard_map/ppermute | solution.py:25
  48.6 0.2 pad_maximum_fusion.5
  48.8 0.3 pad_maximum_fusion.3
  49.1 1.9 %collective-permute-start.4 = (f32[7,16,3]{2,1,0:T(8,128)S(1)}, f32[7,16,3]{2,1,0:T(8,128)S(1)}, u32[]{:S(2)}, u32[]{:S(2)}) collective-permute-start(f32[7,16,3]{2,1,0:T(8,128)S(1)} %get-tuple-element.56), channel_id=1, source_target_pairs={{0,65},{1,66},{2,67},{3,68},{4,69},{5,70},{6,71},{7,72},{8,73},{9,... | collective-permute-start | bytes 4040 | tf_op jit(solution)/shard_map/ppermute | solution.py:110
  51.0 0.9 slice.443
  52.0 0.9 pad_maximum_fusion.7
  52.9 0.7 fusion.80
  53.7 0.1 select_reduce_fusion.1
  54.2 5.6 %collective-permute-done.4 = f32[7,16,3]{2,1,0:T(8,128)S(1)} collective-permute-done((f32[7,16,3]{2,1,0:T(8,128)S(1)}, f32[7,16,3]{2,1,0:T(8,128)S(1)}, u32[]{:S(2)}, u32[]{:S(2)}) %collective-permute-start.4) | collective-permute-done | bytes 1376 | tf_op jit(solution)/shard_map/ppermute | solution.py:110
  59.8 0.1 pad_maximum_fusion.6
  60.0 1.1 add_add_fusion.2
  61.1 0.4 fusion.64
  61.5 1.7 %fusion.87 = (f32[28,16,260]{2,1,0:T(8,128)S(1)}, f32[28,16,260]{2,1,0:T(8,128)S(1)}, f32[28,16,260]{2,1,0:T(8,128)}, f32[28,16,260]{2,1,0:T(8,128)}) fusion(f32[31,16,262]{2,1,0:T(8,128)S(1)} %pad_maximum_fusion.1, f32[30,16,262]{2,1,0:T(8,128)S(1)} %get-tuple-element.38, f32[28]{0:T(128)S(1)} %get-tuple-element.76), kind=kLoop, calls=%fused_computation.196 | loop fusion | flops 349440 | bytes 3261552 | tf_op jit(solution)/shard_map/slice | solution.py:99
  63.2 2.0 %add_add_fusion.1 = (f32[26,16,258]{2,1,0:T(8,128)}, f32[26,16,258]{2,1,0:T(8,128)}, f32[26,16,258]{2,1,0:T(8,128)}, f32[26,16,258]{2,1,0:T(8,128)}) fusion(f32[26]{0:T(128)S(1)} %get-tuple-element.73, f32[30,16,262]{2,1,0:T(8,128)S(1)} %get-tuple-element.38, f32[31,16,262]{2,1,0:T(8,128)S(1)} %pad_maximum_fusion.1, ...), kind=kLoop, calls=%fused_computation.116 | loop fusion | flops 429312 | bytes 3045480 | tf_op jit(solution)/shard_map/add | solution.py:91
  65.2 3.7 %divide_multiply_fusion = (f32[4,30,16,262]{3,2,1,0:T(8,128)S(1)}, f32[4,30,16,262]{3,2,1,0:T(8,128)}) fusion(f32[30,262]{1,0:T(8,128)S(1)} %and_convert_fusion.1, f32[30,16,262]{2,1,0:T(8,128)S(1)} %get-tuple-element.37, f32[30]{0:T(128)S(1)} %get-tuple-element.65, f32[4,16,262]{2,1,0:T(8,128)S(1)} %fusion.69, f32[30]{0:T(128)S(1)} %get-tuple-element.66, ...), kind=kLoop, calls=%fused_computation.21 | loop fusion | flops 12072960 | bytes 4827688 | tf_op jit(solution)/shard_map/mul | solution.py:189
  68.9 8.4 %fusion.20 = f32[4,28,16,260]{3,2,1,0:T(8,128)S(1)} fusion(f32[4,30,16,262]{3,2,1,0:T(8,128)S(1)} %get-tuple-element.47, f32[4,30,16,262]{3,2,1,0:T(8,128)} %get-tuple-element.48, f32[28,260]{1,0:T(8,128)S(1)} %slice_bitcast_fusion.4, f32[28,16,260]{2,1,0:T(8,128)S(1)} %get-tuple-element.43, f32[28,16,260]{2,1,0:T(8,128)} %get-tuple-element.45, ...), kind=kLoop, calls=%fused_computation.46 | loop fusion | flops 12113920 | bytes 22797824 | tf_op jit(solution)/shard_map/mul | solution.py:203
  77.4 8.5 %fusion.41 = f32[4,26,16,258]{3,2,1,0:T(8,128)S(1)} fusion(f32[4,28,16,260]{3,2,1,0:T(8,128)S(1)} %fusion.20, f32[4,30,16,262]{3,2,1,0:T(8,128)} %get-tuple-element.48, f32[26,258]{1,0:T(8,128)S(1)} %slice_bitcast_fusion.3, f32[26,16,258]{2,1,0:T(8,128)} %get-tuple-element.33, f32[26,16,258]{2,1,0:T(8,128)} %get-tuple-element.46, ...), kind=kLoop, calls=%fused_computation.70 | loop fusion | flops 11162112 | bytes 20734464 | tf_op jit(solution)/shard_map/mul | solution.py:203
  85.9 5.0 %fusion.67 = (f32[16,256]{1,0:T(8,128)S(1)}, f32[24,16,256]{2,1,0:T(8,128)S(1)}, f32[4,24,16,256]{3,2,1,0:T(8,128)}) fusion(f32[4,30,16,262]{3,2,1,0:T(8,128)S(1)} %copy-done.1, f32[24,16,256]{2,1,0:T(8,128)S(1)} %copy-done.4, f32[24,16,256]{2,1,0:T(8,128)S(1)} %copy-done.3, f32[4,26,16,258]{3,2,1,0:T(8,128)S(1)} %fusion.41, ...), kind=kLoop, calls=%fused_computation.117 | loop fusion | flops 10907648 | bytes 15549952 | tf_op jit(solution)/shard_map/reduce_sum | solution.py:206
  90.9 0.7 collective-permute-start.14
  91.6 0.7 collective-permute-start.13
  92.2 1.6 %collective-permute-start.12 = (f32[16,256]{1,0:T(8,128)S(1)}, f32[16,256]{1,0:T(8,128)S(1)}, u32[]{:S(2)}, u32[]{:S(2)}) collective-permute-start(f32[16,256]{1,0:T(8,128)S(1)} %get-tuple-element.26), channel_id=1, source_target_pairs={{0,320},{64,384},{128,448},{1,321},{65,385},{129,449},{2,322},{66,... | collective-permute-start | bytes 49160 | tf_op jit(solution)/shard_map/ppermute | solution.py:25
  93.9 3.8 %collective-permute-start.11 = (f32[16,256]{1,0:T(8,128)S(1)}, f32[16,256]{1,0:T(8,128)S(1)}, u32[]{:S(2)}, u32[]{:S(2)}) collective-permute-start(f32[16,256]{1,0:T(8,128)S(1)} %get-tuple-element.26), channel_id=1, source_target_pairs={{0,256},{64,320},{128,384},{192,448},{1,257},{65,321},{129,385},{1... | collective-permute-start | bytes 49160 | tf_op jit(solution)/shard_map/ppermute | solution.py:25
  97.7 1.5 %collective-permute-start.10 = (f32[16,256]{1,0:T(8,128)S(1)}, f32[16,256]{1,0:T(8,128)S(1)}, u32[]{:S(2)}, u32[]{:S(2)}) collective-permute-start(f32[16,256]{1,0:T(8,128)S(1)} %get-tuple-element.26), channel_id=1, source_target_pairs={{0,192},{64,256},{128,320},{192,384},{256,448},{1,193},{65,257},{1... | collective-permute-start | bytes 49160 | tf_op jit(solution)/shard_map/ppermute | solution.py:25
  99.2 3.2 %collective-permute-start.8 = (f32[16,256]{1,0:T(8,128)S(1)}, f32[16,256]{1,0:T(8,128)S(1)}, u32[]{:S(2)}, u32[]{:S(2)}) collective-permute-start(f32[16,256]{1,0:T(8,128)S(1)} %get-tuple-element.26), channel_id=1, source_target_pairs={{0,64},{64,128},{128,192},{192,256},{256,320},{320,384},{384,448},... | collective-permute-start | bytes 49160 | tf_op jit(solution)/shard_map/ppermute | solution.py:25
  102.4 1.9 %collective-permute-start.9 = (f32[16,256]{1,0:T(8,128)S(1)}, f32[16,256]{1,0:T(8,128)S(1)}, u32[]{:S(2)}, u32[]{:S(2)}) collective-permute-start(f32[16,256]{1,0:T(8,128)S(1)} %get-tuple-element.26), channel_id=1, source_target_pairs={{0,128},{64,192},{128,256},{192,320},{256,384},{320,448},{1,129},{... | collective-permute-start | bytes 49160 | tf_op jit(solution)/shard_map/ppermute | solution.py:25
  104.3 0.5 collective-permute-done.8
  104.8 4.7 %collective-permute-done.9 = f32[16,256]{1,0:T(8,128)S(1)} collective-permute-done((f32[16,256]{1,0:T(8,128)S(1)}, f32[16,256]{1,0:T(8,128)S(1)}, u32[]{:S(2)}, u32[]{:S(2)}) %collective-permute-start.9) | collective-permute-done | bytes 16416 | tf_op jit(solution)/shard_map/ppermute | solution.py:25
  109.5 0.8 add_multiply_fusion
  (55 shorter events, 1.1 us)
Async XLA Ops:
  0.6 14.3 %copy-start = (f32[4,3,16,256]{3,2,1,0:T(8,128)S(1)}, f32[4,3,16,256]{3,2,1,0:T(8,128)}, u32[]{:S(2)}) copy-start(f32[4,3,16,256]{3,2,1,0:T(8,128)} %param.11) | copy-start | bytes 589828
  0.6 25.6 %copy-start.2 = (f32[24,16,256]{2,1,0:T(8,128)S(1)}, f32[24,16,256]{2,1,0:T(8,128)}, u32[]{:S(2)}) copy-start(f32[24,16,256]{2,1,0:T(8,128)} %param.15) | copy-start | bytes 1179652
  3.0 49.0 %collective-permute-start.7 = (f32[6,16,3]{2,1,0:T(8,128)}, f32[6,16,3]{2,1,0:T(8,128)}, u32[]{:S(2)}, u32[]{:S(2)}) collective-permute-start(f32[6,16,3]{2,1,0:T(8,128)} %get-tuple-element.59), channel_id=1, source_target_pairs={{65,0},{66,1},{67,2},{68,3},{69,4},{70,5},{71,6},{72,7},{73,8},{74... | collective-permute-start | bytes 3464 | tf_op jit(solution)/shard_map/ppermute | solution.py:110
  9.1 40.0 %collective-permute-start.1 = (f32[7,16,256]{2,1,0:T(8,128)}, f32[7,16,256]{2,1,0:T(8,128)}, u32[]{:S(2)}, u32[]{:S(2)}) collective-permute-start(f32[7,16,256]{2,1,0:T(8,128)} %select_maximum_fusion.6), channel_id=1, source_target_pairs={{64,0},{128,64},{192,128},{256,192},{320,256},{384,320},{448,384},... | collective-permute-start | bytes 344072 | tf_op jit(solution)/shard_map/ppermute | solution.py:25
  11.5 40.4 %collective-permute-start.6 = (f32[6,16,3]{2,1,0:T(8,128)S(1)}, f32[6,16,3]{2,1,0:T(8,128)}, u32[]{:S(2)}, u32[]{:S(2)}) collective-permute-start(f32[6,16,3]{2,1,0:T(8,128)S(1)} %get-tuple-element.58), channel_id=1, source_target_pairs={{64,1},{65,2},{66,3},{67,4},{68,5},{69,6},{70,7},{71,8},{72,9},{73... | collective-permute-start | bytes 3464 | tf_op jit(solution)/shard_map/ppermute | solution.py:110
  15.0 33.6 %copy-start.3 = (f32[24,16,256]{2,1,0:T(8,128)S(1)}, f32[24,16,256]{2,1,0:T(8,128)}, u32[]{:S(2)}) copy-start(f32[24,16,256]{2,1,0:T(8,128)} %param.14) | copy-start | bytes 1179652
  17.0 19.0 %collective-permute-start.3 = (f32[60,16,3]{2,1,0:T(8,128)S(1)}, f32[60,16,3]{2,1,0:T(8,128)S(1)}, u32[]{:S(2)}, u32[]{:S(2)}) collective-permute-start(f32[60,16,3]{2,1,0:T(8,128)S(1)} %get-tuple-element.40), channel_id=1, source_target_pairs={{1,0},{2,1},{3,2},{4,3},{5,4},{6,5},{7,6},{8,7},{9,8},{10,9},{11,1... | collective-permute-start | bytes 34568 | tf_op jit(solution)/shard_map/ppermute | solution.py:25
  24.3 21.2 %collective-permute-start.2 = (f32[60,16,3]{2,1,0:T(8,128)S(1)}, f32[60,16,3]{2,1,0:T(8,128)S(1)}, u32[]{:S(2)}, u32[]{:S(2)}) collective-permute-start(f32[60,16,3]{2,1,0:T(8,128)S(1)} %get-tuple-element.39), channel_id=1, source_target_pairs={{0,1},{1,2},{2,3},{3,4},{4,5},{5,6},{6,7},{7,8},{8,9},{9,10},{10,1... | collective-permute-start | bytes 34568 | tf_op jit(solution)/shard_map/ppermute | solution.py:25
  36.0 17.6 %copy-start.6 = (s32[24]{0:T(128)S(1)}, s32[24]{0:T(128)}, u32[]{:S(2)}) copy-start(s32[24]{0:T(128)} %param.13) | copy-start | bytes 292
  36.0 17.7 %copy-start.7 = (f32[4]{0:T(128)S(1)}, f32[4]{0:T(128)}, u32[]{:S(2)}) copy-start(f32[4]{0:T(128)} %constant.138.clone) | copy-start | bytes 52
  36.0 17.7 %copy-start.8 = (f32[4]{0:T(128)S(1)}, f32[4]{0:T(128)}, u32[]{:S(2)}) copy-start(f32[4]{0:T(128)} %constant.139.clone) | copy-start | bytes 52
  36.0 18.2 %collective-permute-start.5 = (f32[7,16,3]{2,1,0:T(8,128)S(1)}, f32[7,16,3]{2,1,0:T(8,128)S(1)}, u32[]{:S(2)}, u32[]{:S(2)}) collective-permute-start(f32[7,16,3]{2,1,0:T(8,128)S(1)} %get-tuple-element.57), channel_id=1, source_target_pairs={{1,64},{2,65},{3,66},{4,67},{5,68},{6,69},{7,70},{8,71},{9,72},{10... | collective-permute-start | bytes 4040 | tf_op jit(solution)/shard_map/ppermute | solution.py:110
  45.5 8.1 %collective-permute-start = (f32[8,16,256]{2,1,0:T(8,128)S(1)}, f32[8,16,256]{2,1,0:T(8,128)S(1)}, u32[]{:S(2)}, u32[]{:S(2)}) collective-permute-start(f32[8,16,256]{2,1,0:T(8,128)S(1)} %select_maximum_fusion.5), channel_id=1, source_target_pairs={{0,64},{64,128},{128,192},{192,256},{256,320},{320,384},{384,448},... | collective-permute-start | bytes 393224 | tf_op jit(solution)/shard_map/ppermute | solution.py:25
  49.1 10.7 %collective-permute-start.4 = (f32[7,16,3]{2,1,0:T(8,128)S(1)}, f32[7,16,3]{2,1,0:T(8,128)S(1)}, u32[]{:S(2)}, u32[]{:S(2)}) collective-permute-start(f32[7,16,3]{2,1,0:T(8,128)S(1)} %get-tuple-element.56), channel_id=1, source_target_pairs={{0,65},{1,66},{2,67},{3,68},{4,69},{5,70},{6,71},{7,72},{8,73},{9,... | collective-permute-start | bytes 4040 | tf_op jit(solution)/shard_map/ppermute | solution.py:110
  77.3 8.5 %copy-start.1 = (f32[4,30,16,262]{3,2,1,0:T(8,128)S(1)}, f32[4,30,16,262]{3,2,1,0:T(8,128)}, u32[]{:S(2)}) copy-start(f32[4,30,16,262]{3,2,1,0:T(8,128)} %get-tuple-element.48) | copy-start | bytes 6036484
  77.4 8.5 %copy-start.4 = (f32[24,16,256]{2,1,0:T(8,128)S(1)}, f32[24,16,256]{2,1,0:T(8,128)}, u32[]{:S(2)}) copy-start(f32[24,16,256]{2,1,0:T(8,128)} %get-tuple-element.31) | copy-start | bytes 1179652
  77.4 8.5 %copy-start.5 = (f32[24,16,256]{2,1,0:T(8,128)S(1)}, f32[24,16,256]{2,1,0:T(8,128)}, u32[]{:S(2)}) copy-start(f32[24,16,256]{2,1,0:T(8,128)} %get-tuple-element.32) | copy-start | bytes 1179652
  90.9 8.3 %collective-permute-start.14 = (f32[16,256]{1,0:T(8,128)S(1)}, f32[16,256]{1,0:T(8,128)S(1)}, u32[]{:S(2)}, u32[]{:S(2)}) collective-permute-start(f32[16,256]{1,0:T(8,128)S(1)} %get-tuple-element.26), channel_id=1, source_target_pairs={{0,448},{1,449},{2,450},{3,451},{4,452},{5,453},{6,454},{7,455},{8... | collective-permute-start | bytes 49160 | tf_op jit(solution)/shard_map/ppermute | solution.py:25
  91.6 10.8 %collective-permute-start.13 = (f32[16,256]{1,0:T(8,128)S(1)}, f32[16,256]{1,0:T(8,128)S(1)}, u32[]{:S(2)}, u32[]{:S(2)}) collective-permute-start(f32[16,256]{1,0:T(8,128)S(1)} %get-tuple-element.26), channel_id=1, source_target_pairs={{0,384},{64,448},{1,385},{65,449},{2,386},{66,450},{3,387},{67,451... | collective-permute-start | bytes 49160 | tf_op jit(solution)/shard_map/ppermute | solution.py:25
  92.2 12.1 %collective-permute-start.12 = (f32[16,256]{1,0:T(8,128)S(1)}, f32[16,256]{1,0:T(8,128)S(1)}, u32[]{:S(2)}, u32[]{:S(2)}) collective-permute-start(f32[16,256]{1,0:T(8,128)S(1)} %get-tuple-element.26), channel_id=1, source_target_pairs={{0,320},{64,384},{128,448},{1,321},{65,385},{129,449},{2,322},{66,... | collective-permute-start | bytes 49160 | tf_op jit(solution)/shard_map/ppermute | solution.py:25
  93.9 10.5 %collective-permute-start.11 = (f32[16,256]{1,0:T(8,128)S(1)}, f32[16,256]{1,0:T(8,128)S(1)}, u32[]{:S(2)}, u32[]{:S(2)}) collective-permute-start(f32[16,256]{1,0:T(8,128)S(1)} %get-tuple-element.26), channel_id=1, source_target_pairs={{0,256},{64,320},{128,384},{192,448},{1,257},{65,321},{129,385},{1... | collective-permute-start | bytes 49160 | tf_op jit(solution)/shard_map/ppermute | solution.py:25
  97.7 6.7 %collective-permute-start.10 = (f32[16,256]{1,0:T(8,128)S(1)}, f32[16,256]{1,0:T(8,128)S(1)}, u32[]{:S(2)}, u32[]{:S(2)}) collective-permute-start(f32[16,256]{1,0:T(8,128)S(1)} %get-tuple-element.26), channel_id=1, source_target_pairs={{0,192},{64,256},{128,320},{192,384},{256,448},{1,193},{65,257},{1... | collective-permute-start | bytes 49160 | tf_op jit(solution)/shard_map/ppermute | solution.py:25
  99.2 5.6 %collective-permute-start.8 = (f32[16,256]{1,0:T(8,128)S(1)}, f32[16,256]{1,0:T(8,128)S(1)}, u32[]{:S(2)}, u32[]{:S(2)}) collective-permute-start(f32[16,256]{1,0:T(8,128)S(1)} %get-tuple-element.26), channel_id=1, source_target_pairs={{0,64},{64,128},{128,192},{192,256},{256,320},{320,384},{384,448},... | collective-permute-start | bytes 49160 | tf_op jit(solution)/shard_map/ppermute | solution.py:25
  102.4 7.1 %collective-permute-start.9 = (f32[16,256]{1,0:T(8,128)S(1)}, f32[16,256]{1,0:T(8,128)S(1)}, u32[]{:S(2)}, u32[]{:S(2)}) collective-permute-start(f32[16,256]{1,0:T(8,128)S(1)} %get-tuple-element.26), channel_id=1, source_target_pairs={{0,128},{64,192},{128,256},{192,320},{256,384},{320,448},{1,129},{... | collective-permute-start | bytes 49160 | tf_op jit(solution)/shard_map/ppermute | solution.py:25

commit v3 on v1

--- a/solution.py
+++ b/solution.py
@@ -161,16 +161,13 @@
         if iteration < ITERS - 1:
             adjoint = adjoint * trim(inside, by, 0, 2)
     source = trim(source_e, halo, 1, 3)
-    summed = jnp.sum(adjoint * source, axis=0)
-    running = jnp.cumsum(summed, axis=0)
-    inclusive = running[-1]
-    prefix = jnp.zeros_like(inclusive)
-    shift = 1
-    while shift < ply_count:
-        arrived = passed_along(inclusive, "ply", shift)
+    product = adjoint * source
+    total = jnp.sum(product, axis=(0, 1))
+    arrivals = [passed_along(total, "ply", shift) for shift in range(1, ply_count)]
+    running = jnp.cumsum(jnp.sum(product, axis=0), axis=0)
+    prefix = arrivals[0]
+    for arrived in arrivals[1:]:
         prefix = prefix + arrived
-        inclusive = inclusive + arrived
-        shift *= 2
     through = (running + prefix[None]) / (ply_local * ply_count)
     return (adjoint, through)
 

time: 98.5 us -> 91.3 us (0.927)
  the two profiles are of different devices: /device:TPU:448 before, /device:TPU:262 now
where the time goes in v3:
time: 91.3 us; the launch traced here: 90.9 us
  starting transfers between devices  36.8 us (40%)
  other arithmetic  35.7 us (39%)
  waiting for transfers between devices  15.9 us (17%)
  local copies, waits for them, and re-layouts  1.35 us (1%)
  between operations  1.04 us (1%)
    ppermute x13, starting transfers between devices, passed_along(): return lax.ppermute(array, axis, pairs)  36.8 us
    mul x2, other arithmetic, body(): adjoint = adjoint * trim(inside, by, 0, 2)  16.9 us
    ppermute x13, waiting for transfers between devices, passed_along(): return lax.ppermute(array, axis, pairs)  15.9 us
    reduce_sum x1, other arithmetic, body(): total = jnp.sum(product, axis=(0, 1))  5.02 us
    mul x1, other arithmetic, body(): adjoint = relaxation * source_e / diagonal_sum * inside  3.68 us
    add x2, other arithmetic, sweep(): 2.0 * cond_rows + 2.0 * cond_cols + coupling_up + coupling_down + stiffening  3.15 us
  transfers between devices with their start and end apart: 13, of which 5 were waited for; matrix products, arithmetic and copies ran while one was open for 1% of the time, Pallas kernels for 0%

profile of v3, /device:TPU:262, one launch (start us, length us, event | category | flops | bytes accessed | tf_op | source)
XLA Modules:
  0.0 90.9 jit_solution(3439098599538748584)
XLA Ops:
  0.7 0.8 compare_select_fusion
  1.5 0.7 compare_and_fusion.1
  2.1 0.1 broadcast_in_dim.16
  2.2 0.1 broadcast_in_dim.17
  2.3 0.6 gather_fusion
  2.9 0.1 bitcast_select_fusion
  3.0 1.2 %pad_maximum_fusion.1 = f32[60,16,256]{2,1,0:T(8,128)S(1)} fusion(f32[24,16,256]{2,1,0:T(8,128)} %param.11, f32[24,16,256]{2,1,0:T(8,128)} %param.10, f32[12,16,256]{2,1,0:T(8,128)S(1)} %bitcast_select_fusion), kind=kLoop, calls=%fused_computation.96 | loop fusion | flops 491520 | bytes 1966080 | tf_op jit(solution)/shard_map/concatenate | solution.py:112
  4.2 0.2 fusion.96
  4.4 4.7 %collective-permute-start.3 = (f32[60,16,3]{2,1,0:T(8,128)S(1)}, f32[60,16,3]{2,1,0:T(8,128)S(1)}, u32[]{:S(2)}, u32[]{:S(2)}) collective-permute-start(f32[60,16,3]{2,1,0:T(8,128)S(1)} %get-tuple-element.16), channel_id=1, source_target_pairs={{1,0},{2,1},{3,2},{4,3},{5,4},{6,5},{7,6},{8,7},{9,8},{10,9},{11,1... | collective-permute-start | bytes 34568 | tf_op jit(solution)/shard_map/ppermute | solution.py:25
  9.1 1.9 %collective-permute-start.2 = (f32[60,16,3]{2,1,0:T(8,128)S(1)}, f32[60,16,3]{2,1,0:T(8,128)S(1)}, u32[]{:S(2)}, u32[]{:S(2)}) collective-permute-start(f32[60,16,3]{2,1,0:T(8,128)S(1)} %get-tuple-element.15), channel_id=1, source_target_pairs={{0,1},{1,2},{2,3},{3,4},{4,5},{5,6},{6,7},{7,8},{8,9},{9,10},{10,1... | collective-permute-start | bytes 34568 | tf_op jit(solution)/shard_map/ppermute | solution.py:25
  11.1 2.7 %collective-permute-start.1 = (s32[3]{0:T(128)S(1)}, s32[3]{0:T(128)S(1)}, u32[]{:S(2)}, u32[]{:S(2)}) collective-permute-start(s32[3]{0:T(128)S(1)} %get-tuple-element.51), channel_id=1, source_target_pairs={{64,0},{128,64},{192,128},{256,192},{320,256},{384,320},{448,384},... | collective-permute-start | bytes 44 | tf_op jit(solution)/shard_map/ppermute | solution.py:25
  13.8 5.2 %collective-permute-start = (s32[3]{0:T(128)S(1)}, s32[3]{0:T(128)S(1)}, u32[]{:S(2)}, u32[]{:S(2)}) collective-permute-start(s32[3]{0:T(128)S(1)} %get-tuple-element.50), channel_id=1, source_target_pairs={{0,64},{64,128},{128,192},{192,256},{256,320},{320,384},{384,448},... | collective-permute-start | bytes 44 | tf_op jit(solution)/shard_map/ppermute | solution.py:25
  19.1 0.1 and_convert_fusion.1
  19.1 0.1 and_convert_fusion
  19.2 0.1 slice_bitcast_fusion.4
  19.3 0.1 slice_bitcast_fusion.3
  19.4 0.9 collective-permute-done
  20.3 0.1 pad_add_fusion
  20.4 0.1 select_reduce_fusion.1
  20.5 0.1 slice_bitcast_fusion.6
  20.6 0.1 slice_bitcast_fusion.10
  20.7 0.1 slice_bitcast_fusion.8
  20.9 6.9 %collective-permute-done.2 = f32[60,16,3]{2,1,0:T(8,128)S(1)} collective-permute-done((f32[60,16,3]{2,1,0:T(8,128)S(1)}, f32[60,16,3]{2,1,0:T(8,128)S(1)}, u32[]{:S(2)}, u32[]{:S(2)}) %collective-permute-start.2) | collective-permute-done | bytes 11552 | tf_op jit(solution)/shard_map/ppermute | solution.py:25
  27.8 0.6 pad_maximum_fusion
  28.4 0.1 fusion.95
  28.5 0.1 fusion.74
  28.6 2.7 %collective-permute-start.5 = (f32[6,16,262]{2,1,0:T(8,128)S(1)}, f32[6,16,262]{2,1,0:T(8,128)S(1)}, u32[]{:S(2)}, u32[]{:S(2)}) collective-permute-start(f32[6,16,262]{2,1,0:T(8,128)S(1)} %fusion.74), channel_id=1, source_target_pairs={{64,0},{128,64},{192,128},{256,192},{320,256},{384,320},{448,384},... | collective-permute-start | bytes 301832 | tf_op jit(solution)/shard_map/ppermute | solution.py:25
  31.4 0.1 fusion.66
  31.5 5.2 %collective-permute-start.4 = (f32[7,16,262]{2,1,0:T(8,128)S(1)}, f32[7,16,262]{2,1,0:T(8,128)S(1)}, u32[]{:S(2)}, u32[]{:S(2)}) collective-permute-start(f32[7,16,262]{2,1,0:T(8,128)S(1)} %fusion.66), channel_id=1, source_target_pairs={{0,64},{64,128},{128,192},{192,256},{256,320},{320,384},{384,448},... | collective-permute-start | bytes 352136 | tf_op jit(solution)/shard_map/ppermute | solution.py:25
  36.7 1.0 %collective-permute-done.5 = f32[6,16,262]{2,1,0:T(8,128)S(1)} collective-permute-done((f32[6,16,262]{2,1,0:T(8,128)S(1)}, f32[6,16,262]{2,1,0:T(8,128)S(1)}, u32[]{:S(2)}, u32[]{:S(2)}) %collective-permute-start.5) | collective-permute-done | bytes 100640 | tf_op jit(solution)/shard_map/ppermute | solution.py:25
  37.8 1.8 %collective-permute-done.4 = f32[7,16,262]{2,1,0:T(8,128)S(1)} collective-permute-done((f32[7,16,262]{2,1,0:T(8,128)S(1)}, f32[7,16,262]{2,1,0:T(8,128)S(1)}, u32[]{:S(2)}, u32[]{:S(2)}) %collective-permute-start.4) | collective-permute-done | bytes 117408 | tf_op jit(solution)/shard_map/ppermute | solution.py:25
  39.7 1.1 %add_add_fusion.2 = (f32[24,16,256]{2,1,0:T(8,128)}, f32[24,16,256]{2,1,0:T(8,128)}) fusion(f32[24,16,256]{2,1,0:T(8,128)S(1)} %copy-done.3, f32[24,16,256]{2,1,0:T(8,128)S(1)} %copy-done.2, f32[24]{0:T(128)S(1)} %get-tuple-element.42, f32[24,16,262]{2,1,0:T(8,128)S(1)} %get-tuple-element.14, f32[4,16,262]{2,1,0:T(8,128)S(1)} %slice.366), kind=kLoop, calls=%fused_computation.111 | loop fusion | flops 393216 | bytes 2042464 | tf_op jit(solution)/shard_map/add | solution.py:91
  40.8 0.2 pad_maximum_fusion.3
  41.0 1.7 %fusion.97 = (f32[28,16,260]{2,1,0:T(8,128)S(1)}, f32[28,16,260]{2,1,0:T(8,128)S(1)}, f32[28,16,260]{2,1,0:T(8,128)}, f32[28,16,260]{2,1,0:T(8,128)}) fusion(f32[31,16,262]{2,1,0:T(8,128)S(1)} %pad_maximum_fusion.2, f32[30,16,262]{2,1,0:T(8,128)S(1)} %get-tuple-element.23, f32[28]{0:T(128)S(1)} %get-tuple-element.48), kind=kLoop, calls=%fused_computation.195 | loop fusion | flops 349440 | bytes 3261552 | tf_op jit(solution)/shard_map/slice | solution.py:99
  42.7 2.1 %add_add_fusion.1 = (f32[26,16,258]{2,1,0:T(8,128)}, f32[26,16,258]{2,1,0:T(8,128)}, f32[26,16,258]{2,1,0:T(8,128)}, f32[26,16,258]{2,1,0:T(8,128)}) fusion(f32[26]{0:T(128)S(1)} %get-tuple-element.45, f32[30,16,262]{2,1,0:T(8,128)S(1)} %get-tuple-element.23, f32[31,16,262]{2,1,0:T(8,128)S(1)} %pad_maximum_fusion.2, ...), kind=kLoop, calls=%fused_computation.106 | loop fusion | flops 429312 | bytes 3045480 | tf_op jit(solution)/shard_map/add | solution.py:91
  44.8 3.7 %divide_multiply_fusion = (f32[4,30,16,262]{3,2,1,0:T(8,128)S(1)}, f32[4,30,16,262]{3,2,1,0:T(8,128)}) fusion(f32[30,262]{1,0:T(8,128)S(1)} %and_convert_fusion.1, f32[30,16,262]{2,1,0:T(8,128)S(1)} %get-tuple-element.24, f32[30]{0:T(128)S(1)} %get-tuple-element.37, f32[4,16,262]{2,1,0:T(8,128)S(1)} %fusion.83, f32[30]{0:T(128)S(1)} %get-tuple-element.38, ...), kind=kLoop, calls=%fused_computation.21 | loop fusion | flops 12072960 | bytes 4827688 | tf_op jit(solution)/shard_map/mul | solution.py:148
  48.4 8.4 %fusion.20 = f32[4,28,16,260]{3,2,1,0:T(8,128)S(1)} fusion(f32[4,30,16,262]{3,2,1,0:T(8,128)S(1)} %get-tuple-element.25, f32[4,30,16,262]{3,2,1,0:T(8,128)} %get-tuple-element.26, f32[28,260]{1,0:T(8,128)S(1)} %slice_bitcast_fusion.4, f32[28,16,260]{2,1,0:T(8,128)S(1)} %get-tuple-element.19, f32[28,16,260]{2,1,0:T(8,128)} %get-tuple-element.21, ...), kind=kLoop, calls=%fused_computation.46 | loop fusion | flops 12113920 | bytes 22797824 | tf_op jit(solution)/shard_map/mul | solution.py:162
  56.9 8.5 %fusion.41 = f32[4,26,16,258]{3,2,1,0:T(8,128)S(1)} fusion(f32[4,28,16,260]{3,2,1,0:T(8,128)S(1)} %fusion.20, f32[4,30,16,262]{3,2,1,0:T(8,128)} %get-tuple-element.26, f32[26,258]{1,0:T(8,128)S(1)} %slice_bitcast_fusion.3, f32[26,16,258]{2,1,0:T(8,128)} %get-tuple-element.9, f32[26,16,258]{2,1,0:T(8,128)} %get-tuple-element.22, ...), kind=kLoop, calls=%fused_computation.70 | loop fusion | flops 11162112 | bytes 20734464 | tf_op jit(solution)/shard_map/mul | solution.py:162
  65.4 5.0 %fusion.64 = (f32[16,256]{1,0:T(8,128)S(1)}, f32[24,16,256]{2,1,0:T(8,128)S(1)}, f32[4,24,16,256]{3,2,1,0:T(8,128)}) fusion(f32[4,30,16,262]{3,2,1,0:T(8,128)S(1)} %copy-done.1, f32[24,16,256]{2,1,0:T(8,128)S(1)} %copy-done.4, f32[24,16,256]{2,1,0:T(8,128)S(1)} %copy-done.3, f32[4,26,16,258]{3,2,1,0:T(8,128)S(1)} %fusion.41, ...), kind=kLoop, calls=%fused_computation.107 | loop fusion | flops 10907648 | bytes 15549952 | tf_op jit(solution)/shard_map/reduce_sum | solution.py:165
  70.4 0.7 collective-permute-start.12
  71.1 0.7 collective-permute-start.11
  71.8 0.7 collective-permute-start.10
  72.4 4.6 %collective-permute-start.9 = (f32[16,256]{1,0:T(8,128)S(1)}, f32[16,256]{1,0:T(8,128)S(1)}, u32[]{:S(2)}, u32[]{:S(2)}) collective-permute-start(f32[16,256]{1,0:T(8,128)S(1)} %get-tuple-element.2), channel_id=1, source_target_pairs={{0,256},{64,320},{128,384},{192,448},{1,257},{65,321},{129,385},{1... | collective-permute-start | bytes 49160 | tf_op jit(solution)/shard_map/ppermute | solution.py:25
  77.0 1.9 %collective-permute-start.8 = (f32[16,256]{1,0:T(8,128)S(1)}, f32[16,256]{1,0:T(8,128)S(1)}, u32[]{:S(2)}, u32[]{:S(2)}) collective-permute-start(f32[16,256]{1,0:T(8,128)S(1)} %get-tuple-element.2), channel_id=1, source_target_pairs={{0,192},{64,256},{128,320},{192,384},{256,448},{1,193},{65,257},{1... | collective-permute-start | bytes 49160 | tf_op jit(solution)/shard_map/ppermute | solution.py:25
  78.9 4.0 %collective-permute-start.6 = (f32[16,256]{1,0:T(8,128)S(1)}, f32[16,256]{1,0:T(8,128)S(1)}, u32[]{:S(2)}, u32[]{:S(2)}) collective-permute-start(f32[16,256]{1,0:T(8,128)S(1)} %get-tuple-element.2), channel_id=1, source_target_pairs={{0,64},{64,128},{128,192},{192,256},{256,320},{320,384},{384,448},... | collective-permute-start | bytes 49160 | tf_op jit(solution)/shard_map/ppermute | solution.py:25
  82.9 1.9 %collective-permute-start.7 = (f32[16,256]{1,0:T(8,128)S(1)}, f32[16,256]{1,0:T(8,128)S(1)}, u32[]{:S(2)}, u32[]{:S(2)}) collective-permute-start(f32[16,256]{1,0:T(8,128)S(1)} %get-tuple-element.2), channel_id=1, source_target_pairs={{0,128},{64,192},{128,256},{192,320},{256,384},{320,448},{1,129},{... | collective-permute-start | bytes 49160 | tf_op jit(solution)/shard_map/ppermute | solution.py:25
  84.9 5.2 %collective-permute-done.7 = f32[16,256]{1,0:T(8,128)S(1)} collective-permute-done((f32[16,256]{1,0:T(8,128)S(1)}, f32[16,256]{1,0:T(8,128)S(1)}, u32[]{:S(2)}, u32[]{:S(2)}) %collective-permute-start.7) | collective-permute-done | bytes 16416 | tf_op jit(solution)/shard_map/ppermute | solution.py:25
  90.1 0.8 add_multiply_fusion
  (42 shorter events, 0.5 us)
Async XLA Ops:
  0.6 1.7 %copy-start = (f32[4,3,16,256]{3,2,1,0:T(8,128)S(1)}, f32[4,3,16,256]{3,2,1,0:T(8,128)}, u32[]{:S(2)}) copy-start(f32[4,3,16,256]{3,2,1,0:T(8,128)} %param.7) | copy-start | bytes 589828
  0.6 19.7 %copy-start.7 = (f32[4]{0:T(128)S(1)}, f32[4]{0:T(128)}, u32[]{:S(2)}) copy-start(f32[4]{0:T(128)} %constant.90.clone) | copy-start | bytes 52
  0.7 19.7 %copy-start.8 = (f32[4]{0:T(128)S(1)}, f32[4]{0:T(128)}, u32[]{:S(2)}) copy-start(f32[4]{0:T(128)} %constant.91.clone) | copy-start | bytes 52
  0.7 27.1 %copy-start.2 = (f32[24,16,256]{2,1,0:T(8,128)S(1)}, f32[24,16,256]{2,1,0:T(8,128)}, u32[]{:S(2)}) copy-start(f32[24,16,256]{2,1,0:T(8,128)} %param.11) | copy-start | bytes 1179652
  0.7 27.1 %copy-start.3 = (f32[24,16,256]{2,1,0:T(8,128)S(1)}, f32[24,16,256]{2,1,0:T(8,128)}, u32[]{:S(2)}) copy-start(f32[24,16,256]{2,1,0:T(8,128)} %param.10) | copy-start | bytes 1179652
  0.7 10.3 %copy-start.6 = (s32[24]{0:T(128)S(1)}, s32[24]{0:T(128)}, u32[]{:S(2)}) copy-start(s32[24]{0:T(128)} %param.9) | copy-start | bytes 292
  4.4 16.5 %collective-permute-start.3 = (f32[60,16,3]{2,1,0:T(8,128)S(1)}, f32[60,16,3]{2,1,0:T(8,128)S(1)}, u32[]{:S(2)}, u32[]{:S(2)}) collective-permute-start(f32[60,16,3]{2,1,0:T(8,128)S(1)} %get-tuple-element.16), channel_id=1, source_target_pairs={{1,0},{2,1},{3,2},{4,3},{5,4},{6,5},{7,6},{8,7},{9,8},{10,9},{11,1... | collective-permute-start | bytes 34568 | tf_op jit(solution)/shard_map/ppermute | solution.py:25
  9.1 18.7 %collective-permute-start.2 = (f32[60,16,3]{2,1,0:T(8,128)S(1)}, f32[60,16,3]{2,1,0:T(8,128)S(1)}, u32[]{:S(2)}, u32[]{:S(2)}) collective-permute-start(f32[60,16,3]{2,1,0:T(8,128)S(1)} %get-tuple-element.15), channel_id=1, source_target_pairs={{0,1},{1,2},{2,3},{3,4},{4,5},{5,6},{6,7},{7,8},{8,9},{9,10},{10,1... | collective-permute-start | bytes 34568 | tf_op jit(solution)/shard_map/ppermute | solution.py:25
  11.1 8.3 %collective-permute-start.1 = (s32[3]{0:T(128)S(1)}, s32[3]{0:T(128)S(1)}, u32[]{:S(2)}, u32[]{:S(2)}) collective-permute-start(s32[3]{0:T(128)S(1)} %get-tuple-element.51), channel_id=1, source_target_pairs={{64,0},{128,64},{192,128},{256,192},{320,256},{384,320},{448,384},... | collective-permute-start | bytes 44 | tf_op jit(solution)/shard_map/ppermute | solution.py:25
  13.8 6.5 %collective-permute-start = (s32[3]{0:T(128)S(1)}, s32[3]{0:T(128)S(1)}, u32[]{:S(2)}, u32[]{:S(2)}) collective-permute-start(s32[3]{0:T(128)S(1)} %get-tuple-element.50), channel_id=1, source_target_pairs={{0,64},{64,128},{128,192},{192,256},{256,320},{320,384},{384,448},... | collective-permute-start | bytes 44 | tf_op jit(solution)/shard_map/ppermute | solution.py:25
  28.6 9.1 %collective-permute-start.5 = (f32[6,16,262]{2,1,0:T(8,128)S(1)}, f32[6,16,262]{2,1,0:T(8,128)S(1)}, u32[]{:S(2)}, u32[]{:S(2)}) collective-permute-start(f32[6,16,262]{2,1,0:T(8,128)S(1)} %fusion.74), channel_id=1, source_target_pairs={{64,0},{128,64},{192,128},{256,192},{320,256},{384,320},{448,384},... | collective-permute-start | bytes 301832 | tf_op jit(solution)/shard_map/ppermute | solution.py:25
  31.5 8.1 %collective-permute-start.4 = (f32[7,16,262]{2,1,0:T(8,128)S(1)}, f32[7,16,262]{2,1,0:T(8,128)S(1)}, u32[]{:S(2)}, u32[]{:S(2)}) collective-permute-start(f32[7,16,262]{2,1,0:T(8,128)S(1)} %fusion.66), channel_id=1, source_target_pairs={{0,64},{64,128},{128,192},{192,256},{256,320},{320,384},{384,448},... | collective-permute-start | bytes 352136 | tf_op jit(solution)/shard_map/ppermute | solution.py:25
  56.9 8.5 %copy-start.1 = (f32[4,30,16,262]{3,2,1,0:T(8,128)S(1)}, f32[4,30,16,262]{3,2,1,0:T(8,128)}, u32[]{:S(2)}) copy-start(f32[4,30,16,262]{3,2,1,0:T(8,128)} %get-tuple-element.26) | copy-start | bytes 6036484
  56.9 8.5 %copy-start.4 = (f32[24,16,256]{2,1,0:T(8,128)S(1)}, f32[24,16,256]{2,1,0:T(8,128)}, u32[]{:S(2)}) copy-start(f32[24,16,256]{2,1,0:T(8,128)} %get-tuple-element.7) | copy-start | bytes 1179652
  56.9 8.5 %copy-start.5 = (f32[24,16,256]{2,1,0:T(8,128)S(1)}, f32[24,16,256]{2,1,0:T(8,128)}, u32[]{:S(2)}) copy-start(f32[24,16,256]{2,1,0:T(8,128)} %get-tuple-element.8) | copy-start | bytes 1179652
  70.4 8.5 %collective-permute-start.12 = (f32[16,256]{1,0:T(8,128)S(1)}, f32[16,256]{1,0:T(8,128)S(1)}, u32[]{:S(2)}, u32[]{:S(2)}) collective-permute-start(f32[16,256]{1,0:T(8,128)S(1)} %get-tuple-element.2), channel_id=1, source_target_pairs={{0,448},{1,449},{2,450},{3,451},{4,452},{5,453},{6,454},{7,455},{8... | collective-permute-start | bytes 49160 | tf_op jit(solution)/shard_map/ppermute | solution.py:25
  71.1 11.8 %collective-permute-start.11 = (f32[16,256]{1,0:T(8,128)S(1)}, f32[16,256]{1,0:T(8,128)S(1)}, u32[]{:S(2)}, u32[]{:S(2)}) collective-permute-start(f32[16,256]{1,0:T(8,128)S(1)} %get-tuple-element.2), channel_id=1, source_target_pairs={{0,384},{64,448},{1,385},{65,449},{2,386},{66,450},{3,387},{67,451... | collective-permute-start | bytes 49160 | tf_op jit(solution)/shard_map/ppermute | solution.py:25
  71.8 13.1 %collective-permute-start.10 = (f32[16,256]{1,0:T(8,128)S(1)}, f32[16,256]{1,0:T(8,128)S(1)}, u32[]{:S(2)}, u32[]{:S(2)}) collective-permute-start(f32[16,256]{1,0:T(8,128)S(1)} %get-tuple-element.2), channel_id=1, source_target_pairs={{0,320},{64,384},{128,448},{1,321},{65,385},{129,449},{2,322},{66,... | collective-permute-start | bytes 49160 | tf_op jit(solution)/shard_map/ppermute | solution.py:25
  72.4 12.4 %collective-permute-start.9 = (f32[16,256]{1,0:T(8,128)S(1)}, f32[16,256]{1,0:T(8,128)S(1)}, u32[]{:S(2)}, u32[]{:S(2)}) collective-permute-start(f32[16,256]{1,0:T(8,128)S(1)} %get-tuple-element.2), channel_id=1, source_target_pairs={{0,256},{64,320},{128,384},{192,448},{1,257},{65,321},{129,385},{1... | collective-permute-start | bytes 49160 | tf_op jit(solution)/shard_map/ppermute | solution.py:25
  77.0 7.9 %collective-permute-start.8 = (f32[16,256]{1,0:T(8,128)S(1)}, f32[16,256]{1,0:T(8,128)S(1)}, u32[]{:S(2)}, u32[]{:S(2)}) collective-permute-start(f32[16,256]{1,0:T(8,128)S(1)} %get-tuple-element.2), channel_id=1, source_target_pairs={{0,192},{64,256},{128,320},{192,384},{256,448},{1,193},{65,257},{1... | collective-permute-start | bytes 49160 | tf_op jit(solution)/shard_map/ppermute | solution.py:25
  78.9 5.9 %collective-permute-start.6 = (f32[16,256]{1,0:T(8,128)S(1)}, f32[16,256]{1,0:T(8,128)S(1)}, u32[]{:S(2)}, u32[]{:S(2)}) collective-permute-start(f32[16,256]{1,0:T(8,128)S(1)} %get-tuple-element.2), channel_id=1, source_target_pairs={{0,64},{64,128},{128,192},{192,256},{256,320},{320,384},{384,448},... | collective-permute-start | bytes 49160 | tf_op jit(solution)/shard_map/ppermute | solution.py:25
  82.9 7.1 %collective-permute-start.7 = (f32[16,256]{1,0:T(8,128)S(1)}, f32[16,256]{1,0:T(8,128)S(1)}, u32[]{:S(2)}, u32[]{:S(2)}) collective-permute-start(f32[16,256]{1,0:T(8,128)S(1)} %get-tuple-element.2), channel_id=1, source_target_pairs={{0,128},{64,192},{128,256},{192,320},{256,384},{320,448},{1,129},{... | collective-permute-start | bytes 49160 | tf_op jit(solution)/shard_map/ppermute | solution.py:25

commit v4 on v3

--- a/solution.py
+++ b/solution.py
@@ -63,7 +63,7 @@
     return first + second + 2.0 * square_shear * shear_stress
 
 
-def sweep(padded, source, stiffening, coupling_up, coupling_down, cond_rows, cond_cols, cond_cross):
+def sweep(padded, source, stiffening, coupling_up, coupling_down, cond_rows, cond_cols, cond_cross, scale):
     widths = [(0, 0)] * (padded.ndim - 2) + [(1, 1), (0, 0)]
     framed = jnp.pad(padded, widths)
     centre = framed[..., 1:-1, 1:-1, 1:-1]
@@ -88,8 +88,7 @@
         + coupling_down * (centre - beneath)
         + stiffening * centre
     )
-    diagonal_sum = 2.0 * cond_rows + 2.0 * cond_cols + coupling_up + coupling_down + stiffening
-    return centre + relaxation * (source - image) / diagonal_sum
+    return centre + (source - image) * scale
 
 
 def trim(array, by, ply_dim, col_dim):
@@ -117,13 +116,40 @@
     strain_e = packed[: cases * 3].reshape(cases, 3, rows, width)
     stiff_c = packed[cases * 3 : cases * 3 + ply_local]
     inter_c = packed[cases * 3 + ply_local :]
+    angle_plane = jnp.zeros((1, rows, width), jnp.float32)
     below = passed_along(
-        jnp.concatenate([stiff_c[ply_local - halo :], inter_c[ply_local - halo - 1 :]], axis=0),
+        jnp.concatenate(
+            [
+                stiff_c[ply_local - halo :],
+                inter_c[ply_local - halo - 1 :],
+                angle_plane.at[0, 0, :halo].set(angle_ids[ply_local - halo :].astype(jnp.float32)),
+            ],
+            axis=0,
+        ),
         "ply",
         1,
     )
-    above = passed_along(jnp.concatenate([stiff_c[:halo], inter_c[:halo]], axis=0), "ply", -1)
-    angles = with_halos(angle_ids, "ply", 0, halo, halo)
+    above = passed_along(
+        jnp.concatenate(
+            [
+                stiff_c[:halo],
+                inter_c[:halo],
+                angle_plane.at[0, 0, :halo].set(angle_ids[:halo].astype(jnp.float32)),
+            ],
+            axis=0,
+        ),
+        "ply",
+        -1,
+    )
+    angles = jnp.concatenate(
+        [
+            below[2 * halo + 1, 0, :halo].astype(jnp.int32),
+            angle_ids,
+            above[2 * halo, 0, :halo].astype(jnp.int32),
+        ]
+    )
+    below = below[: 2 * halo + 1]
+    above = above[: 2 * halo]
     stiff_e = jnp.concatenate([below[:halo], stiff_c, above[:halo]], axis=0)
     inter_all = jnp.concatenate([below[halo:], inter_c, above[halo:]], axis=0)
     up_e = inter_all[1:]
@@ -145,7 +171,8 @@
     ).astype(jnp.float32)
 
     diagonal_sum = 2.0 * cond_rows + 2.0 * cond_cols + up_e + down_e + stiff_e
-    adjoint = relaxation * source_e / diagonal_sum * inside
+    scale_e = relaxation / diagonal_sum
+    adjoint = source_e * scale_e * inside
     for iteration in range(1, ITERS):
         by = iteration
         adjoint = sweep(
@@ -157,17 +184,19 @@
             cond_rows[by : cond_rows.shape[0] - by],
             cond_cols[by : cond_cols.shape[0] - by],
             cond_cross[by : cond_cross.shape[0] - by],
+            trim(scale_e, by, 0, 2),
         )
         if iteration < ITERS - 1:
             adjoint = adjoint * trim(inside, by, 0, 2)
     source = trim(source_e, halo, 1, 3)
     product = adjoint * source
     total = jnp.sum(product, axis=(0, 1))
-    arrivals = [passed_along(total, "ply", shift) for shift in range(1, ply_count)]
+    totals = lax.all_to_all(
+        jnp.broadcast_to(total[None], (ply_count,) + total.shape), "ply", 0, 0, tiled=True
+    )
+    lower = (jnp.arange(ply_count) < lax.axis_index("ply")).astype(jnp.float32)
+    prefix = jnp.sum(totals * lower[:, None, None], axis=0)
     running = jnp.cumsum(jnp.sum(product, axis=0), axis=0)
-    prefix = arrivals[0]
-    for arrived in arrivals[1:]:
-        prefix = prefix + arrived
     through = (running + prefix[None]) / (ply_local * ply_count)
     return (adjoint, through)
 

time: 91.3 us -> 87.3 us (0.956)
  the two profiles are of different devices: /device:TPU:262 before, /device:TPU:448 now
where the time goes in v4:
time: 87.3 us; the launch traced here: 86.5 us
  other arithmetic  32.9 us (38%)
  waiting for transfers between devices  24.9 us (29%)
  starting transfers between devices  18.2 us (21%)
  local copies, waits for them, and re-layouts  9.64 us (11%)
  between operations  0.94 us (1%)
    ppermute x4, waiting for transfers between devices, passed_along(): return lax.ppermute(array, axis, pairs)  18.3 us
    mul x2, other arithmetic, body(): adjoint = adjoint * trim(inside, by, 0, 2)  17 us
    ppermute x4, starting transfers between devices, passed_along(): return lax.ppermute(array, axis, pairs)  13.3 us
    slice x7, local copies, waits for them, and re-layouts, trim(): return lax.slice_in_dim(array, by, array.shape[col_dim] - by, axis=col_dim)  7.58 us
    all_to_all x1, waiting for transfers between devices, body(): lax.all_to_all(jnp.broadcast_to(total[None], (ply_count,) + total.shape),...  6.57 us
    reduce_sum x1, other arithmetic, body(): total = jnp.sum(product, axis=(0, 1))  5.06 us
    all_to_all x1, starting transfers between devices, body(): lax.all_to_all(jnp.broadcast_to(total[None], (ply_count,) + total.shape),...  4.94 us
    mul x1, other arithmetic, body(): adjoint = source_e * scale_e * inside  3.57 us
  transfers between devices with their start and end apart: 5, of which 4 were waited for; matrix products, arithmetic and copies ran while one was open for 1% of the time, Pallas kernels for 0%

profile of v4, /device:TPU:448, one launch (start us, length us, event | category | flops | bytes accessed | tf_op | source)
XLA Modules:
  0.0 86.5 jit_solution(17374474782701279292)
XLA Ops:
  0.7 0.7 compare_select_fusion
  1.4 0.7 compare_and_fusion.1
  2.1 0.1 broadcast_in_dim.18
  2.2 0.1 broadcast_in_dim.19
  2.3 0.6 gather_fusion
  2.8 0.1 bitcast_select_fusion
  2.9 1.2 %pad_maximum_fusion = f32[60,16,256]{2,1,0:T(8,128)S(1)} fusion(f32[24,16,256]{2,1,0:T(8,128)} %param.15, f32[24,16,256]{2,1,0:T(8,128)} %param.14, f32[12,16,256]{2,1,0:T(8,128)S(1)} %bitcast_select_fusion), kind=kLoop, calls=%fused_computation.96 | loop fusion | flops 491520 | bytes 1966080 | tf_op jit(solution)/shard_map/concatenate | solution.py:111
  4.1 0.2 fusion.92
  4.3 1.9 %collective-permute-start = (f32[60,16,3]{2,1,0:T(8,128)S(1)}, f32[60,16,3]{2,1,0:T(8,128)S(1)}, u32[]{:S(2)}, u32[]{:S(2)}) collective-permute-start(f32[60,16,3]{2,1,0:T(8,128)S(1)} %get-tuple-element.35), channel_id=1, source_target_pairs={{0,1},{1,2},{2,3},{3,4},{4,5},{5,6},{6,7},{7,8},{8,9},{9,10},{10,1... | collective-permute-start | bytes 34568 | tf_op jit(solution)/shard_map/ppermute | solution.py:25
  6.2 6.7 %collective-permute-start.1 = (f32[60,16,3]{2,1,0:T(8,128)S(1)}, f32[60,16,3]{2,1,0:T(8,128)S(1)}, u32[]{:S(2)}, u32[]{:S(2)}) collective-permute-start(f32[60,16,3]{2,1,0:T(8,128)S(1)} %get-tuple-element.36), channel_id=1, source_target_pairs={{1,0},{2,1},{3,2},{4,3},{5,4},{6,5},{7,6},{8,7},{9,8},{10,9},{11,1... | collective-permute-start | bytes 34568 | tf_op jit(solution)/shard_map/ppermute | solution.py:25
  12.9 0.1 and_convert_fusion.1
  13.0 0.1 and_convert_fusion
  13.1 0.1 slice_bitcast_fusion.4
  13.2 0.1 slice_bitcast_fusion.3
  13.2 0.1 convert_bitcast_fusion.1
  13.3 6.9 %collective-permute-done = f32[60,16,3]{2,1,0:T(8,128)S(1)} collective-permute-done((f32[60,16,3]{2,1,0:T(8,128)S(1)}, f32[60,16,3]{2,1,0:T(8,128)S(1)}, u32[]{:S(2)}, u32[]{:S(2)}) %collective-permute-start) | collective-permute-done | bytes 11552 | tf_op jit(solution)/shard_map/ppermute | solution.py:25
  20.2 4.3 %collective-permute-done.1 = f32[60,16,3]{2,1,0:T(8,128)S(1)} collective-permute-done((f32[60,16,3]{2,1,0:T(8,128)S(1)}, f32[60,16,3]{2,1,0:T(8,128)S(1)}, u32[]{:S(2)}, u32[]{:S(2)}) %collective-permute-start.1) | collective-permute-done | bytes 11552 | tf_op jit(solution)/shard_map/ppermute | solution.py:25
  24.5 0.2 pad_maximum_fusion.5
  24.7 0.1 select_maximum_fusion.3
  24.9 3.4 %collective-permute-start.2 = (f32[8,16,262]{2,1,0:T(8,128)S(1)}, f32[8,16,262]{2,1,0:T(8,128)S(1)}, u32[]{:S(2)}, u32[]{:S(2)}) collective-permute-start(f32[8,16,262]{2,1,0:T(8,128)S(1)} %select_maximum_fusion.3), channel_id=1, source_target_pairs={{0,64},{64,128},{128,192},{192,256},{256,320},{320,384},{384,448},... | collective-permute-start | bytes 402440 | tf_op jit(solution)/shard_map/ppermute | solution.py:25
  28.3 0.1 select_maximum_fusion.10
  28.4 1.3 %collective-permute-start.3 = (f32[7,16,262]{2,1,0:T(8,128)S(1)}, f32[7,16,262]{2,1,0:T(8,128)S(1)}, u32[]{:S(2)}, u32[]{:S(2)}) collective-permute-start(f32[7,16,262]{2,1,0:T(8,128)S(1)} %select_maximum_fusion.10), channel_id=1, source_target_pairs={{64,0},{128,64},{192,128},{256,192},{320,256},{384,320},{448,384},... | collective-permute-start | bytes 352136 | tf_op jit(solution)/shard_map/ppermute | solution.py:25
  29.7 0.3 pad_maximum_fusion.3
  30.0 7.1 %collective-permute-done.3 = f32[7,16,262]{2,1,0:T(8,128)S(1)} collective-permute-done((f32[7,16,262]{2,1,0:T(8,128)S(1)}, f32[7,16,262]{2,1,0:T(8,128)S(1)}, u32[]{:S(2)}, u32[]{:S(2)}) %collective-permute-start.3) | collective-permute-done | bytes 117408 | tf_op jit(solution)/shard_map/ppermute | solution.py:25
  37.1 0.1 pad_add_fusion
  37.2 0.1 select_reduce_fusion.1
  37.3 0.1 multiply_bitcast_fusion.1
  37.4 0.1 multiply_bitcast_fusion.2
  37.6 1.2 %fusion.93 = (f32[28,16,260]{2,1,0:T(8,128)S(1)}, f32[28,16,260]{2,1,0:T(8,128)}) fusion(f32[31,16,262]{2,1,0:T(8,128)S(1)} %pad_maximum_fusion.1), kind=kLoop, calls=%fused_computation.206 | loop fusion | bytes 1863680 | tf_op jit(solution)/shard_map/slice | solution.py:98
  38.8 0.3 fusion.63
  39.2 1.1 %slice.455 = f32[28,16,260]{2,1,0:T(8,128)} slice(f32[30,16,262]{2,1,0:T(8,128)S(1)} %get-tuple-element.34), slice={[1:29], [0:16], [1:261]} | slice | bytes 931840 | tf_op jit(solution)/shard_map/slice | solution.py:98
  40.3 1.1 %slice.467 = f32[26,16,258]{2,1,0:T(8,128)} slice(f32[30,16,262]{2,1,0:T(8,128)S(1)} %get-tuple-element.34), slice={[2:28], [0:16], [2:260]} | slice | bytes 858624 | tf_op jit(solution)/shard_map/slice | solution.py:98
  41.3 1.1 %slice.456 = f32[28,16,260]{2,1,0:T(8,128)} slice(f32[30,16,262]{2,1,0:T(8,128)S(1)} %get-tuple-element.33), slice={[1:29], [0:16], [1:261]} | slice | bytes 931840 | tf_op jit(solution)/shard_map/slice | solution.py:98
  42.4 1.1 %slice.468 = f32[26,16,258]{2,1,0:T(8,128)} slice(f32[30,16,262]{2,1,0:T(8,128)S(1)} %get-tuple-element.33), slice={[2:28], [0:16], [2:260]} | slice | bytes 858624 | tf_op jit(solution)/shard_map/slice | solution.py:98
  43.6 1.1 %slice.462 = f32[26,16,258]{2,1,0:T(8,128)} slice(f32[31,16,262]{2,1,0:T(8,128)S(1)} %pad_maximum_fusion.1), slice={[3:29], [0:16], [2:260]} | slice | bytes 858624 | tf_op jit(solution)/shard_map/slice | solution.py:98
  44.7 1.1 %fusion.65 = f32[26,16,258]{2,1,0:T(8,128)} fusion(f32[4,16,262]{2,1,0:T(8,128)S(1)} %slice.441, f32[24,16,262]{2,1,0:T(8,128)S(1)} %pad_maximum_fusion.3), kind=kLoop, calls=%fused_computation.111 | loop fusion | flops 107328 | bytes 898816 | tf_op jit(solution)/shard_map/concatenate | solution.py:154
  45.8 0.1 multiply_bitcast_fusion
  45.9 0.9 %slice.476 = f32[24,16,256]{2,1,0:T(8,128)} slice(f32[30,16,262]{2,1,0:T(8,128)S(1)} %get-tuple-element.33), slice={[3:27], [0:16], [3:259]} | slice | bytes 786432 | tf_op jit(solution)/shard_map/slice | solution.py:98
  46.9 0.9 %pad_maximum_fusion.4 = f32[24,16,256]{2,1,0:T(8,128)} fusion(f32[24,16,262]{2,1,0:T(8,128)S(1)} %pad_maximum_fusion.3, f32[4,16,262]{2,1,0:T(8,128)S(1)} %slice.441), kind=kLoop, calls=%fused_computation.115 | loop fusion | flops 98304 | bytes 862720 | tf_op jit(solution)/shard_map/concatenate | solution.py:154
  47.8 3.6 %multiply_multiply_fusion = (f32[4,30,16,262]{3,2,1,0:T(8,128)S(1)}, f32[4,30,16,262]{3,2,1,0:T(8,128)}) fusion(f32[30,262]{1,0:T(8,128)S(1)} %and_convert_fusion.1, f32[30,16,262]{2,1,0:T(8,128)S(1)} %get-tuple-element.33, f32[30]{0:T(128)S(1)} %get-tuple-element.51, f32[4,16,262]{2,1,0:T(8,128)S(1)} %fusion.78, f32[30]{0:T(128)S(1)} %get-tuple-element.52, ...), kind=kLoop, calls=%fused_computation.21 | loop fusion | flops 11569920 | bytes 4827688 | tf_op jit(solution)/shard_map/mul | solution.py:175
  51.4 8.5 %fusion.11 = f32[4,28,16,260]{3,2,1,0:T(8,128)S(1)} fusion(f32[4,30,16,262]{3,2,1,0:T(8,128)S(1)} %get-tuple-element.39, f32[4,30,16,262]{3,2,1,0:T(8,128)} %get-tuple-element.40, f32[28,260]{1,0:T(8,128)S(1)} %slice_bitcast_fusion.4, f32[28,16,260]{2,1,0:T(8,128)} %slice.456, f32[28,16,260]{2,1,0:T(8,128)} %slice.455, f32[28,16,260]{2,1,0:T(8,128)} %get-tuple-element.38, ...), kind=kLoop, calls=%fused_computation.34 | loop fusion | flops 11648000 | bytes 22575616 | tf_op jit(solution)/shard_map/mul | solution.py:190
  59.9 8.4 %fusion.31 = f32[4,26,16,258]{3,2,1,0:T(8,128)S(1)} fusion(f32[4,28,16,260]{3,2,1,0:T(8,128)S(1)} %fusion.11, f32[4,30,16,262]{3,2,1,0:T(8,128)} %get-tuple-element.40, f32[26,258]{1,0:T(8,128)S(1)} %slice_bitcast_fusion.3, f32[26,16,258]{2,1,0:T(8,128)} %slice.468, f32[26,16,258]{2,1,0:T(8,128)} %slice.467, f32[26,16,258]{2,1,0:T(8,128)} %fusion.65, ...), kind=kLoop, calls=%fused_computation.57 | loop fusion | flops 10732800 | bytes 20734464 | tf_op jit(solution)/shard_map/mul | solution.py:190
  68.4 5.1 %fusion.66 = (f32[16,256]{1,0:T(8,128)S(1)}, f32[24,16,256]{2,1,0:T(8,128)S(1)}, f32[4,24,16,256]{3,2,1,0:T(8,128)}) fusion(f32[4,30,16,262]{3,2,1,0:T(8,128)S(1)} %copy-done.1, f32[24,16,256]{2,1,0:T(8,128)S(1)} %copy-done.4, f32[24,16,256]{2,1,0:T(8,128)S(1)} %copy-done.3, f32[4,26,16,258]{3,2,1,0:T(8,128)S(1)} %fusion.31, ...), kind=kLoop, calls=%fused_computation.112 | loop fusion | flops 10514432 | bytes 15549952 | tf_op jit(solution)/shard_map/reduce_sum | solution.py:193
  73.5 0.7 broadcast_in_dim.23
  74.1 4.9 %all-to-all-start = ((f32[8,16,256]{2,1,0:T(8,128)}), f32[8,16,256]{2,1,0:T(8,128)S(1)}, u32[]{:S(2)}, u32[]{:S(2)}) async-start(f32[8,16,256]{2,1,0:T(8,128)} %broadcast_in_dim.23), calls=%async_computation | async-start | bytes 262144 | tf_op jit(solution)/shard_map/all_to_all | solution.py:194
  79.1 6.6 %all-to-all-done = f32[8,16,256]{2,1,0:T(8,128)S(1)} async-done(((f32[8,16,256]{2,1,0:T(8,128)}), f32[8,16,256]{2,1,0:T(8,128)S(1)}, u32[]{:S(2)}, u32[]{:S(2)}) %all-to-all-start) | async-done | bytes 131104 | tf_op jit(solution)/shard_map/all_to_all | solution.py:194
  85.6 0.1 multiply_reduce_fusion
  85.7 0.8 fusion.59
  (36 shorter events, 0.4 us)
Async XLA Ops:
  0.6 1.6 %copy-start = (f32[4,3,16,256]{3,2,1,0:T(8,128)S(1)}, f32[4,3,16,256]{3,2,1,0:T(8,128)}, u32[]{:S(2)}) copy-start(f32[4,3,16,256]{3,2,1,0:T(8,128)} %param.11) | copy-start | bytes 589828
  0.6 23.8 %copy-start.3 = (f32[24,16,256]{2,1,0:T(8,128)S(1)}, f32[24,16,256]{2,1,0:T(8,128)}, u32[]{:S(2)}) copy-start(f32[24,16,256]{2,1,0:T(8,128)} %param.14) | copy-start | bytes 1179652
  0.7 23.8 %copy-start.2 = (f32[24,16,256]{2,1,0:T(8,128)S(1)}, f32[24,16,256]{2,1,0:T(8,128)}, u32[]{:S(2)}) copy-start(f32[24,16,256]{2,1,0:T(8,128)} %param.15) | copy-start | bytes 1179652
  0.7 12.6 %copy-start.6 = (s32[24]{0:T(128)S(1)}, s32[24]{0:T(128)}, u32[]{:S(2)}) copy-start(s32[24]{0:T(128)} %param.13) | copy-start | bytes 292
  4.3 15.9 %collective-permute-start = (f32[60,16,3]{2,1,0:T(8,128)S(1)}, f32[60,16,3]{2,1,0:T(8,128)S(1)}, u32[]{:S(2)}, u32[]{:S(2)}) collective-permute-start(f32[60,16,3]{2,1,0:T(8,128)S(1)} %get-tuple-element.35), channel_id=1, source_target_pairs={{0,1},{1,2},{2,3},{3,4},{4,5},{5,6},{6,7},{7,8},{8,9},{9,10},{10,1... | collective-permute-start | bytes 34568 | tf_op jit(solution)/shard_map/ppermute | solution.py:25
  6.2 18.3 %collective-permute-start.1 = (f32[60,16,3]{2,1,0:T(8,128)S(1)}, f32[60,16,3]{2,1,0:T(8,128)S(1)}, u32[]{:S(2)}, u32[]{:S(2)}) collective-permute-start(f32[60,16,3]{2,1,0:T(8,128)S(1)} %get-tuple-element.36), channel_id=1, source_target_pairs={{1,0},{2,1},{3,2},{4,3},{5,4},{6,5},{7,6},{8,7},{9,8},{10,9},{11,1... | collective-permute-start | bytes 34568 | tf_op jit(solution)/shard_map/ppermute | solution.py:25
  24.8 12.4 %copy-start.7 = (f32[4]{0:T(128)S(1)}, f32[4]{0:T(128)}, u32[]{:S(2)}) copy-start(f32[4]{0:T(128)} %constant.132.clone) | copy-start | bytes 52
  24.8 12.4 %copy-start.8 = (f32[4]{0:T(128)S(1)}, f32[4]{0:T(128)}, u32[]{:S(2)}) copy-start(f32[4]{0:T(128)} %constant.133.clone) | copy-start | bytes 52
  24.9 12.3 %collective-permute-start.2 = (f32[8,16,262]{2,1,0:T(8,128)S(1)}, f32[8,16,262]{2,1,0:T(8,128)S(1)}, u32[]{:S(2)}, u32[]{:S(2)}) collective-permute-start(f32[8,16,262]{2,1,0:T(8,128)S(1)} %select_maximum_fusion.3), channel_id=1, source_target_pairs={{0,64},{64,128},{128,192},{192,256},{256,320},{320,384},{384,448},... | collective-permute-start | bytes 402440 | tf_op jit(solution)/shard_map/ppermute | solution.py:25
  28.4 8.7 %collective-permute-start.3 = (f32[7,16,262]{2,1,0:T(8,128)S(1)}, f32[7,16,262]{2,1,0:T(8,128)S(1)}, u32[]{:S(2)}, u32[]{:S(2)}) collective-permute-start(f32[7,16,262]{2,1,0:T(8,128)S(1)} %select_maximum_fusion.10), channel_id=1, source_target_pairs={{64,0},{128,64},{192,128},{256,192},{320,256},{384,320},{448,384},... | collective-permute-start | bytes 352136 | tf_op jit(solution)/shard_map/ppermute | solution.py:25
  59.9 8.5 %copy-start.1 = (f32[4,30,16,262]{3,2,1,0:T(8,128)S(1)}, f32[4,30,16,262]{3,2,1,0:T(8,128)}, u32[]{:S(2)}) copy-start(f32[4,30,16,262]{3,2,1,0:T(8,128)} %get-tuple-element.40) | copy-start | bytes 6036484
  59.9 8.5 %copy-start.4 = (f32[24,16,256]{2,1,0:T(8,128)S(1)}, f32[24,16,256]{2,1,0:T(8,128)}, u32[]{:S(2)}) copy-start(f32[24,16,256]{2,1,0:T(8,128)} %slice.476) | copy-start | bytes 1179652
  59.9 8.5 %copy-start.5 = (f32[24,16,256]{2,1,0:T(8,128)S(1)}, f32[24,16,256]{2,1,0:T(8,128)}, u32[]{:S(2)}) copy-start(f32[24,16,256]{2,1,0:T(8,128)} %pad_maximum_fusion.4) | copy-start | bytes 1179652
  74.1 11.5 %all-to-all-start = ((f32[8,16,256]{2,1,0:T(8,128)}), f32[8,16,256]{2,1,0:T(8,128)S(1)}, u32[]{:S(2)}, u32[]{:S(2)}) async-start(f32[8,16,256]{2,1,0:T(8,128)} %broadcast_in_dim.23), calls=%async_computation | async-start | bytes 262144 | tf_op jit(solution)/shard_map/all_to_all | solution.py:194

commit v5 on v4

--- a/solution.py
+++ b/solution.py
@@ -63,7 +63,7 @@
     return first + second + 2.0 * square_shear * shear_stress
 
 
-def sweep(padded, source, stiffening, coupling_up, coupling_down, cond_rows, cond_cols, cond_cross, scale):
+def sweep(padded, source, stiffening, coupling_up, coupling_down, cond_rows, cond_cols, cond_cross):
     widths = [(0, 0)] * (padded.ndim - 2) + [(1, 1), (0, 0)]
     framed = jnp.pad(padded, widths)
     centre = framed[..., 1:-1, 1:-1, 1:-1]
@@ -88,7 +88,8 @@
         + coupling_down * (centre - beneath)
         + stiffening * centre
     )
-    return centre + (source - image) * scale
+    diagonal_sum = 2.0 * cond_rows + 2.0 * cond_cols + coupling_up + coupling_down + stiffening
+    return centre + relaxation * (source - image) / diagonal_sum
 
 
 def trim(array, by, ply_dim, col_dim):
@@ -171,8 +172,7 @@
     ).astype(jnp.float32)
 
     diagonal_sum = 2.0 * cond_rows + 2.0 * cond_cols + up_e + down_e + stiff_e
-    scale_e = relaxation / diagonal_sum
-    adjoint = source_e * scale_e * inside
+    adjoint = relaxation * source_e / diagonal_sum * inside
     for iteration in range(1, ITERS):
         by = iteration
         adjoint = sweep(
@@ -184,7 +184,6 @@
             cond_rows[by : cond_rows.shape[0] - by],
             cond_cols[by : cond_cols.shape[0] - by],
             cond_cross[by : cond_cross.shape[0] - by],
-            trim(scale_e, by, 0, 2),
         )
         if iteration < ITERS - 1:
             adjoint = adjoint * trim(inside, by, 0, 2)

time: 87.3 us -> 85.1 us (0.975)
  local copies, waits for them, and re-layouts: 9.64 us -> 1.84 us
  starting transfers between devices: 18.2 us -> 21.4 us
  other arithmetic: 32.9 us -> 35.7 us
    slice x7 -> x0, local copies, waits for them, and re-layouts: 7.58 us -> none  [trim(): return lax.slice_in_dim(array, by, array.shape[col_dim] - by, axis=col_dim)]
    all_to_all x1, starting transfers between devices: 4.94 us -> 8.06 us  [body(): lax.all_to_all(jnp.broadcast_to(total[None], (ply_count,) + total.shape),...]
    add x1 -> x2, other arithmetic: 0.01 us -> 3.13 us  [sweep(): 2.0 * cond_rows + 2.0 * cond_cols + coupling_up + coupling_down + stiffening]
    concatenate x3 -> x1, other arithmetic: 2.05 us -> 0.05 us  [body(): inter_all = jnp.concatenate([below[halo:], inter_c, above[halo:]], axis=0)]
    slice x0 -> x1, other arithmetic: none -> 1.73 us  [trim(): return lax.slice_in_dim(array, by, array.shape[col_dim] - by, axis=col_dim)]
    mul x4 -> x5, other arithmetic: 3.79 us -> 3.9 us  [the longest x1 3.66 us: body(): adjoint = relaxation * source_e / diagonal_sum * inside]
  transfers between devices with their start and end apart: 5 -> 5, of which waited for: 4 -> 5; matrix products, arithmetic and copies ran while one was open for 1% -> 1% of each run, Pallas kernels for 0% -> 0%
where the time goes in v5:
time: 85.1 us; the launch traced here: 84.6 us
  other arithmetic  35.7 us (42%)
  waiting for transfers between devices  24.7 us (29%)
  starting transfers between devices  21.4 us (25%)
  local copies, waits for them, and re-layouts  1.84 us (2%)
  between operations  0.93 us (1%)
    ppermute x4, waiting for transfers between devices, passed_along(): return lax.ppermute(array, axis, pairs)  18.1 us
    mul x2, other arithmetic, body(): adjoint = adjoint * trim(inside, by, 0, 2)  16.9 us
    ppermute x4, starting transfers between devices, passed_along(): return lax.ppermute(array, axis, pairs)  13.4 us
    all_to_all x1, starting transfers between devices, body(): lax.all_to_all(jnp.broadcast_to(total[None], (ply_count,) + total.shape),...  8.06 us
    all_to_all x1, waiting for transfers between devices, body(): lax.all_to_all(jnp.broadcast_to(total[None], (ply_count,) + total.shape),...  6.57 us
    reduce_sum x1, other arithmetic, body(): total = jnp.sum(product, axis=(0, 1))  5.04 us
    mul x1, other arithmetic, body(): adjoint = relaxation * source_e / diagonal_sum * inside  3.66 us
    add x2, other arithmetic, sweep(): 2.0 * cond_rows + 2.0 * cond_cols + coupling_up + coupling_down + stiffening  3.13 us
  transfers between devices with their start and end apart: 5, of which 5 were waited for; matrix products, arithmetic and copies ran while one was open for 1% of the time, Pallas kernels for 0%

profile of v5, /device:TPU:448, one launch (start us, length us, event | category | flops | bytes accessed | tf_op | source)
XLA Modules:
  0.0 84.6 jit_solution(8657772378228076390)
XLA Ops:
  0.6 0.0 copy-start
  0.6 0.0 copy-start.2
  0.7 0.7 compare_select_fusion
  1.4 0.7 compare_and_fusion.1
  2.1 0.1 broadcast_in_dim.18
  2.2 0.1 broadcast_in_dim.19
  2.3 0.6 gather_fusion
  2.8 0.1 bitcast_select_fusion
  2.9 1.2 %pad_maximum_fusion = f32[60,16,256]{2,1,0:T(8,128)S(1)} fusion(f32[24,16,256]{2,1,0:T(8,128)} %param.15, f32[24,16,256]{2,1,0:T(8,128)} %param.14, f32[12,16,256]{2,1,0:T(8,128)S(1)} %bitcast_select_fusion), kind=kLoop, calls=%fused_computation.99 | loop fusion | flops 491520 | bytes 1966080 | tf_op jit(solution)/shard_map/concatenate | solution.py:112
  4.1 0.2 fusion.95
  4.3 5.6 %collective-permute-start.1 = (f32[60,16,3]{2,1,0:T(8,128)S(1)}, f32[60,16,3]{2,1,0:T(8,128)S(1)}, u32[]{:S(2)}, u32[]{:S(2)}) collective-permute-start(f32[60,16,3]{2,1,0:T(8,128)S(1)} %get-tuple-element.40), channel_id=1, source_target_pairs={{1,0},{2,1},{3,2},{4,3},{5,4},{6,5},{7,6},{8,7},{9,8},{10,9},{11,1... | collective-permute-start | bytes 34568 | tf_op jit(solution)/shard_map/ppermute | solution.py:25
  9.9 1.9 %collective-permute-start = (f32[60,16,3]{2,1,0:T(8,128)S(1)}, f32[60,16,3]{2,1,0:T(8,128)S(1)}, u32[]{:S(2)}, u32[]{:S(2)}) collective-permute-start(f32[60,16,3]{2,1,0:T(8,128)S(1)} %get-tuple-element.39), channel_id=1, source_target_pairs={{0,1},{1,2},{2,3},{3,4},{4,5},{5,6},{6,7},{7,8},{8,9},{9,10},{10,1... | collective-permute-start | bytes 34568 | tf_op jit(solution)/shard_map/ppermute | solution.py:25
  11.9 0.1 and_convert_fusion.1
  11.9 0.1 and_convert_fusion
  12.0 0.1 slice_bitcast_fusion.4
  12.1 0.1 slice_bitcast_fusion.3
  12.2 0.1 convert_bitcast_fusion.1
  12.3 9.3 %collective-permute-done.1 = f32[60,16,3]{2,1,0:T(8,128)S(1)} collective-permute-done((f32[60,16,3]{2,1,0:T(8,128)S(1)}, f32[60,16,3]{2,1,0:T(8,128)S(1)}, u32[]{:S(2)}, u32[]{:S(2)}) %collective-permute-start.1) | collective-permute-done | bytes 11552 | tf_op jit(solution)/shard_map/ppermute | solution.py:25
  21.5 6.0 %collective-permute-done = f32[60,16,3]{2,1,0:T(8,128)S(1)} collective-permute-done((f32[60,16,3]{2,1,0:T(8,128)S(1)}, f32[60,16,3]{2,1,0:T(8,128)S(1)}, u32[]{:S(2)}, u32[]{:S(2)}) %collective-permute-start) | collective-permute-done | bytes 11552 | tf_op jit(solution)/shard_map/ppermute | solution.py:25
  27.5 0.2 pad_maximum_fusion.5
  27.8 0.1 select_maximum_fusion.10
  27.9 0.0 copy-start.7
  27.9 0.0 copy-start.8
  27.9 1.3 %collective-permute-start.3 = (f32[7,16,262]{2,1,0:T(8,128)S(1)}, f32[7,16,262]{2,1,0:T(8,128)S(1)}, u32[]{:S(2)}, u32[]{:S(2)}) collective-permute-start(f32[7,16,262]{2,1,0:T(8,128)S(1)} %select_maximum_fusion.10), channel_id=1, source_target_pairs={{64,0},{128,64},{192,128},{256,192},{320,256},{384,320},{448,384},... | collective-permute-start | bytes 352136 | tf_op jit(solution)/shard_map/ppermute | solution.py:25
  29.2 0.1 select_maximum_fusion.3
  29.3 4.6 %collective-permute-start.2 = (f32[8,16,262]{2,1,0:T(8,128)S(1)}, f32[8,16,262]{2,1,0:T(8,128)S(1)}, u32[]{:S(2)}, u32[]{:S(2)}) collective-permute-start(f32[8,16,262]{2,1,0:T(8,128)S(1)} %select_maximum_fusion.3), channel_id=1, source_target_pairs={{0,64},{64,128},{128,192},{192,256},{256,320},{320,384},{384,448},... | collective-permute-start | bytes 402440 | tf_op jit(solution)/shard_map/ppermute | solution.py:25
  33.9 0.3 pad_maximum_fusion.3
  34.2 1.0 %collective-permute-done.3 = f32[7,16,262]{2,1,0:T(8,128)S(1)} collective-permute-done((f32[7,16,262]{2,1,0:T(8,128)S(1)}, f32[7,16,262]{2,1,0:T(8,128)S(1)}, u32[]{:S(2)}, u32[]{:S(2)}) %collective-permute-start.3) | collective-permute-done | bytes 117408 | tf_op jit(solution)/shard_map/ppermute | solution.py:25
  35.2 1.8 %collective-permute-done.2 = f32[8,16,262]{2,1,0:T(8,128)S(1)} collective-permute-done((f32[8,16,262]{2,1,0:T(8,128)S(1)}, f32[8,16,262]{2,1,0:T(8,128)S(1)}, u32[]{:S(2)}, u32[]{:S(2)}) %collective-permute-start.2) | collective-permute-done | bytes 134176 | tf_op jit(solution)/shard_map/ppermute | solution.py:25
  37.1 0.1 pad_add_fusion
  37.2 0.1 select_reduce_fusion.1
  37.3 0.1 slice_bitcast_fusion.6
  37.4 0.1 slice_bitcast_fusion.10
  37.4 0.1 slice_bitcast_fusion.8
  37.5 0.1 pad_maximum_fusion.1
  37.6 1.1 %add_add_fusion.2 = (f32[24,16,256]{2,1,0:T(8,128)}, f32[24,16,256]{2,1,0:T(8,128)}) fusion(f32[24,16,256]{2,1,0:T(8,128)S(1)} %copy-done.3, f32[24,16,256]{2,1,0:T(8,128)S(1)} %copy-done.2, f32[24]{0:T(128)S(1)} %get-tuple-element.64, f32[24,16,262]{2,1,0:T(8,128)S(1)} %pad_maximum_fusion.3, f32[4,16,262]{2,1,0:T(8,128)S(1)} %slice.423), kind=kLoop, calls=%fused_computation.120 | loop fusion | flops 393216 | bytes 2042464 | tf_op jit(solution)/shard_map/add | solution.py:91
  38.7 0.3 fusion.65
  39.0 1.7 %fusion.96 = (f32[28,16,260]{2,1,0:T(8,128)S(1)}, f32[28,16,260]{2,1,0:T(8,128)S(1)}, f32[28,16,260]{2,1,0:T(8,128)}, f32[28,16,260]{2,1,0:T(8,128)}) fusion(f32[31,16,262]{2,1,0:T(8,128)S(1)} %pad_maximum_fusion.1, f32[30,16,262]{2,1,0:T(8,128)S(1)} %get-tuple-element.38, f32[28]{0:T(128)S(1)} %get-tuple-element.70), kind=kLoop, calls=%fused_computation.214 | loop fusion | flops 349440 | bytes 3261552 | tf_op jit(solution)/shard_map/slice | solution.py:99
  40.7 2.0 %add_add_fusion.1 = (f32[26,16,258]{2,1,0:T(8,128)}, f32[26,16,258]{2,1,0:T(8,128)}, f32[26,16,258]{2,1,0:T(8,128)}, f32[26,16,258]{2,1,0:T(8,128)}) fusion(f32[26]{0:T(128)S(1)} %get-tuple-element.67, f32[30,16,262]{2,1,0:T(8,128)S(1)} %get-tuple-element.38, f32[31,16,262]{2,1,0:T(8,128)S(1)} %pad_maximum_fusion.1, ...), kind=kLoop, calls=%fused_computation.115 | loop fusion | flops 429312 | bytes 3045480 | tf_op jit(solution)/shard_map/add | solution.py:91
  42.8 3.7 %divide_multiply_fusion = (f32[4,30,16,262]{3,2,1,0:T(8,128)S(1)}, f32[4,30,16,262]{3,2,1,0:T(8,128)}) fusion(f32[30,262]{1,0:T(8,128)S(1)} %and_convert_fusion.1, f32[30,16,262]{2,1,0:T(8,128)S(1)} %get-tuple-element.37, f32[30]{0:T(128)S(1)} %get-tuple-element.59, f32[4,16,262]{2,1,0:T(8,128)S(1)} %fusion.80, f32[30]{0:T(128)S(1)} %get-tuple-element.60, ...), kind=kLoop, calls=%fused_computation.21 | loop fusion | flops 12072960 | bytes 4827688 | tf_op jit(solution)/shard_map/mul | solution.py:175
  46.4 8.4 %fusion.20 = f32[4,28,16,260]{3,2,1,0:T(8,128)S(1)} fusion(f32[4,30,16,262]{3,2,1,0:T(8,128)S(1)} %get-tuple-element.47, f32[4,30,16,262]{3,2,1,0:T(8,128)} %get-tuple-element.48, f32[28,260]{1,0:T(8,128)S(1)} %slice_bitcast_fusion.4, f32[28,16,260]{2,1,0:T(8,128)S(1)} %get-tuple-element.43, f32[28,16,260]{2,1,0:T(8,128)} %get-tuple-element.45, ...), kind=kLoop, calls=%fused_computation.46 | loop fusion | flops 12113920 | bytes 22797824 | tf_op jit(solution)/shard_map/mul | solution.py:189
  54.9 8.5 %fusion.41 = f32[4,26,16,258]{3,2,1,0:T(8,128)S(1)} fusion(f32[4,28,16,260]{3,2,1,0:T(8,128)S(1)} %fusion.20, f32[4,30,16,262]{3,2,1,0:T(8,128)} %get-tuple-element.48, f32[26,258]{1,0:T(8,128)S(1)} %slice_bitcast_fusion.3, f32[26,16,258]{2,1,0:T(8,128)} %get-tuple-element.33, f32[26,16,258]{2,1,0:T(8,128)} %get-tuple-element.46, ...), kind=kLoop, calls=%fused_computation.70 | loop fusion | flops 11162112 | bytes 20734464 | tf_op jit(solution)/shard_map/mul | solution.py:189
  63.4 5.0 %fusion.68 = (f32[16,256]{1,0:T(8,128)S(1)}, f32[24,16,256]{2,1,0:T(8,128)S(1)}, f32[4,24,16,256]{3,2,1,0:T(8,128)}) fusion(f32[4,30,16,262]{3,2,1,0:T(8,128)S(1)} %copy-done.1, f32[24,16,256]{2,1,0:T(8,128)S(1)} %copy-done.4, f32[24,16,256]{2,1,0:T(8,128)S(1)} %copy-done.3, f32[4,26,16,258]{3,2,1,0:T(8,128)S(1)} %fusion.41, ...), kind=kLoop, calls=%fused_computation.116 | loop fusion | flops 10907648 | bytes 15549952 | tf_op jit(solution)/shard_map/reduce_sum | solution.py:192
  68.4 0.7 broadcast_in_dim.23
  69.1 8.1 %all-to-all-start = ((f32[8,16,256]{2,1,0:T(8,128)}), f32[8,16,256]{2,1,0:T(8,128)S(1)}, u32[]{:S(2)}, u32[]{:S(2)}) async-start(f32[8,16,256]{2,1,0:T(8,128)} %broadcast_in_dim.23), calls=%async_computation | async-start | bytes 262144 | tf_op jit(solution)/shard_map/all_to_all | solution.py:193
  77.2 6.6 %all-to-all-done = f32[8,16,256]{2,1,0:T(8,128)S(1)} async-done(((f32[8,16,256]{2,1,0:T(8,128)}), f32[8,16,256]{2,1,0:T(8,128)S(1)}, u32[]{:S(2)}, u32[]{:S(2)}) %all-to-all-start) | async-done | bytes 131104 | tf_op jit(solution)/shard_map/all_to_all | solution.py:193
  83.7 0.1 multiply_reduce_fusion
  83.8 0.8 fusion.62
  (27 shorter events, 0.1 us)
Async XLA Ops:
  0.6 1.6 %copy-start = (f32[4,3,16,256]{3,2,1,0:T(8,128)S(1)}, f32[4,3,16,256]{3,2,1,0:T(8,128)}, u32[]{:S(2)}) copy-start(f32[4,3,16,256]{3,2,1,0:T(8,128)} %param.11) | copy-start | bytes 589828
  0.6 26.9 %copy-start.2 = (f32[24,16,256]{2,1,0:T(8,128)S(1)}, f32[24,16,256]{2,1,0:T(8,128)}, u32[]{:S(2)}) copy-start(f32[24,16,256]{2,1,0:T(8,128)} %param.15) | copy-start | bytes 1179652
  0.7 26.9 %copy-start.3 = (f32[24,16,256]{2,1,0:T(8,128)S(1)}, f32[24,16,256]{2,1,0:T(8,128)}, u32[]{:S(2)}) copy-start(f32[24,16,256]{2,1,0:T(8,128)} %param.14) | copy-start | bytes 1179652
  0.7 11.5 %copy-start.6 = (s32[24]{0:T(128)S(1)}, s32[24]{0:T(128)}, u32[]{:S(2)}) copy-start(s32[24]{0:T(128)} %param.13) | copy-start | bytes 292
  4.3 17.2 %collective-permute-start.1 = (f32[60,16,3]{2,1,0:T(8,128)S(1)}, f32[60,16,3]{2,1,0:T(8,128)S(1)}, u32[]{:S(2)}, u32[]{:S(2)}) collective-permute-start(f32[60,16,3]{2,1,0:T(8,128)S(1)} %get-tuple-element.40), channel_id=1, source_target_pairs={{1,0},{2,1},{3,2},{4,3},{5,4},{6,5},{7,6},{8,7},{9,8},{10,9},{11,1... | collective-permute-start | bytes 34568 | tf_op jit(solution)/shard_map/ppermute | solution.py:25
  9.9 17.6 %collective-permute-start = (f32[60,16,3]{2,1,0:T(8,128)S(1)}, f32[60,16,3]{2,1,0:T(8,128)S(1)}, u32[]{:S(2)}, u32[]{:S(2)}) collective-permute-start(f32[60,16,3]{2,1,0:T(8,128)S(1)} %get-tuple-element.39), channel_id=1, source_target_pairs={{0,1},{1,2},{2,3},{3,4},{4,5},{5,6},{6,7},{7,8},{8,9},{9,10},{10,1... | collective-permute-start | bytes 34568 | tf_op jit(solution)/shard_map/ppermute | solution.py:25
  27.9 9.3 %copy-start.7 = (f32[4]{0:T(128)S(1)}, f32[4]{0:T(128)}, u32[]{:S(2)}) copy-start(f32[4]{0:T(128)} %constant.138.clone) | copy-start | bytes 52
  27.9 9.3 %copy-start.8 = (f32[4]{0:T(128)S(1)}, f32[4]{0:T(128)}, u32[]{:S(2)}) copy-start(f32[4]{0:T(128)} %constant.139.clone) | copy-start | bytes 52
  27.9 7.3 %collective-permute-start.3 = (f32[7,16,262]{2,1,0:T(8,128)S(1)}, f32[7,16,262]{2,1,0:T(8,128)S(1)}, u32[]{:S(2)}, u32[]{:S(2)}) collective-permute-start(f32[7,16,262]{2,1,0:T(8,128)S(1)} %select_maximum_fusion.10), channel_id=1, source_target_pairs={{64,0},{128,64},{192,128},{256,192},{320,256},{384,320},{448,384},... | collective-permute-start | bytes 352136 | tf_op jit(solution)/shard_map/ppermute | solution.py:25
  29.3 7.7 %collective-permute-start.2 = (f32[8,16,262]{2,1,0:T(8,128)S(1)}, f32[8,16,262]{2,1,0:T(8,128)S(1)}, u32[]{:S(2)}, u32[]{:S(2)}) collective-permute-start(f32[8,16,262]{2,1,0:T(8,128)S(1)} %select_maximum_fusion.3), channel_id=1, source_target_pairs={{0,64},{64,128},{128,192},{192,256},{256,320},{320,384},{384,448},... | collective-permute-start | bytes 402440 | tf_op jit(solution)/shard_map/ppermute | solution.py:25
  54.9 8.5 %copy-start.1 = (f32[4,30,16,262]{3,2,1,0:T(8,128)S(1)}, f32[4,30,16,262]{3,2,1,0:T(8,128)}, u32[]{:S(2)}) copy-start(f32[4,30,16,262]{3,2,1,0:T(8,128)} %get-tuple-element.48) | copy-start | bytes 6036484
  54.9 8.5 %copy-start.4 = (f32[24,16,256]{2,1,0:T(8,128)S(1)}, f32[24,16,256]{2,1,0:T(8,128)}, u32[]{:S(2)}) copy-start(f32[24,16,256]{2,1,0:T(8,128)} %get-tuple-element.31) | copy-start | bytes 1179652
  54.9 8.5 %copy-start.5 = (f32[24,16,256]{2,1,0:T(8,128)S(1)}, f32[24,16,256]{2,1,0:T(8,128)}, u32[]{:S(2)}) copy-start(f32[24,16,256]{2,1,0:T(8,128)} %get-tuple-element.32) | copy-start | bytes 1179652
  69.1 14.6 %all-to-all-start = ((f32[8,16,256]{2,1,0:T(8,128)}), f32[8,16,256]{2,1,0:T(8,128)S(1)}, u32[]{:S(2)}, u32[]{:S(2)}) async-start(f32[8,16,256]{2,1,0:T(8,128)} %broadcast_in_dim.23), calls=%async_computation | async-start | bytes 262144 | tf_op jit(solution)/shard_map/all_to_all | solution.py:193

commit v6 on v5

--- a/solution.py
+++ b/solution.py
@@ -172,21 +172,36 @@
     ).astype(jnp.float32)
 
     diagonal_sum = 2.0 * cond_rows + 2.0 * cond_cols + up_e + down_e + stiff_e
-    adjoint = relaxation * source_e / diagonal_sum * inside
+    scale = relaxation / diagonal_sum
+    forced = relaxation * source_e / diagonal_sum
+    scale_up = scale * up_e
+    scale_down = scale * down_e
+    half_cross = 0.5 * cond_cross
+    adjoint = forced * inside
     for iteration in range(1, ITERS):
-        by = iteration
-        adjoint = sweep(
-            adjoint,
-            trim(source_e, by, 1, 3),
-            trim(stiff_e, by, 0, 2),
-            trim(up_e, by, 0, 2),
-            trim(down_e, by, 0, 2),
-            cond_rows[by : cond_rows.shape[0] - by],
-            cond_cols[by : cond_cols.shape[0] - by],
-            cond_cross[by : cond_cross.shape[0] - by],
+        framed = jnp.pad(adjoint, ((0, 0), (1, 1), (1, 1), (1, 1)))
+        centre = framed[:, 1:-1, 1:-1, 1:-1]
+        along_rows = framed[:, 1:-1, 2:, 1:-1] + framed[:, 1:-1, :-2, 1:-1]
+        along_cols = framed[:, 1:-1, 1:-1, 2:] + framed[:, 1:-1, 1:-1, :-2]
+        diagonal_pairs = (
+            framed[:, 1:-1, 2:, 2:]
+            + framed[:, 1:-1, :-2, :-2]
+            - framed[:, 1:-1, 2:, :-2]
+            - framed[:, 1:-1, :-2, 2:]
+        )
+        overhead = framed[:, 2:, 1:-1, 1:-1]
+        beneath = framed[:, :-2, 1:-1, 1:-1]
+        in_plane = cond_rows * along_rows + cond_cols * along_cols + half_cross * diagonal_pairs
+        adjoint = (
+            (1.0 - relaxation) * centre
+            + forced
+            + scale * in_plane
+            + scale_up * overhead
+            + scale_down * beneath
         )
         if iteration < ITERS - 1:
-            adjoint = adjoint * trim(inside, by, 0, 2)
+            adjoint = adjoint * inside
+    adjoint = trim(adjoint, halo, 1, 3)
     source = trim(source_e, halo, 1, 3)
     product = adjoint * source
     total = jnp.sum(product, axis=(0, 1))

time: 85.1 us -> 105 us (1.23)
  other arithmetic: 35.7 us -> 53 us
  local copies, waits for them, and re-layouts: 1.84 us -> 5.27 us
  waiting for transfers between devices: 24.7 us -> 22.6 us
  starting transfers between devices: 21.4 us -> 22.5 us
    div x0 -> x2, other arithmetic: none -> 11.6 us  [the longest x1 11.2 us: body(): forced = relaxation * source_e / diagonal_sum]
    mul x7 -> x5, other arithmetic: 20.8 us -> 28.4 us  [the longest x1 17.3 us: body(): adjoint = adjoint * inside]
    slice x0 -> x4, local copies, waits for them, and re-layouts: none -> 3.56 us  [trim(): return lax.slice_in_dim(array, by, array.shape[col_dim] - by, axis=col_dim)]
    add x4 -> x0, other arithmetic: 3.47 us -> none  [the longest x2 3.13 us: sweep(): 2.0 * cond_rows + 2.0 * cond_cols + coupling_up + coupling_down + stiffening]
    reduce_sum x1, other arithmetic: 5.04 us -> 8.41 us  [body(): total = jnp.sum(product, axis=(0, 1))]
    ppermute x4, waiting for transfers between devices: 18.1 us -> 16 us  [passed_along(): return lax.ppermute(array, axis, pairs)]
    slice x2 -> x0, other arithmetic: 2 us -> none  [the longest x1 1.73 us: trim(): return lax.slice_in_dim(array, by, array.shape[col_dim] - by, axis=col_dim)]
    ppermute x4, starting transfers between devices: 13.4 us -> 14.4 us  [passed_along(): return lax.ppermute(array, axis, pairs)]
  transfers between devices with their start and end apart: 5 -> 5, of which waited for: 5 -> 5; matrix products, arithmetic and copies ran while one was open for 1% -> 0% of each run, Pallas kernels for 0% -> 0%
where the time goes in v6:
time: 105 us; the launch traced here: 104 us
  other arithmetic  53 us (50%)
  waiting for transfers between devices  22.6 us (22%)
  starting transfers between devices  22.5 us (21%)
  local copies, waits for them, and re-layouts  5.27 us (5%)
    mul x1, other arithmetic, body(): adjoint = adjoint * inside  17.3 us
    ppermute x4, waiting for transfers between devices, passed_along(): return lax.ppermute(array, axis, pairs)  16 us
    ppermute x4, starting transfers between devices, passed_along(): return lax.ppermute(array, axis, pairs)  14.4 us
    div x1, other arithmetic, body(): forced = relaxation * source_e / diagonal_sum  11.2 us
    mul x1, other arithmetic, body(): cond_rows * along_rows + cond_cols * along_cols  8.52 us
    reduce_sum x1, other arithmetic, body(): total = jnp.sum(product, axis=(0, 1))  8.41 us
    all_to_all x1, starting transfers between devices, body(): lax.all_to_all(jnp.broadcast_to(total[None], (ply_count,) + total.shape),...  8.06 us
    all_to_all x1, waiting for transfers between devices, body(): lax.all_to_all(jnp.broadcast_to(total[None], (ply_count,) + total.shape),...  6.57 us
  transfers between devices with their start and end apart: 5, of which 5 were waited for; matrix products, arithmetic and copies ran while one was open for 0% of the time, Pallas kernels for 0%

profile of v6, /device:TPU:448, one launch (start us, length us, event | category | flops | bytes accessed | tf_op | source)
XLA Modules:
  0.0 104.2 jit_solution(5472270338024488563)
XLA Ops:
  0.6 0.0 copy-start
  0.6 0.0 copy-start.1
  0.7 0.0 copy-start.2
  0.7 0.7 compare_and_fusion.1
  1.4 0.7 compare_select_fusion
  2.1 0.1 broadcast_in_dim.18
  2.2 0.1 broadcast_in_dim.19
  2.3 0.0 copy-done
  2.3 0.6 gather_fusion
  2.8 0.1 bitcast_select_fusion
  2.9 1.2 %pad_maximum_fusion = f32[60,16,256]{2,1,0:T(8,128)S(1)} fusion(f32[24,16,256]{2,1,0:T(8,128)} %param.15, f32[24,16,256]{2,1,0:T(8,128)} %param.14, f32[12,16,256]{2,1,0:T(8,128)S(1)} %bitcast_select_fusion), kind=kLoop, calls=%fused_computation.95 | loop fusion | flops 491520 | bytes 1966080 | tf_op jit(solution)/shard_map/concatenate | solution.py:112
  4.1 0.2 fusion.78
  4.3 1.9 %collective-permute-start = (f32[60,16,3]{2,1,0:T(8,128)S(1)}, f32[60,16,3]{2,1,0:T(8,128)S(1)}, u32[]{:S(2)}, u32[]{:S(2)}) collective-permute-start(f32[60,16,3]{2,1,0:T(8,128)S(1)} %get-tuple-element.47), channel_id=1, source_target_pairs={{0,1},{1,2},{2,3},{3,4},{4,5},{5,6},{6,7},{7,8},{8,9},{9,10},{10,1... | collective-permute-start | bytes 34568 | tf_op jit(solution)/shard_map/ppermute | solution.py:25
  6.2 6.7 %collective-permute-start.1 = (f32[60,16,3]{2,1,0:T(8,128)S(1)}, f32[60,16,3]{2,1,0:T(8,128)S(1)}, u32[]{:S(2)}, u32[]{:S(2)}) collective-permute-start(f32[60,16,3]{2,1,0:T(8,128)S(1)} %get-tuple-element.48), channel_id=1, source_target_pairs={{1,0},{2,1},{3,2},{4,3},{5,4},{6,5},{7,6},{8,7},{9,8},{10,9},{11,1... | collective-permute-start | bytes 34568 | tf_op jit(solution)/shard_map/ppermute | solution.py:25
  12.9 0.1 and_convert_fusion
  13.0 0.1 convert_bitcast_fusion.1
  13.1 7.1 %collective-permute-done = f32[60,16,3]{2,1,0:T(8,128)S(1)} collective-permute-done((f32[60,16,3]{2,1,0:T(8,128)S(1)}, f32[60,16,3]{2,1,0:T(8,128)S(1)}, u32[]{:S(2)}, u32[]{:S(2)}) %collective-permute-start) | collective-permute-done | bytes 11552 | tf_op jit(solution)/shard_map/ppermute | solution.py:25
  20.2 4.3 %collective-permute-done.1 = f32[60,16,3]{2,1,0:T(8,128)S(1)} collective-permute-done((f32[60,16,3]{2,1,0:T(8,128)S(1)}, f32[60,16,3]{2,1,0:T(8,128)S(1)}, u32[]{:S(2)}, u32[]{:S(2)}) %collective-permute-start.1) | collective-permute-done | bytes 11552 | tf_op jit(solution)/shard_map/ppermute | solution.py:25
  24.5 0.1 select_maximum_fusion.13
  24.6 0.0 copy-start.12
  24.6 0.0 copy-start.13
  24.6 1.3 %collective-permute-start.3 = (f32[7,16,262]{2,1,0:T(8,128)S(1)}, f32[7,16,262]{2,1,0:T(8,128)S(1)}, u32[]{:S(2)}, u32[]{:S(2)}) collective-permute-start(f32[7,16,262]{2,1,0:T(8,128)S(1)} %select_maximum_fusion.13), channel_id=1, source_target_pairs={{64,0},{128,64},{192,128},{256,192},{320,256},{384,320},{448,384},... | collective-permute-start | bytes 352136 | tf_op jit(solution)/shard_map/ppermute | solution.py:25
  25.9 0.1 select_maximum_fusion.6
  26.1 4.6 %collective-permute-start.2 = (f32[8,16,262]{2,1,0:T(8,128)S(1)}, f32[8,16,262]{2,1,0:T(8,128)S(1)}, u32[]{:S(2)}, u32[]{:S(2)}) collective-permute-start(f32[8,16,262]{2,1,0:T(8,128)S(1)} %select_maximum_fusion.6), channel_id=1, source_target_pairs={{0,64},{64,128},{128,192},{192,256},{256,320},{320,384},{384,448},... | collective-permute-start | bytes 402440 | tf_op jit(solution)/shard_map/ppermute | solution.py:25
  30.6 0.2 pad_maximum_fusion.3
  30.8 2.8 %collective-permute-done.3 = f32[7,16,262]{2,1,0:T(8,128)S(1)} collective-permute-done((f32[7,16,262]{2,1,0:T(8,128)S(1)}, f32[7,16,262]{2,1,0:T(8,128)S(1)}, u32[]{:S(2)}, u32[]{:S(2)}) %collective-permute-start.3) | collective-permute-done | bytes 117408 | tf_op jit(solution)/shard_map/ppermute | solution.py:25
  33.6 1.8 %collective-permute-done.2 = f32[8,16,262]{2,1,0:T(8,128)S(1)} collective-permute-done((f32[8,16,262]{2,1,0:T(8,128)S(1)}, f32[8,16,262]{2,1,0:T(8,128)S(1)}, u32[]{:S(2)}, u32[]{:S(2)}) %collective-permute-start.2) | collective-permute-done | bytes 134176 | tf_op jit(solution)/shard_map/ppermute | solution.py:25
  35.5 0.1 pad_add_fusion
  35.5 0.1 select_reduce_fusion
  35.7 0.6 slice.292
  36.3 0.3 fusion.48
  36.6 0.3 broadcast_divide_fusion
  37.0 1.0 slice.296
  38.0 0.1 slice_multiply_fusion.6
  38.1 0.0 copy-start.3
  38.1 1.0 slice.297
  39.1 0.9 slice.299
  40.0 2.5 %broadcast_multiply_fusion = f32[4,30,16,262]{3,2,1,0:T(8,128)S(1)} fusion(f32[30,262]{1,0:T(8,128)S(1)} %and_convert_fusion, f32[30,16,262]{2,1,0:T(8,128)S(1)} %get-tuple-element.32, f32[30]{0:T(128)S(1)} %get-tuple-element.57, f32[4,16,262]{2,1,0:T(8,128)S(1)} %fusion.66, f32[30]{0:T(128)S(1)} %get-tuple-element.61, ...), kind=kLoop, calls=%fused_computation.88 | loop fusion | flops 12072960 | bytes 2815528 | tf_op jit(solution)/shard_map/mul | solution.py:180
  42.5 11.2 %multiply_divide_fusion = (f32[4,30,16,262]{3,2,1,0:T(8,128)}, f32[4,30,16,262]{3,2,1,0:T(8,128)}, f32[4,30,16,262]{3,2,1,0:T(8,128)}) fusion(f32[30,16,262]{2,1,0:T(8,128)S(1)} %get-tuple-element.32, f32[30]{0:T(128)S(1)} %get-tuple-element.57, f32[4,16,262]{2,1,0:T(8,128)S(1)} %fusion.66, f32[30]{0:T(128)S(1)} %get-tuple-element.61, ...), kind=kLoop, calls=%fused_computation.74 | loop fusion | flops 21127680 | bytes 10361488 | tf_op jit(solution)/shard_map/div | solution.py:176
  53.7 17.3 %fusion.25 = f32[4,30,16,262]{3,2,1,0:T(8,128)S(1)} fusion(f32[4,30,16,262]{3,2,1,0:T(8,128)} %get-tuple-element.46, f32[30,16,262]{2,1,0:T(8,128)} %copy-done.3, f32[30,16,262]{2,1,0:T(8,128)S(1)} %get-tuple-element.43, f32[30]{0:T(128)S(1)} %copy-done.9, f32[30]{0:T(128)S(1)} %get-tuple-element.59, f32[30]{0:T(128)S(1)} %get-tuple-element.60, ...), kind=kLoop, calls=%fused_computation.58 | loop fusion | flops 21127680 | bytes 6337168 | tf_op jit(solution)/shard_map/mul | solution.py:203
  71.1 0.0 copy-start.7
  71.1 8.5 %fusion.35 = (f32[4,30,16,262]{3,2,1,0:T(8,128)}, f32[4,30,16,262]{3,2,1,0:T(8,128)}, f32[4,30,16,262]{3,2,1,0:T(8,128)}, f32[4,30,16,262]{3,2,1,0:T(8,128)}, f32[4,30,16,262]{3,2,1,0:T(8,128)}) fusion(f32[4,30,16,262]{3,2,1,0:T(8,128)S(1)} %fusion.25, f32[30]{0:T(128)S(1)} %get-tuple-element.60, f32[30]{0:T(128)S(1)} %get-tuple-element.59), kind=kLoop, calls=%fused_computation.68 | loop fusion | flops 3521280 | bytes 12073200 | tf_op jit(solution)/shard_map/mul | solution.py:194
  79.6 8.4 %fusion.54 = (f32[16,256]{1,0:T(8,128)S(1)}, f32[24,16,256]{2,1,0:T(8,128)S(1)}, f32[4,24,16,256]{3,2,1,0:T(8,128)}) fusion(f32[4,30,16,262]{3,2,1,0:T(8,128)} %get-tuple-element.49, f32[4,30,16,262]{3,2,1,0:T(8,128)} %get-tuple-element.42, f32[24,16,256]{2,1,0:T(8,128)S(1)} %copy-done.7, f32[4,30,16,262]{3,2,1,0:T(8,128)} %get-tuple-element.41, ...), kind=kLoop, calls=%fused_computation.113 | loop fusion | flops 5402624 | bytes 15745120 | tf_op jit(solution)/shard_map/reduce_sum | solution.py:207
  88.0 0.7 broadcast_in_dim.23
  88.7 8.1 %all-to-all-start = ((f32[8,16,256]{2,1,0:T(8,128)}), f32[8,16,256]{2,1,0:T(8,128)S(1)}, u32[]{:S(2)}, u32[]{:S(2)}) async-start(f32[8,16,256]{2,1,0:T(8,128)} %broadcast_in_dim.23), calls=%async_computation | async-start | bytes 262144 | tf_op jit(solution)/shard_map/all_to_all | solution.py:208
  96.8 6.6 %all-to-all-done = f32[8,16,256]{2,1,0:T(8,128)S(1)} async-done(((f32[8,16,256]{2,1,0:T(8,128)}), f32[8,16,256]{2,1,0:T(8,128)S(1)}, u32[]{:S(2)}, u32[]{:S(2)}) %all-to-all-start) | async-done | bytes 131104 | tf_op jit(solution)/shard_map/all_to_all | solution.py:208
  103.3 0.1 multiply_reduce_fusion
  103.4 0.8 fusion.46
  (32 shorter events, 0.1 us)
Async XLA Ops:
  0.6 1.6 %copy-start = (f32[4,3,16,256]{3,2,1,0:T(8,128)S(1)}, f32[4,3,16,256]{3,2,1,0:T(8,128)}, u32[]{:S(2)}) copy-start(f32[4,3,16,256]{3,2,1,0:T(8,128)} %param.11) | copy-start | bytes 589828
  0.6 23.8 %copy-start.1 = (f32[24,16,256]{2,1,0:T(8,128)S(1)}, f32[24,16,256]{2,1,0:T(8,128)}, u32[]{:S(2)}) copy-start(f32[24,16,256]{2,1,0:T(8,128)} %param.15) | copy-start | bytes 1179652
  0.7 23.8 %copy-start.2 = (f32[24,16,256]{2,1,0:T(8,128)S(1)}, f32[24,16,256]{2,1,0:T(8,128)}, u32[]{:S(2)}) copy-start(f32[24,16,256]{2,1,0:T(8,128)} %param.14) | copy-start | bytes 1179652
  0.7 12.3 %copy-start.10 = (s32[24]{0:T(128)S(1)}, s32[24]{0:T(128)}, u32[]{:S(2)}) copy-start(s32[24]{0:T(128)} %param.13) | copy-start | bytes 292
  4.3 15.9 %collective-permute-start = (f32[60,16,3]{2,1,0:T(8,128)S(1)}, f32[60,16,3]{2,1,0:T(8,128)S(1)}, u32[]{:S(2)}, u32[]{:S(2)}) collective-permute-start(f32[60,16,3]{2,1,0:T(8,128)S(1)} %get-tuple-element.47), channel_id=1, source_target_pairs={{0,1},{1,2},{2,3},{3,4},{4,5},{5,6},{6,7},{7,8},{8,9},{9,10},{10,1... | collective-permute-start | bytes 34568 | tf_op jit(solution)/shard_map/ppermute | solution.py:25
  6.2 18.3 %collective-permute-start.1 = (f32[60,16,3]{2,1,0:T(8,128)S(1)}, f32[60,16,3]{2,1,0:T(8,128)S(1)}, u32[]{:S(2)}, u32[]{:S(2)}) collective-permute-start(f32[60,16,3]{2,1,0:T(8,128)S(1)} %get-tuple-element.48), channel_id=1, source_target_pairs={{1,0},{2,1},{3,2},{4,3},{5,4},{6,5},{7,6},{8,7},{9,8},{10,9},{11,1... | collective-permute-start | bytes 34568 | tf_op jit(solution)/shard_map/ppermute | solution.py:25
  24.6 10.9 %copy-start.12 = (f32[4]{0:T(128)S(1)}, f32[4]{0:T(128)}, u32[]{:S(2)}) copy-start(f32[4]{0:T(128)} %constant.131.clone) | copy-start | bytes 52
  24.6 10.9 %copy-start.13 = (f32[4]{0:T(128)S(1)}, f32[4]{0:T(128)}, u32[]{:S(2)}) copy-start(f32[4]{0:T(128)} %constant.130.clone) | copy-start | bytes 52
  24.6 9.0 %collective-permute-start.3 = (f32[7,16,262]{2,1,0:T(8,128)S(1)}, f32[7,16,262]{2,1,0:T(8,128)S(1)}, u32[]{:S(2)}, u32[]{:S(2)}) collective-permute-start(f32[7,16,262]{2,1,0:T(8,128)S(1)} %select_maximum_fusion.13), channel_id=1, source_target_pairs={{64,0},{128,64},{192,128},{256,192},{320,256},{384,320},{448,384},... | collective-permute-start | bytes 352136 | tf_op jit(solution)/shard_map/ppermute | solution.py:25
  26.1 9.4 %collective-permute-start.2 = (f32[8,16,262]{2,1,0:T(8,128)S(1)}, f32[8,16,262]{2,1,0:T(8,128)S(1)}, u32[]{:S(2)}, u32[]{:S(2)}) collective-permute-start(f32[8,16,262]{2,1,0:T(8,128)S(1)} %select_maximum_fusion.6), channel_id=1, source_target_pairs={{0,64},{64,128},{128,192},{192,256},{256,320},{320,384},{384,448},... | collective-permute-start | bytes 402440 | tf_op jit(solution)/shard_map/ppermute | solution.py:25
  35.6 0.7 copy-start.8
  37.0 3.1 %copy-start.4 = (f32[30,16,262]{2,1,0:T(8,128)}, f32[30,16,262]{2,1,0:T(8,128)S(1)}, u32[]{:S(2)}) copy-start(f32[30,16,262]{2,1,0:T(8,128)S(1)} %get-tuple-element.31) | copy-start | bytes 1509124
  38.1 1.9 %copy-start.3 = (f32[30,16,262]{2,1,0:T(8,128)}, f32[30,16,262]{2,1,0:T(8,128)S(1)}, u32[]{:S(2)}) copy-start(f32[30,16,262]{2,1,0:T(8,128)S(1)} %get-tuple-element.44) | copy-start | bytes 1509124
  38.1 4.4 %copy-start.9 = (f32[30]{0:T(128)S(1)}, f32[30]{0:T(128)}, u32[]{:S(2)}) copy-start(f32[30]{0:T(128)} %copy-done.8) | copy-start | bytes 364
  71.0 8.6 %copy-start.5 = (f32[24,16,256]{2,1,0:T(8,128)S(1)}, f32[24,16,256]{2,1,0:T(8,128)}, u32[]{:S(2)}) copy-start(f32[24,16,256]{2,1,0:T(8,128)} %slice.296) | copy-start | bytes 1179652
  71.0 8.6 %copy-start.6 = (f32[24,16,256]{2,1,0:T(8,128)S(1)}, f32[24,16,256]{2,1,0:T(8,128)}, u32[]{:S(2)}) copy-start(f32[24,16,256]{2,1,0:T(8,128)} %slice.297) | copy-start | bytes 1179652
  71.1 8.5 %copy-start.7 = (f32[24,16,256]{2,1,0:T(8,128)S(1)}, f32[24,16,256]{2,1,0:T(8,128)}, u32[]{:S(2)}) copy-start(f32[24,16,256]{2,1,0:T(8,128)} %slice.299) | copy-start | bytes 1179652
  71.1 8.5 %copy-start.11 = (f32[24]{0:T(128)S(1)}, f32[24]{0:T(128)}, u32[]{:S(2)}) copy-start(f32[24]{0:T(128)} %slice.292) | copy-start | bytes 292
  88.7 14.6 %all-to-all-start = ((f32[8,16,256]{2,1,0:T(8,128)}), f32[8,16,256]{2,1,0:T(8,128)S(1)}, u32[]{:S(2)}, u32[]{:S(2)}) async-start(f32[8,16,256]{2,1,0:T(8,128)} %broadcast_in_dim.23), calls=%async_computation | async-start | bytes 262144 | tf_op jit(solution)/shard_map/all_to_all | solution.py:208

commit v7 on v5

--- a/solution.py
+++ b/solution.py
@@ -2,6 +2,8 @@
 import jax.numpy as jnp
 from jax import lax
 from jax.sharding import PartitionSpec as P
+from jax.experimental import pallas as pl
+from jax.experimental.pallas import tpu as pltpu
 
 ITERS = 4
 
@@ -92,6 +94,85 @@
     return centre + relaxation * (source - image) / diagonal_sum
 
 
+def sweeps_kernel(tab, ply_mask, strain_ref, stiff_ref, inter_ref, col_mask_ref, adj_ref, acc_ref, src_s, a_s, b_s):
+    case = pl.program_id(0)
+    planes, rows, lanes = stiff_ref.shape
+    halo = ITERS - 1
+    own_planes, own_cols = acc_ref.shape[0], acc_ref.shape[2]
+    col_mask = col_mask_ref[...]
+    row = lax.broadcasted_iota(jnp.int32, (rows, lanes), 0)
+    keep_a = (jnp.abs(pltpu.roll(row, 1, 0) - row) == 1).astype(jnp.float32)
+    keep_b = (jnp.abs(pltpu.roll(row, rows - 1, 0) - row) == 1).astype(jnp.float32)
+    strain_x = strain_ref[0, 0]
+    strain_y = strain_ref[0, 1]
+    strain_xy = strain_ref[0, 2]
+
+    def diagonal_at(p):
+        cond_rows, cond_cols = tab[0, p], tab[1, p]
+        return 2.0 * cond_rows + 2.0 * cond_cols + inter_ref[p + 1] + inter_ref[p] + stiff_ref[p]
+
+    def first(p, carry):
+        source = tsai_wu(strain_x, strain_y, strain_xy, tab[3, p], tab[4, p])
+        src_s[p] = source
+        a_s[p] = relaxation * source / diagonal_at(p) * (ply_mask[p] * col_mask)
+        return carry
+
+    lax.fori_loop(0, planes, first, 0)
+    buffers = (a_s, b_s)
+    for iteration in range(1, ITERS):
+        previous, following = buffers[(iteration - 1) % 2], buffers[iteration % 2]
+        masked = iteration < ITERS - 1
+
+        def step(p, carry, previous=previous, following=following, masked=masked):
+            centre = previous[p]
+            row_a = pltpu.roll(centre, 1, 0) * keep_a
+            row_b = pltpu.roll(centre, rows - 1, 0) * keep_b
+            along_rows = row_a + row_b
+            along_cols = pltpu.roll(centre, 1, 1) + pltpu.roll(centre, lanes - 1, 1)
+            diagonal_pairs = (
+                pltpu.roll(row_a, 1, 1)
+                + pltpu.roll(row_b, lanes - 1, 1)
+                - pltpu.roll(row_a, lanes - 1, 1)
+                - pltpu.roll(row_b, 1, 1)
+            )
+            cond_rows, cond_cols, cond_cross = tab[0, p], tab[1, p], tab[2, p]
+            coupling_up = inter_ref[p + 1]
+            coupling_down = inter_ref[p]
+            stiffening = stiff_ref[p]
+            image = (
+                cond_rows * (2.0 * centre - along_rows)
+                + cond_cols * (2.0 * centre - along_cols)
+                - 0.5 * cond_cross * diagonal_pairs
+            )
+            image = (
+                image
+                + coupling_up * (centre - previous[p + 1])
+                + coupling_down * (centre - previous[p - 1])
+                + stiffening * centre
+            )
+            diagonal_sum = 2.0 * cond_rows + 2.0 * cond_cols + coupling_up + coupling_down + stiffening
+            value = centre + relaxation * (src_s[p] - image) / diagonal_sum
+            if masked:
+                value = value * (ply_mask[p] * col_mask)
+            following[p] = value
+            return carry
+
+        lax.fori_loop(iteration, planes - iteration, step, 0)
+    final = buffers[(ITERS - 1) % 2]
+
+    @pl.when(case == 0)
+    def _():
+        acc_ref[...] = jnp.zeros(acc_ref.shape, jnp.float32)
+
+    def store(p, carry):
+        value = final[p + halo][:, :own_cols]
+        adj_ref[0, p] = value
+        acc_ref[p] = acc_ref[p] + value * src_s[p + halo][:, :own_cols]
+        return carry
+
+    lax.fori_loop(0, own_planes, store, 0)
+
+
 def trim(array, by, ply_dim, col_dim):
     if by == 0:
         return array
@@ -109,15 +190,18 @@
     chosen = jnp.take(strain, case_ids, axis=0)
     rows = chosen.shape[2]
 
-    packed = jnp.concatenate(
+    lanes = -(-(col_local + 2 * halo) // 128) * 128
+    flat = jnp.concatenate(
         [chosen.reshape(cases * 3, rows, col_local), stiffening, interface], axis=0
     )
-    packed = with_halos(packed, "tile", 2, halo, halo)
-    width = col_local + 2 * halo
-    strain_e = packed[: cases * 3].reshape(cases, 3, rows, width)
+    left = passed_along(flat[..., col_local - halo :], "tile", 1)
+    right = passed_along(flat[..., :halo], "tile", -1)
+    gap = jnp.zeros(flat.shape[:2] + (lanes - col_local - 2 * halo,), jnp.float32)
+    packed = jnp.concatenate([flat, right, gap, left], axis=2)
+    strain_e = packed[: cases * 3].reshape(cases, 3, rows, lanes)
     stiff_c = packed[cases * 3 : cases * 3 + ply_local]
     inter_c = packed[cases * 3 + ply_local :]
-    angle_plane = jnp.zeros((1, rows, width), jnp.float32)
+    angle_plane = jnp.zeros((1, rows, lanes), jnp.float32)
     below = passed_along(
         jnp.concatenate(
             [
@@ -149,53 +233,51 @@
             above[2 * halo, 0, :halo].astype(jnp.int32),
         ]
     )
-    below = below[: 2 * halo + 1]
-    above = above[: 2 * halo]
     stiff_e = jnp.concatenate([below[:halo], stiff_c, above[:halo]], axis=0)
-    inter_all = jnp.concatenate([below[halo:], inter_c, above[halo:]], axis=0)
-    up_e = inter_all[1:]
-    down_e = inter_all[:-1]
+    inter_all = jnp.concatenate([below[halo : 2 * halo + 1], inter_c, above[halo : 2 * halo]], axis=0)
 
     cond_rows, cond_cols, cond_cross, ply_cosine, ply_sine = ply_tables(angles)
-    source_e = tsai_wu(
-        strain_e[:, 0][:, None],
-        strain_e[:, 1][:, None],
-        strain_e[:, 2][:, None],
-        ply_cosine,
-        ply_sine,
-    )
-    ply_at = lax.axis_index("ply") * ply_local - halo + jnp.arange(ply_local + 2 * halo)
-    col_at = lax.axis_index("tile") * col_local - halo + jnp.arange(width)
-    inside = (
-        ((ply_at >= 0) & (ply_at < ply_local * ply_count))[:, None, None]
-        & ((col_at >= 0) & (col_at < col_local * tile_count))[None, None, :]
-    ).astype(jnp.float32)
-
-    diagonal_sum = 2.0 * cond_rows + 2.0 * cond_cols + up_e + down_e + stiff_e
-    adjoint = relaxation * source_e / diagonal_sum * inside
-    for iteration in range(1, ITERS):
-        by = iteration
-        adjoint = sweep(
-            adjoint,
-            trim(source_e, by, 1, 3),
-            trim(stiff_e, by, 0, 2),
-            trim(up_e, by, 0, 2),
-            trim(down_e, by, 0, 2),
-            cond_rows[by : cond_rows.shape[0] - by],
-            cond_cols[by : cond_cols.shape[0] - by],
-            cond_cross[by : cond_cross.shape[0] - by],
-        )
-        if iteration < ITERS - 1:
-            adjoint = adjoint * trim(inside, by, 0, 2)
-    source = trim(source_e, halo, 1, 3)
-    product = adjoint * source
-    total = jnp.sum(product, axis=(0, 1))
+    tab = jnp.stack(
+        [t.reshape(-1) for t in (cond_rows, cond_cols, cond_cross, ply_cosine, ply_sine)]
+    )
+    planes = ply_local + 2 * halo
+    ply_at = lax.axis_index("ply") * ply_local - halo + jnp.arange(planes)
+    ply_mask = ((ply_at >= 0) & (ply_at < ply_local * ply_count)).astype(jnp.float32)
+    lane = jnp.arange(lanes)
+    col_at = lax.axis_index("tile") * col_local + jnp.where(lane >= lanes - halo, lane - lanes, lane)
+    col_ok = (lane < col_local + halo) | (lane >= lanes - halo)
+    col_ok = col_ok & (col_at >= 0) & (col_at < col_local * tile_count)
+    col_mask = jnp.broadcast_to(col_ok.astype(jnp.float32)[None, :], (rows, lanes))
+
+    adjoint, summed = pl.pallas_call(
+        sweeps_kernel,
+        grid=(cases,),
+        in_specs=[
+            pl.BlockSpec(memory_space=pltpu.SMEM),
+            pl.BlockSpec(memory_space=pltpu.SMEM),
+            pl.BlockSpec((1, 3, rows, lanes), lambda c: (c, 0, 0, 0)),
+            pl.BlockSpec((planes, rows, lanes), lambda c: (0, 0, 0)),
+            pl.BlockSpec((planes + 1, rows, lanes), lambda c: (0, 0, 0)),
+            pl.BlockSpec((rows, lanes), lambda c: (0, 0)),
+        ],
+        out_specs=[
+            pl.BlockSpec((1, ply_local, rows, col_local), lambda c: (c, 0, 0, 0)),
+            pl.BlockSpec((ply_local, rows, col_local), lambda c: (0, 0, 0)),
+        ],
+        out_shape=[
+            jax.ShapeDtypeStruct((cases, ply_local, rows, col_local), jnp.float32),
+            jax.ShapeDtypeStruct((ply_local, rows, col_local), jnp.float32),
+        ],
+        scratch_shapes=[pltpu.VMEM((planes, rows, lanes), jnp.float32)] * 3,
+        compiler_params=pltpu.CompilerParams(dimension_semantics=("arbitrary",)),
+    )(tab, ply_mask, strain_e, stiff_e, inter_all, col_mask)
+    total = jnp.sum(summed, axis=0)
     totals = lax.all_to_all(
         jnp.broadcast_to(total[None], (ply_count,) + total.shape), "ply", 0, 0, tiled=True
     )
     lower = (jnp.arange(ply_count) < lax.axis_index("ply")).astype(jnp.float32)
     prefix = jnp.sum(totals * lower[:, None, None], axis=0)
-    running = jnp.cumsum(jnp.sum(product, axis=0), axis=0)
+    running = jnp.cumsum(summed, axis=0)
     through = (running + prefix[None]) / (ply_local * ply_count)
     return (adjoint, through)
 

time: 85.1 us -> 105 us (1.23)
  Pallas kernels: 0 us -> 45 us
  other arithmetic: 35.7 us -> 8.4 us
  local copies, waits for them, and re-layouts: 1.84 us -> 3.77 us
    pallas_call x0 -> x1, Pallas kernels: none -> 45 us  [body(): pl.pallas_call(sweeps_kernel, grid=(cases,), in_specs=[pl.BlockSpec(memor...]
    mul x7 -> x0, other arithmetic: 20.8 us -> none  [the longest x2 16.9 us: body(): adjoint = adjoint * trim(inside, by, 0, 2)]
    reduce_sum x1, other arithmetic: 5.04 us -> 1.03 us  [body(): total = jnp.sum(summed, axis=0)]
    add x4 -> x0, other arithmetic: 3.47 us -> none  [the longest x2 3.13 us: sweep(): 2.0 * cond_rows + 2.0 * cond_cols + coupling_up + coupling_down + stiffening]
    slice x3 -> x0, other arithmetic: 2.17 us -> none  [the longest x1 1.73 us: trim(): return lax.slice_in_dim(array, by, array.shape[col_dim] - by, axis=col_dim)]
    concatenate x1 -> x3, other arithmetic: 0.05 us -> 2.09 us  [the longest x1 0.93 us: body(): jnp.concatenate([below[halo:2 * halo + 1], inter_c, above[halo:2 * halo]]...]
where the time goes in v7:
time: 105 us; the launch traced here: 104 us
  Pallas kernels  45 us (43%)
  waiting for transfers between devices  24.7 us (24%)
  starting transfers between devices  21.6 us (21%)
  other arithmetic  8.4 us (8%)
  local copies, waits for them, and re-layouts  3.77 us (4%)
    pallas_call x1, Pallas kernels, body(): pl.pallas_call(sweeps_kernel, grid=(cases,), in_specs=[pl.BlockSpec(memor...  45 us
    ppermute x4, waiting for transfers between devices, passed_along(): return lax.ppermute(array, axis, pairs)  18.1 us
    ppermute x4, starting transfers between devices, passed_along(): return lax.ppermute(array, axis, pairs)  13.5 us
    all_to_all x1, starting transfers between devices, body(): lax.all_to_all(jnp.broadcast_to(total[None], (ply_count,) + total.shape),...  8.06 us
    all_to_all x1, waiting for transfers between devices, body(): lax.all_to_all(jnp.broadcast_to(total[None], (ply_count,) + total.shape),...  6.57 us
  transfers between devices with their start and end apart: 5, of which 5 were waited for; matrix products, arithmetic and copies ran while one was open for 1% of the time, Pallas kernels for 0%

profile of v7, /device:TPU:448, one launch (start us, length us, event | category | flops | bytes accessed | tf_op | source)
XLA Modules:
  0.0 104.3 jit_solution(11326065740380938541)
XLA Ops:
  0.6 0.0 copy-start
  0.6 0.7 compare_and_fusion
  1.3 0.7 compare_select_fusion
  2.0 0.1 broadcast_in_dim.38
  2.1 0.1 broadcast_in_dim.39
  2.2 0.0 copy-done
  2.2 0.6 gather_fusion
  2.7 0.1 bitcast_select_fusion
  2.8 1.2 %pad_maximum_fusion.1 = f32[60,16,256]{2,1,0:T(8,128)S(1)} fusion(f32[24,16,256]{2,1,0:T(8,128)} %param.15, f32[24,16,256]{2,1,0:T(8,128)} %param.14, f32[12,16,256]{2,1,0:T(8,128)S(1)} %bitcast_select_fusion), kind=kLoop, calls=%fused_computation.4 | loop fusion | flops 491520 | bytes 1966080 | tf_op jit(solution)/shard_map/concatenate | solution.py:194
  4.0 0.0 copy-start.3
  4.0 0.0 copy-start.1
  4.0 0.0 copy-start.2
  4.1 0.2 fusion.14
  4.3 5.7 %collective-permute-start = (f32[60,16,3]{2,1,0:T(8,128)S(1)}, f32[60,16,3]{2,1,0:T(8,128)S(1)}, u32[]{:S(2)}, u32[]{:S(2)}) collective-permute-start(f32[60,16,3]{2,1,0:T(8,128)S(1)} %get-tuple-element.37), channel_id=1, source_target_pairs={{1,0},{2,1},{3,2},{4,3},{5,4},{6,5},{7,6},{8,7},{9,8},{10,9},{11,1... | collective-permute-start | bytes 34568 | tf_op jit(solution)/shard_map/ppermute | solution.py:27
  10.0 1.9 %collective-permute-start.1 = (f32[60,16,3]{2,1,0:T(8,128)S(1)}, f32[60,16,3]{2,1,0:T(8,128)S(1)}, u32[]{:S(2)}, u32[]{:S(2)}) collective-permute-start(f32[60,16,3]{2,1,0:T(8,128)S(1)} %get-tuple-element.38), channel_id=1, source_target_pairs={{0,1},{1,2},{2,3},{3,4},{4,5},{5,6},{6,7},{7,8},{8,9},{9,10},{10,1... | collective-permute-start | bytes 34568 | tf_op jit(solution)/shard_map/ppermute | solution.py:27
  11.9 0.0 copy-done.3
  11.9 0.1 convert_bitcast_fusion.1
  12.0 0.5 and_convert_fusion.ply_mask
  12.5 0.1 pad.27.clone
  12.6 9.0 %collective-permute-done = f32[60,16,3]{2,1,0:T(8,128)S(1)} collective-permute-done((f32[60,16,3]{2,1,0:T(8,128)S(1)}, f32[60,16,3]{2,1,0:T(8,128)S(1)}, u32[]{:S(2)}, u32[]{:S(2)}) %collective-permute-start) | collective-permute-done | bytes 11552 | tf_op jit(solution)/shard_map/ppermute | solution.py:27
  21.6 6.0 %collective-permute-done.1 = f32[60,16,3]{2,1,0:T(8,128)S(1)} collective-permute-done((f32[60,16,3]{2,1,0:T(8,128)S(1)}, f32[60,16,3]{2,1,0:T(8,128)S(1)}, u32[]{:S(2)}, u32[]{:S(2)}) %collective-permute-start.1) | collective-permute-done | bytes 11552 | tf_op jit(solution)/shard_map/ppermute | solution.py:27
  27.6 0.0 copy-done.1
  27.6 0.0 copy-done.2
  27.6 0.2 pad_maximum_fusion
  27.9 0.7 slice.124
  28.7 1.3 %collective-permute-start.3 = (f32[7,16,384]{2,1,0:T(8,128)S(1)}, f32[7,16,384]{2,1,0:T(8,128)S(1)}, u32[]{:S(2)}, u32[]{:S(2)}) collective-permute-start(f32[7,16,384]{2,1,0:T(8,128)S(1)} %select_maximum_fusion.1), channel_id=1, source_target_pairs={{64,0},{128,64},{192,128},{256,192},{320,256},{384,320},{448,384},... | collective-permute-start | bytes 516104 | tf_op jit(solution)/shard_map/ppermute | solution.py:27
  30.0 0.0 copy-start.4
  30.0 0.0 copy-start.5
  30.0 4.6 %collective-permute-start.2 = (f32[8,16,384]{2,1,0:T(8,128)S(1)}, f32[8,16,384]{2,1,0:T(8,128)S(1)}, u32[]{:S(2)}, u32[]{:S(2)}) collective-permute-start(f32[8,16,384]{2,1,0:T(8,128)S(1)} %select_maximum_fusion), channel_id=1, source_target_pairs={{0,64},{64,128},{128,192},{192,256},{256,320},{320,384},{384,448},... | collective-permute-start | bytes 589832 | tf_op jit(solution)/shard_map/ppermute | solution.py:27
  34.6 0.1 fusion.12
  34.7 1.3 %collective-permute-done.3 = f32[7,16,384]{2,1,0:T(8,128)S(1)} collective-permute-done((f32[7,16,384]{2,1,0:T(8,128)S(1)}, f32[7,16,384]{2,1,0:T(8,128)S(1)}, u32[]{:S(2)}, u32[]{:S(2)}) %collective-permute-start.3) | collective-permute-done | bytes 172064 | tf_op jit(solution)/shard_map/ppermute | solution.py:27
  36.0 1.7 %collective-permute-done.2 = f32[8,16,384]{2,1,0:T(8,128)S(1)} collective-permute-done((f32[8,16,384]{2,1,0:T(8,128)S(1)}, f32[8,16,384]{2,1,0:T(8,128)S(1)}, u32[]{:S(2)}, u32[]{:S(2)}) %collective-permute-start.2) | collective-permute-done | bytes 196640 | tf_op jit(solution)/shard_map/ppermute | solution.py:27
  37.7 0.1 pad_add_fusion
  37.8 0.0 copy-done.4
  37.8 0.0 copy-done.5
  37.8 0.1 select_reduce_fusion.1
  37.9 0.9 pad_maximum_fusion.2.inter_ref
  38.9 0.9 pad_maximum_fusion.3.stiff_ref
  39.8 0.6 stack.3.tab
  40.4 0.6 broadcast_in_dim.44.col_mask_ref
  41.0 45.0 %shard_map.86 = (f32[4,24,16,256]{3,2,1,0:T(8,128)}, f32[24,16,256]{2,1,0:T(8,128)}) custom-call(f32[5,30]{1,0:T(8,128)} %stack.3.tab, f32[30]{0:T(128)} %and_convert_fusion.ply_mask, f32[4,3,16,384]{3,2,1,0:T(8,128)} %bitcast.20, f32[30,16,384]{2,1,0:T(8,128)} %pad_maximum_fusion.3.stiff_ref, f32[31,16,384]{2,1,0:T(8,128)} %pad_maximum_fusion.2.inter_ref, ...), custom_call_target="tpu_custom_call" | custom-call | tf_op jit(solution)/shard_map/pallas_call | solution.py:252
  86.0 1.0 reduce_sum.44
  87.1 0.7 broadcast_in_dim.45
  87.7 8.1 %all-to-all-start = ((f32[8,16,256]{2,1,0:T(8,128)}), f32[8,16,256]{2,1,0:T(8,128)S(1)}, u32[]{:S(2)}, u32[]{:S(2)}) async-start(f32[8,16,256]{2,1,0:T(8,128)} %broadcast_in_dim.45), calls=%async_computation | async-start | bytes 262144 | tf_op jit(solution)/shard_map/all_to_all | solution.py:275
  95.8 6.6 %all-to-all-done = f32[8,16,256]{2,1,0:T(8,128)S(1)} async-done(((f32[8,16,256]{2,1,0:T(8,128)}), f32[8,16,256]{2,1,0:T(8,128)S(1)}, u32[]{:S(2)}, u32[]{:S(2)}) %all-to-all-start) | async-done | bytes 131104 | tf_op jit(solution)/shard_map/all_to_all | solution.py:275
  102.4 0.1 multiply_reduce_fusion
  102.5 1.8 %fusion = f32[24,16,256]{2,1,0:T(8,128)} fusion(f32[24,16,256]{2,1,0:T(8,128)} %get-tuple-element.29, f32[16,256]{1,0:T(8,128)S(1)} %multiply_reduce_fusion), kind=kOutput, calls=%fused_computation.3 | output fusion | flops 2457600 | bytes 802816 | tf_op jit(solution)/shard_map/jit(cumsum)/reduce_window_sum | solution.py:280
  (14 shorter events, 0.1 us)
Async XLA Ops:
  0.6 1.5 %copy-start = (f32[4,3,16,256]{3,2,1,0:T(8,128)S(1)}, f32[4,3,16,256]{3,2,1,0:T(8,128)}, u32[]{:S(2)}) copy-start(f32[4,3,16,256]{3,2,1,0:T(8,128)} %param.11) | copy-start | bytes 589828
  4.0 7.9 %copy-start.3 = (s32[24]{0:T(128)S(1)}, s32[24]{0:T(128)}, u32[]{:S(2)}) copy-start(s32[24]{0:T(128)} %param.13) | copy-start | bytes 292
  4.0 23.6 %copy-start.1 = (f32[24,16,256]{2,1,0:T(8,128)S(1)}, f32[24,16,256]{2,1,0:T(8,128)}, u32[]{:S(2)}) copy-start(f32[24,16,256]{2,1,0:T(8,128)} %param.15) | copy-start | bytes 1179652
  4.0 23.6 %copy-start.2 = (f32[24,16,256]{2,1,0:T(8,128)S(1)}, f32[24,16,256]{2,1,0:T(8,128)}, u32[]{:S(2)}) copy-start(f32[24,16,256]{2,1,0:T(8,128)} %param.14) | copy-start | bytes 1179652
  4.3 17.4 %collective-permute-start = (f32[60,16,3]{2,1,0:T(8,128)S(1)}, f32[60,16,3]{2,1,0:T(8,128)S(1)}, u32[]{:S(2)}, u32[]{:S(2)}) collective-permute-start(f32[60,16,3]{2,1,0:T(8,128)S(1)} %get-tuple-element.37), channel_id=1, source_target_pairs={{1,0},{2,1},{3,2},{4,3},{5,4},{6,5},{7,6},{8,7},{9,8},{10,9},{11,1... | collective-permute-start | bytes 34568 | tf_op jit(solution)/shard_map/ppermute | solution.py:27
  10.0 17.6 %collective-permute-start.1 = (f32[60,16,3]{2,1,0:T(8,128)S(1)}, f32[60,16,3]{2,1,0:T(8,128)S(1)}, u32[]{:S(2)}, u32[]{:S(2)}) collective-permute-start(f32[60,16,3]{2,1,0:T(8,128)S(1)} %get-tuple-element.38), channel_id=1, source_target_pairs={{0,1},{1,2},{2,3},{3,4},{4,5},{5,6},{6,7},{7,8},{8,9},{9,10},{10,1... | collective-permute-start | bytes 34568 | tf_op jit(solution)/shard_map/ppermute | solution.py:27
  28.7 7.3 %collective-permute-start.3 = (f32[7,16,384]{2,1,0:T(8,128)S(1)}, f32[7,16,384]{2,1,0:T(8,128)S(1)}, u32[]{:S(2)}, u32[]{:S(2)}) collective-permute-start(f32[7,16,384]{2,1,0:T(8,128)S(1)} %select_maximum_fusion.1), channel_id=1, source_target_pairs={{64,0},{128,64},{192,128},{256,192},{320,256},{384,320},{448,384},... | collective-permute-start | bytes 516104 | tf_op jit(solution)/shard_map/ppermute | solution.py:27
  30.0 7.9 %copy-start.4 = (f32[4]{0:T(128)S(1)}, f32[4]{0:T(128)}, u32[]{:S(2)}) copy-start(f32[4]{0:T(128)} %constant.113.clone) | copy-start | bytes 52
  30.0 7.8 %copy-start.5 = (f32[4]{0:T(128)S(1)}, f32[4]{0:T(128)}, u32[]{:S(2)}) copy-start(f32[4]{0:T(128)} %constant.112.clone) | copy-start | bytes 52
  30.0 7.7 %collective-permute-start.2 = (f32[8,16,384]{2,1,0:T(8,128)S(1)}, f32[8,16,384]{2,1,0:T(8,128)S(1)}, u32[]{:S(2)}, u32[]{:S(2)}) collective-permute-start(f32[8,16,384]{2,1,0:T(8,128)S(1)} %select_maximum_fusion), channel_id=1, source_target_pairs={{0,64},{64,128},{128,192},{192,256},{256,320},{320,384},{384,448},... | collective-permute-start | bytes 589832 | tf_op jit(solution)/shard_map/ppermute | solution.py:27
  87.7 14.6 %all-to-all-start = ((f32[8,16,256]{2,1,0:T(8,128)}), f32[8,16,256]{2,1,0:T(8,128)S(1)}, u32[]{:S(2)}, u32[]{:S(2)}) async-start(f32[8,16,256]{2,1,0:T(8,128)} %broadcast_in_dim.45), calls=%async_computation | async-start | bytes 262144 | tf_op jit(solution)/shard_map/all_to_all | solution.py:275

commit v8 on v7

--- a/solution.py
+++ b/solution.py
@@ -94,7 +94,10 @@
     return centre + relaxation * (source - image) / diagonal_sum
 
 
-def sweeps_kernel(tab, ply_mask, strain_ref, stiff_ref, inter_ref, col_mask_ref, adj_ref, acc_ref, src_s, a_s, b_s):
+def sweeps_kernel(
+    tab, ply_mask, strain_ref, stiff_ref, inter_ref, col_mask_ref, adj_ref, acc_ref,
+    src_s, forced_s, scale_s, up_s, down_s, a_s, b_s,
+):
     case = pl.program_id(0)
     planes, rows, lanes = stiff_ref.shape
     halo = ITERS - 1
@@ -111,10 +114,24 @@
         cond_rows, cond_cols = tab[0, p], tab[1, p]
         return 2.0 * cond_rows + 2.0 * cond_cols + inter_ref[p + 1] + inter_ref[p] + stiff_ref[p]
 
+    @pl.when(case == 0)
+    def _():
+        def scales(p, carry):
+            scale = relaxation / diagonal_at(p)
+            scale_s[p] = scale
+            up_s[p] = scale * inter_ref[p + 1]
+            down_s[p] = scale * inter_ref[p]
+            return carry
+
+        lax.fori_loop(0, planes, scales, 0)
+        acc_ref[...] = jnp.zeros(acc_ref.shape, jnp.float32)
+
     def first(p, carry):
         source = tsai_wu(strain_x, strain_y, strain_xy, tab[3, p], tab[4, p])
+        forced = relaxation * source / diagonal_at(p)
         src_s[p] = source
-        a_s[p] = relaxation * source / diagonal_at(p) * (ply_mask[p] * col_mask)
+        forced_s[p] = forced
+        a_s[p] = forced * (ply_mask[p] * col_mask)
         return carry
 
     lax.fori_loop(0, planes, first, 0)
@@ -135,34 +152,23 @@
                 - pltpu.roll(row_a, lanes - 1, 1)
                 - pltpu.roll(row_b, 1, 1)
             )
-            cond_rows, cond_cols, cond_cross = tab[0, p], tab[1, p], tab[2, p]
-            coupling_up = inter_ref[p + 1]
-            coupling_down = inter_ref[p]
-            stiffening = stiff_ref[p]
-            image = (
-                cond_rows * (2.0 * centre - along_rows)
-                + cond_cols * (2.0 * centre - along_cols)
-                - 0.5 * cond_cross * diagonal_pairs
+            in_plane = (
+                tab[0, p] * along_rows + tab[1, p] * along_cols + (0.5 * tab[2, p]) * diagonal_pairs
             )
-            image = (
-                image
-                + coupling_up * (centre - previous[p + 1])
-                + coupling_down * (centre - previous[p - 1])
-                + stiffening * centre
+            value = (
+                (1.0 - relaxation) * centre
+                + forced_s[p]
+                + scale_s[p] * in_plane
+                + up_s[p] * previous[p + 1]
+                + down_s[p] * previous[p - 1]
             )
-            diagonal_sum = 2.0 * cond_rows + 2.0 * cond_cols + coupling_up + coupling_down + stiffening
-            value = centre + relaxation * (src_s[p] - image) / diagonal_sum
             if masked:
                 value = value * (ply_mask[p] * col_mask)
             following[p] = value
             return carry
 
-        lax.fori_loop(iteration, planes - iteration, step, 0)
+        lax.fori_loop(iteration, planes - iteration, step, 0, unroll=2)
     final = buffers[(ITERS - 1) % 2]
-
-    @pl.when(case == 0)
-    def _():
-        acc_ref[...] = jnp.zeros(acc_ref.shape, jnp.float32)
 
     def store(p, carry):
         value = final[p + halo][:, :own_cols]
@@ -268,7 +274,7 @@
             jax.ShapeDtypeStruct((cases, ply_local, rows, col_local), jnp.float32),
             jax.ShapeDtypeStruct((ply_local, rows, col_local), jnp.float32),
         ],
-        scratch_shapes=[pltpu.VMEM((planes, rows, lanes), jnp.float32)] * 3,
+        scratch_shapes=[pltpu.VMEM((planes, rows, lanes), jnp.float32)] * 7,
         compiler_params=pltpu.CompilerParams(dimension_semantics=("arbitrary",)),
     )(tab, ply_mask, strain_e, stiff_e, inter_all, col_mask)
     total = jnp.sum(summed, axis=0)

time: 105 us -> 92.9 us (0.88)
  Pallas kernels: 45 us -> 33.1 us
    pallas_call x1, Pallas kernels: 45 us -> 33.1 us  [body(): pl.pallas_call(sweeps_kernel, grid=(cases,), in_specs=[pl.BlockSpec(memor...]
where the time goes in v8:
time: 92.9 us; the launch traced here: 92.3 us
  Pallas kernels  33.1 us (36%)
  waiting for transfers between devices  24.7 us (27%)
  starting transfers between devices  21.6 us (23%)
  other arithmetic  8.4 us (9%)
  local copies, waits for them, and re-layouts  3.77 us (4%)
    pallas_call x1, Pallas kernels, body(): pl.pallas_call(sweeps_kernel, grid=(cases,), in_specs=[pl.BlockSpec(memor...  33.1 us
    ppermute x4, waiting for transfers between devices, passed_along(): return lax.ppermute(array, axis, pairs)  18.1 us
    ppermute x4, starting transfers between devices, passed_along(): return lax.ppermute(array, axis, pairs)  13.5 us
    all_to_all x1, starting transfers between devices, body(): lax.all_to_all(jnp.broadcast_to(total[None], (ply_count,) + total.shape),...  8.06 us
    all_to_all x1, waiting for transfers between devices, body(): lax.all_to_all(jnp.broadcast_to(total[None], (ply_count,) + total.shape),...  6.57 us
  transfers between devices with their start and end apart: 5, of which 5 were waited for; matrix products, arithmetic and copies ran while one was open for 1% of the time, Pallas kernels for 0%

profile of v8, /device:TPU:448, one launch (start us, length us, event | category | flops | bytes accessed | tf_op | source)
XLA Modules:
  0.0 92.3 jit_solution(3137669457582857067)
XLA Ops:
  0.6 0.0 copy-start
  0.6 0.7 compare_and_fusion
  1.3 0.7 compare_select_fusion
  2.0 0.1 broadcast_in_dim.38
  2.1 0.1 broadcast_in_dim.39
  2.2 0.0 copy-done
  2.2 0.6 gather_fusion
  2.7 0.1 bitcast_select_fusion
  2.8 1.2 %pad_maximum_fusion.1 = f32[60,16,256]{2,1,0:T(8,128)S(1)} fusion(f32[24,16,256]{2,1,0:T(8,128)} %param.15, f32[24,16,256]{2,1,0:T(8,128)} %param.14, f32[12,16,256]{2,1,0:T(8,128)S(1)} %bitcast_select_fusion), kind=kLoop, calls=%fused_computation.4 | loop fusion | flops 491520 | bytes 1966080 | tf_op jit(solution)/shard_map/concatenate | solution.py:200
  4.0 0.0 copy-start.3
  4.0 0.0 copy-start.1
  4.0 0.0 copy-start.2
  4.1 0.2 fusion.14
  4.3 5.7 %collective-permute-start = (f32[60,16,3]{2,1,0:T(8,128)S(1)}, f32[60,16,3]{2,1,0:T(8,128)S(1)}, u32[]{:S(2)}, u32[]{:S(2)}) collective-permute-start(f32[60,16,3]{2,1,0:T(8,128)S(1)} %get-tuple-element.37), channel_id=1, source_target_pairs={{1,0},{2,1},{3,2},{4,3},{5,4},{6,5},{7,6},{8,7},{9,8},{10,9},{11,1... | collective-permute-start | bytes 34568 | tf_op jit(solution)/shard_map/ppermute | solution.py:27
  10.0 1.9 %collective-permute-start.1 = (f32[60,16,3]{2,1,0:T(8,128)S(1)}, f32[60,16,3]{2,1,0:T(8,128)S(1)}, u32[]{:S(2)}, u32[]{:S(2)}) collective-permute-start(f32[60,16,3]{2,1,0:T(8,128)S(1)} %get-tuple-element.38), channel_id=1, source_target_pairs={{0,1},{1,2},{2,3},{3,4},{4,5},{5,6},{6,7},{7,8},{8,9},{9,10},{10,1... | collective-permute-start | bytes 34568 | tf_op jit(solution)/shard_map/ppermute | solution.py:27
  11.9 0.0 copy-done.3
  11.9 0.1 convert_bitcast_fusion.1
  12.0 0.5 and_convert_fusion.ply_mask
  12.5 0.1 pad.27.clone
  12.6 9.0 %collective-permute-done = f32[60,16,3]{2,1,0:T(8,128)S(1)} collective-permute-done((f32[60,16,3]{2,1,0:T(8,128)S(1)}, f32[60,16,3]{2,1,0:T(8,128)S(1)}, u32[]{:S(2)}, u32[]{:S(2)}) %collective-permute-start) | collective-permute-done | bytes 11552 | tf_op jit(solution)/shard_map/ppermute | solution.py:27
  21.6 6.0 %collective-permute-done.1 = f32[60,16,3]{2,1,0:T(8,128)S(1)} collective-permute-done((f32[60,16,3]{2,1,0:T(8,128)S(1)}, f32[60,16,3]{2,1,0:T(8,128)S(1)}, u32[]{:S(2)}, u32[]{:S(2)}) %collective-permute-start.1) | collective-permute-done | bytes 11552 | tf_op jit(solution)/shard_map/ppermute | solution.py:27
  27.6 0.0 copy-done.1
  27.6 0.0 copy-done.2
  27.6 0.2 pad_maximum_fusion
  27.9 0.7 slice.124
  28.7 1.3 %collective-permute-start.3 = (f32[7,16,384]{2,1,0:T(8,128)S(1)}, f32[7,16,384]{2,1,0:T(8,128)S(1)}, u32[]{:S(2)}, u32[]{:S(2)}) collective-permute-start(f32[7,16,384]{2,1,0:T(8,128)S(1)} %select_maximum_fusion.1), channel_id=1, source_target_pairs={{64,0},{128,64},{192,128},{256,192},{320,256},{384,320},{448,384},... | collective-permute-start | bytes 516104 | tf_op jit(solution)/shard_map/ppermute | solution.py:27
  30.0 0.0 copy-start.4
  30.0 0.0 copy-start.5
  30.0 4.6 %collective-permute-start.2 = (f32[8,16,384]{2,1,0:T(8,128)S(1)}, f32[8,16,384]{2,1,0:T(8,128)S(1)}, u32[]{:S(2)}, u32[]{:S(2)}) collective-permute-start(f32[8,16,384]{2,1,0:T(8,128)S(1)} %select_maximum_fusion), channel_id=1, source_target_pairs={{0,64},{64,128},{128,192},{192,256},{256,320},{320,384},{384,448},... | collective-permute-start | bytes 589832 | tf_op jit(solution)/shard_map/ppermute | solution.py:27
  34.6 0.1 fusion.12
  34.7 1.3 %collective-permute-done.3 = f32[7,16,384]{2,1,0:T(8,128)S(1)} collective-permute-done((f32[7,16,384]{2,1,0:T(8,128)S(1)}, f32[7,16,384]{2,1,0:T(8,128)S(1)}, u32[]{:S(2)}, u32[]{:S(2)}) %collective-permute-start.3) | collective-permute-done | bytes 172064 | tf_op jit(solution)/shard_map/ppermute | solution.py:27
  36.0 1.7 %collective-permute-done.2 = f32[8,16,384]{2,1,0:T(8,128)S(1)} collective-permute-done((f32[8,16,384]{2,1,0:T(8,128)S(1)}, f32[8,16,384]{2,1,0:T(8,128)S(1)}, u32[]{:S(2)}, u32[]{:S(2)}) %collective-permute-start.2) | collective-permute-done | bytes 196640 | tf_op jit(solution)/shard_map/ppermute | solution.py:27
  37.7 0.1 pad_add_fusion
  37.8 0.0 copy-done.4
  37.8 0.0 copy-done.5
  37.8 0.1 select_reduce_fusion.1
  37.9 0.9 %pad_maximum_fusion.2.inter_ref = f32[31,16,384]{2,1,0:T(8,128)} fusion(f32[3,16,384]{2,1,0:T(8,128)S(1)} %get-tuple-element.39, f32[24,16,384]{2,1,0:T(8,128)S(1)} %get-tuple-element.32, f32[4,16,384]{2,1,0:T(8,128)S(1)} %slice.128), kind=kLoop, calls=%fused_computation.5 | loop fusion | flops 380928 | bytes 1523712 | tf_op jit(solution)/shard_map/concatenate | solution.py:243
  38.9 0.9 %pad_maximum_fusion.3.stiff_ref = f32[30,16,384]{2,1,0:T(8,128)} fusion(f32[3,16,384]{2,1,0:T(8,128)S(1)} %get-tuple-element.40, f32[24,16,384]{2,1,0:T(8,128)S(1)} %get-tuple-element.33, f32[3,16,384]{2,1,0:T(8,128)S(1)} %slice.125), kind=kLoop, calls=%fused_computation.6 | loop fusion | flops 368640 | bytes 1474560 | tf_op jit(solution)/shard_map/concatenate | solution.py:242
  39.8 0.6 stack.3.tab
  40.4 0.6 broadcast_in_dim.44.col_mask_ref
  41.0 33.1 %shard_map.86 = (f32[4,24,16,256]{3,2,1,0:T(8,128)}, f32[24,16,256]{2,1,0:T(8,128)}) custom-call(f32[5,30]{1,0:T(8,128)} %stack.3.tab, f32[30]{0:T(128)} %and_convert_fusion.ply_mask, f32[4,3,16,384]{3,2,1,0:T(8,128)} %bitcast.20, f32[30,16,384]{2,1,0:T(8,128)} %pad_maximum_fusion.3.stiff_ref, f32[31,16,384]{2,1,0:T(8,128)} %pad_maximum_fusion.2.inter_ref, ...), custom_call_target="tpu_custom_call" | custom-call | tf_op jit(solution)/shard_map/pallas_call | solution.py:258
  74.1 1.0 %reduce_sum.44 = f32[16,256]{1,0:T(8,128)S(1)} reduce(f32[24,16,256]{2,1,0:T(8,128)} %get-tuple-element.29, f32[]{:T(128)} %constant.97.clone.1), dimensions={0}, to_apply=%region_3.4 | reduce | flops 94208 | bytes 409604 | tf_op jit(solution)/shard_map/reduce_sum | solution.py:280
  75.1 0.7 broadcast_in_dim.45
  75.8 8.1 %all-to-all-start = ((f32[8,16,256]{2,1,0:T(8,128)}), f32[8,16,256]{2,1,0:T(8,128)S(1)}, u32[]{:S(2)}, u32[]{:S(2)}) async-start(f32[8,16,256]{2,1,0:T(8,128)} %broadcast_in_dim.45), calls=%async_computation | async-start | bytes 262144 | tf_op jit(solution)/shard_map/all_to_all | solution.py:281
  83.8 6.6 %all-to-all-done = f32[8,16,256]{2,1,0:T(8,128)S(1)} async-done(((f32[8,16,256]{2,1,0:T(8,128)}), f32[8,16,256]{2,1,0:T(8,128)S(1)}, u32[]{:S(2)}, u32[]{:S(2)}) %all-to-all-start) | async-done | bytes 131104 | tf_op jit(solution)/shard_map/all_to_all | solution.py:281
  90.4 0.1 multiply_reduce_fusion
  90.5 1.8 %fusion = f32[24,16,256]{2,1,0:T(8,128)} fusion(f32[24,16,256]{2,1,0:T(8,128)} %get-tuple-element.29, f32[16,256]{1,0:T(8,128)S(1)} %multiply_reduce_fusion), kind=kOutput, calls=%fused_computation.3 | output fusion | flops 2457600 | bytes 802816 | tf_op jit(solution)/shard_map/jit(cumsum)/reduce_window_sum | solution.py:286
  (14 shorter events, 0.1 us)
Async XLA Ops:
  0.6 1.5 %copy-start = (f32[4,3,16,256]{3,2,1,0:T(8,128)S(1)}, f32[4,3,16,256]{3,2,1,0:T(8,128)}, u32[]{:S(2)}) copy-start(f32[4,3,16,256]{3,2,1,0:T(8,128)} %param.11) | copy-start | bytes 589828
  4.0 7.9 %copy-start.3 = (s32[24]{0:T(128)S(1)}, s32[24]{0:T(128)}, u32[]{:S(2)}) copy-start(s32[24]{0:T(128)} %param.13) | copy-start | bytes 292
  4.0 23.6 %copy-start.1 = (f32[24,16,256]{2,1,0:T(8,128)S(1)}, f32[24,16,256]{2,1,0:T(8,128)}, u32[]{:S(2)}) copy-start(f32[24,16,256]{2,1,0:T(8,128)} %param.15) | copy-start | bytes 1179652
  4.0 23.6 %copy-start.2 = (f32[24,16,256]{2,1,0:T(8,128)S(1)}, f32[24,16,256]{2,1,0:T(8,128)}, u32[]{:S(2)}) copy-start(f32[24,16,256]{2,1,0:T(8,128)} %param.14) | copy-start | bytes 1179652
  4.3 17.4 %collective-permute-start = (f32[60,16,3]{2,1,0:T(8,128)S(1)}, f32[60,16,3]{2,1,0:T(8,128)S(1)}, u32[]{:S(2)}, u32[]{:S(2)}) collective-permute-start(f32[60,16,3]{2,1,0:T(8,128)S(1)} %get-tuple-element.37), channel_id=1, source_target_pairs={{1,0},{2,1},{3,2},{4,3},{5,4},{6,5},{7,6},{8,7},{9,8},{10,9},{11,1... | collective-permute-start | bytes 34568 | tf_op jit(solution)/shard_map/ppermute | solution.py:27
  10.0 17.6 %collective-permute-start.1 = (f32[60,16,3]{2,1,0:T(8,128)S(1)}, f32[60,16,3]{2,1,0:T(8,128)S(1)}, u32[]{:S(2)}, u32[]{:S(2)}) collective-permute-start(f32[60,16,3]{2,1,0:T(8,128)S(1)} %get-tuple-element.38), channel_id=1, source_target_pairs={{0,1},{1,2},{2,3},{3,4},{4,5},{5,6},{6,7},{7,8},{8,9},{9,10},{10,1... | collective-permute-start | bytes 34568 | tf_op jit(solution)/shard_map/ppermute | solution.py:27
  28.7 7.3 %collective-permute-start.3 = (f32[7,16,384]{2,1,0:T(8,128)S(1)}, f32[7,16,384]{2,1,0:T(8,128)S(1)}, u32[]{:S(2)}, u32[]{:S(2)}) collective-permute-start(f32[7,16,384]{2,1,0:T(8,128)S(1)} %select_maximum_fusion.1), channel_id=1, source_target_pairs={{64,0},{128,64},{192,128},{256,192},{320,256},{384,320},{448,384},... | collective-permute-start | bytes 516104 | tf_op jit(solution)/shard_map/ppermute | solution.py:27
  30.0 7.9 %copy-start.4 = (f32[4]{0:T(128)S(1)}, f32[4]{0:T(128)}, u32[]{:S(2)}) copy-start(f32[4]{0:T(128)} %constant.113.clone) | copy-start | bytes 52
  30.0 7.8 %copy-start.5 = (f32[4]{0:T(128)S(1)}, f32[4]{0:T(128)}, u32[]{:S(2)}) copy-start(f32[4]{0:T(128)} %constant.112.clone) | copy-start | bytes 52
  30.0 7.7 %collective-permute-start.2 = (f32[8,16,384]{2,1,0:T(8,128)S(1)}, f32[8,16,384]{2,1,0:T(8,128)S(1)}, u32[]{:S(2)}, u32[]{:S(2)}) collective-permute-start(f32[8,16,384]{2,1,0:T(8,128)S(1)} %select_maximum_fusion), channel_id=1, source_target_pairs={{0,64},{64,128},{128,192},{192,256},{256,320},{320,384},{384,448},... | collective-permute-start | bytes 589832 | tf_op jit(solution)/shard_map/ppermute | solution.py:27
  75.8 14.6 %all-to-all-start = ((f32[8,16,256]{2,1,0:T(8,128)}), f32[8,16,256]{2,1,0:T(8,128)S(1)}, u32[]{:S(2)}, u32[]{:S(2)}) async-start(f32[8,16,256]{2,1,0:T(8,128)} %broadcast_in_dim.45), calls=%async_computation | async-start | bytes 262144 | tf_op jit(solution)/shard_map/all_to_all | solution.py:281

commit v9 on v5

--- a/solution.py
+++ b/solution.py
@@ -106,17 +106,37 @@
     ply_count = lax.axis_size("ply")
     tile_count = lax.axis_size("tile")
     cases = case_ids.shape[0]
-    chosen = jnp.take(strain, case_ids, axis=0)
-    rows = chosen.shape[2]
-
-    packed = jnp.concatenate(
-        [chosen.reshape(cases * 3, rows, col_local), stiffening, interface], axis=0
-    )
-    packed = with_halos(packed, "tile", 2, halo, halo)
+    rows = strain.shape[2]
     width = col_local + 2 * halo
-    strain_e = packed[: cases * 3].reshape(cases, 3, rows, width)
-    stiff_c = packed[cases * 3 : cases * 3 + ply_local]
-    inter_c = packed[cases * 3 + ply_local :]
+
+    def edge(start):
+        return jnp.concatenate(
+            [
+                lax.slice_in_dim(strain, start, start + halo, axis=3).reshape(-1, rows, halo),
+                lax.slice_in_dim(stiffening, start, start + halo, axis=2),
+                lax.slice_in_dim(interface, start, start + halo, axis=2),
+            ],
+            axis=0,
+        )
+
+    left = passed_along(edge(col_local - halo), "tile", 1)
+    right = passed_along(edge(0), "tile", -1)
+    states = strain.shape[0] * 3
+    strain_all = jnp.concatenate(
+        [
+            left[:states].reshape(strain.shape[:3] + (halo,)),
+            strain,
+            right[:states].reshape(strain.shape[:3] + (halo,)),
+        ],
+        axis=3,
+    )
+    strain_e = jnp.take(strain_all, case_ids, axis=0)
+    stiff_c = jnp.concatenate(
+        [left[states : states + ply_local], stiffening, right[states : states + ply_local]], axis=2
+    )
+    inter_c = jnp.concatenate(
+        [left[states + ply_local :], interface, right[states + ply_local :]], axis=2
+    )
     angle_plane = jnp.zeros((1, rows, width), jnp.float32)
     below = passed_along(
         jnp.concatenate(

time: 85.1 us -> 79.7 us (0.937)
  waiting for transfers between devices: 24.7 us -> 13.2 us
  local copies, waits for them, and re-layouts: 1.84 us -> 8.01 us
    ppermute x4, waiting for transfers between devices: 18.1 us -> 6.59 us  [passed_along(): return lax.ppermute(array, axis, pairs)]
    slice x1 -> x11, local copies, waits for them, and re-layouts: 0.19 us -> 4.45 us  [the longest x1 1.2 us: edge(): lax.slice_in_dim(interface, start, start + halo, axis=2)]
    add x2 -> x0, other arithmetic: 3.13 us -> none  [sweep(): 2.0 * cond_rows + 2.0 * cond_cols + coupling_up + coupling_down + stiffening]
    slice x1 -> x3, other arithmetic: 1.73 us -> 4.73 us  [trim(): return lax.slice_in_dim(array, by, array.shape[col_dim] - by, axis=col_dim)]
    mul x3, other arithmetic: 0.22 us -> 1.93 us  [sweep(): cond_rows * (2.0 * centre - along_rows)]
  transfers between devices with their start and end apart: 5 -> 5, of which waited for: 5 -> 3; matrix products, arithmetic and copies ran while one was open for 1% -> 4% of each run, Pallas kernels for 0% -> 0%
where the time goes in v9:
time: 79.7 us; the launch traced here: 79.1 us
  other arithmetic  35.4 us (44%)
  starting transfers between devices  21.4 us (27%)
  waiting for transfers between devices  13.2 us (17%)
  local copies, waits for them, and re-layouts  8.01 us (10%)
  between operations  1.04 us (1%)
    mul x2, other arithmetic, body(): adjoint = adjoint * trim(inside, by, 0, 2)  17.2 us
    ppermute x4, starting transfers between devices, passed_along(): return lax.ppermute(array, axis, pairs)  13.4 us
    all_to_all x1, starting transfers between devices, body(): lax.all_to_all(jnp.broadcast_to(total[None], (ply_count,) + total.shape),...  8.06 us
    ppermute x4, waiting for transfers between devices, passed_along(): return lax.ppermute(array, axis, pairs)  6.59 us
    all_to_all x1, waiting for transfers between devices, body(): lax.all_to_all(jnp.broadcast_to(total[None], (ply_count,) + total.shape),...  6.57 us
    reduce_sum x1, other arithmetic, body(): total = jnp.sum(product, axis=(0, 1))  5.03 us
    slice x3, other arithmetic, trim(): return lax.slice_in_dim(array, by, array.shape[col_dim] - by, axis=col_dim)  4.73 us
    mul x1, other arithmetic, body(): adjoint = relaxation * source_e / diagonal_sum * inside  3.65 us
  transfers between devices with their start and end apart: 5, of which 3 were waited for; matrix products, arithmetic and copies ran while one was open for 4% of the time, Pallas kernels for 0%

profile of v9, /device:TPU:448, one launch (start us, length us, event | category | flops | bytes accessed | tf_op | source)
XLA Modules:
  0.0 79.1 jit_solution(11836656453304551708)
XLA Ops:
  0.7 1.2 %fusion.86 = (f32[24,16,3]{2,1,0:T(8,128)S(1)}, f32[24,16,3]{2,1,0:T(8,128)S(1)}) fusion(f32[24,16,256]{2,1,0:T(8,128)} %param.15), kind=kLoop, calls=%fused_computation.193 | loop fusion | bytes 18432 | tf_op jit(solution)/shard_map/slice | solution.py:117
  1.9 0.2 copy.60
  2.1 1.1 %fusion.85 = (f32[24,16,3]{2,1,0:T(8,128)S(1)}, f32[24,16,3]{2,1,0:T(8,128)S(1)}) fusion(f32[24,16,256]{2,1,0:T(8,128)} %param.14), kind=kLoop, calls=%fused_computation.192 | loop fusion | bytes 18432 | tf_op jit(solution)/shard_map/slice | solution.py:116
  3.2 0.2 copy.59
  3.4 1.0 %fusion.87 = (f32[4,3,16,3]{3,2,1,0:T(8,128)S(1)}, f32[4,3,16,3]{3,2,1,0:T(8,128)S(1)}) fusion(f32[4,3,16,256]{3,2,1,0:T(8,128)} %param.11), kind=kLoop, calls=%fused_computation.194 | loop fusion | bytes 9216 | tf_op jit(solution)/shard_map/slice | solution.py:115
  4.4 0.2 copy.44
  4.7 5.6 %collective-permute-start.1 = (f32[60,16,3]{0,1,2:T(8,128)S(1)}, f32[60,16,3]{0,1,2:T(8,128)S(1)}, u32[]{:S(2)}, u32[]{:S(2)}) collective-permute-start(f32[60,16,3]{0,1,2:T(8,128)S(1)} %pad_maximum_fusion.6), channel_id=1, source_target_pairs={{1,0},{2,1},{3,2},{4,3},{5,4},{6,5},{7,6},{8,7},{9,8},{10,9},{11,1... | collective-permute-start | bytes 34568 | tf_op jit(solution)/shard_map/ppermute | solution.py:25
  10.3 0.2 copy.58
  10.5 0.2 copy.57
  10.7 0.2 copy.40
  11.0 1.9 %collective-permute-start = (f32[60,16,3]{0,1,2:T(8,128)S(1)}, f32[60,16,3]{0,1,2:T(8,128)S(1)}, u32[]{:S(2)}, u32[]{:S(2)}) collective-permute-start(f32[60,16,3]{0,1,2:T(8,128)S(1)} %pad_maximum_fusion.5), channel_id=1, source_target_pairs={{0,1},{1,2},{2,3},{3,4},{4,5},{5,6},{6,7},{7,8},{8,9},{9,10},{10,1... | collective-permute-start | bytes 34568 | tf_op jit(solution)/shard_map/ppermute | solution.py:25
  13.1 0.1 slice_bitcast_fusion.4
  13.2 0.7 slice_bitcast_fusion.3
  14.1 0.2 copy.48
  14.3 4.9 %collective-permute-done = f32[60,16,3]{0,1,2:T(8,128)S(1)} collective-permute-done((f32[60,16,3]{0,1,2:T(8,128)S(1)}, f32[60,16,3]{0,1,2:T(8,128)S(1)}, u32[]{:S(2)}, u32[]{:S(2)}) %collective-permute-start) | collective-permute-done | bytes 11552 | tf_op jit(solution)/shard_map/ppermute | solution.py:25
  19.2 0.2 copy.47
  19.4 0.2 copy.46
  19.6 0.2 copy.45
  19.8 0.1 select_maximum_fusion.3
  20.0 1.3 %collective-permute-start.3 = (f32[7,16,262]{2,1,0:T(8,128)S(1)}, f32[7,16,262]{2,1,0:T(8,128)S(1)}, u32[]{:S(2)}, u32[]{:S(2)}) collective-permute-start(f32[7,16,262]{2,1,0:T(8,128)S(1)} %select_maximum_fusion.3), channel_id=1, source_target_pairs={{64,0},{128,64},{192,128},{256,192},{320,256},{384,320},{448,384},... | collective-permute-start | bytes 352136 | tf_op jit(solution)/shard_map/ppermute | solution.py:25
  21.3 0.1 select_maximum_fusion
  21.4 4.6 %collective-permute-start.2 = (f32[8,16,262]{2,1,0:T(8,128)S(1)}, f32[8,16,262]{2,1,0:T(8,128)S(1)}, u32[]{:S(2)}, u32[]{:S(2)}) collective-permute-start(f32[8,16,262]{2,1,0:T(8,128)S(1)} %select_maximum_fusion), channel_id=1, source_target_pairs={{0,64},{64,128},{128,192},{192,256},{256,320},{320,384},{384,448},... | collective-permute-start | bytes 402440 | tf_op jit(solution)/shard_map/ppermute | solution.py:25
  26.0 0.1 copy.50
  26.0 0.1 copy.52
  26.2 0.1 copy.49
  26.3 0.1 copy.51
  26.5 0.2 pad_maximum_fusion.2
  26.6 0.6 gather_fusion
  27.2 0.1 broadcast_select_fusion
  27.4 1.7 %collective-permute-done.2 = f32[8,16,262]{2,1,0:T(8,128)S(1)} collective-permute-done((f32[8,16,262]{2,1,0:T(8,128)S(1)}, f32[8,16,262]{2,1,0:T(8,128)S(1)}, u32[]{:S(2)}, u32[]{:S(2)}) %collective-permute-start.2) | collective-permute-done | bytes 134176 | tf_op jit(solution)/shard_map/ppermute | solution.py:25
  29.2 0.1 select_reduce_fusion.1
  29.3 0.6 slice_bitcast_fusion.6
  29.9 0.7 slice_bitcast_fusion.10
  30.6 0.7 slice_bitcast_fusion.8
  31.3 0.3 maximum_maximum_fusion
  31.5 0.3 pad_maximum_fusion
  31.8 0.9 %fusion.84 = (f32[24,16,256]{2,1,0:T(8,128)S(1)}, f32[24,16,256]{2,1,0:T(8,128)}) fusion(f32[28,16,262]{2,1,0:T(8,128)S(1)} %maximum_maximum_fusion, f32[24,16,256]{2,1,0:T(8,128)S(1)} %copy-done.2, f32[24,16,256]{2,1,0:T(8,128)S(1)} %copy-done.1, f32[24]{0:T(128)S(1)} %get-tuple-element.73), kind=kLoop, calls=%fused_computation.191 | loop fusion | flops 294912 | bytes 1966176 | tf_op jit(solution)/shard_map/slice | solution.py:99
  32.8 0.3 fusion.63
  33.1 1.7 %fusion.83 = (f32[28,16,260]{2,1,0:T(8,128)S(1)}, f32[28,16,260]{2,1,0:T(8,128)S(1)}, f32[28,16,260]{2,1,0:T(8,128)}, f32[28,16,260]{2,1,0:T(8,128)}) fusion(f32[31,16,262]{2,1,0:T(8,128)S(1)} %pad_maximum_fusion, f32[30,16,262]{2,1,0:T(8,128)S(1)} %get-tuple-element.34, f32[28]{0:T(128)S(1)} %get-tuple-element.79), kind=kLoop, calls=%fused_computation.190 | loop fusion | flops 349440 | bytes 3261552 | tf_op jit(solution)/shard_map/slice | solution.py:99
  34.8 2.1 %fusion.82 = (f32[26,16,258]{2,1,0:T(8,128)}, f32[26,16,258]{2,1,0:T(8,128)}, f32[26,16,258]{2,1,0:T(8,128)}, f32[26,16,258]{2,1,0:T(8,128)}) fusion(f32[31,16,262]{2,1,0:T(8,128)S(1)} %pad_maximum_fusion, f32[30,16,262]{2,1,0:T(8,128)S(1)} %get-tuple-element.34, f32[28,16,262]{2,1,0:T(8,128)S(1)} %maximum_maximum_fusion, f32[26]{0:T(128)S(1)} %get-tuple-element.76), kind=kLoop, calls=%fused_computation.189 | loop fusion | flops 321984 | bytes 3005288 | tf_op jit(solution)/shard_map/slice | solution.py:99
  36.9 3.6 %divide_multiply_fusion = (f32[4,30,16,262]{3,2,1,0:T(8,128)S(1)}, f32[4,30,16,262]{3,2,1,0:T(8,128)}) fusion(f32[30,262]{1,0:T(8,128)S(1)} %and_convert_fusion.1, f32[30,16,262]{2,1,0:T(8,128)S(1)} %get-tuple-element.33, f32[30]{0:T(128)S(1)} %get-tuple-element.68, f32[4,16,262]{2,1,0:T(8,128)S(1)} %get-tuple-element.52, f32[30]{0:T(128)S(1)} %get-tuple-element.69, ...), kind=kLoop, calls=%fused_computation.21 | loop fusion | flops 12072960 | bytes 4827688 | tf_op jit(solution)/shard_map/mul | solution.py:195
  40.5 8.6 %fusion.20 = f32[4,28,16,260]{3,2,1,0:T(8,128)S(1)} fusion(f32[4,30,16,262]{3,2,1,0:T(8,128)S(1)} %get-tuple-element.45, f32[4,30,16,262]{3,2,1,0:T(8,128)} %get-tuple-element.46, f32[28,260]{1,0:T(8,128)S(1)} %slice_bitcast_fusion.4, f32[28,16,260]{2,1,0:T(8,128)S(1)} %get-tuple-element.38, f32[28,16,260]{2,1,0:T(8,128)} %get-tuple-element.40, ...), kind=kLoop, calls=%fused_computation.46 | loop fusion | flops 12113920 | bytes 22797424 | tf_op jit(solution)/shard_map/mul | solution.py:209
  49.2 8.6 %fusion.41 = f32[4,26,16,258]{3,2,1,0:T(8,128)S(1)} fusion(f32[4,28,16,260]{3,2,1,0:T(8,128)S(1)} %fusion.20, f32[4,30,16,262]{3,2,1,0:T(8,128)} %get-tuple-element.46, f32[26,258]{1,0:T(8,128)} %slice_bitcast_fusion.3, f32[26,16,258]{2,1,0:T(8,128)} %get-tuple-element.36, f32[26,16,258]{2,1,0:T(8,128)} %get-tuple-element.41, ...), kind=kLoop, calls=%fused_computation.70 | loop fusion | flops 11162112 | bytes 20710920 | tf_op jit(solution)/shard_map/mul | solution.py:209
  57.8 5.0 %fusion.64 = (f32[16,256]{1,0:T(8,128)S(1)}, f32[24,16,256]{2,1,0:T(8,128)S(1)}, f32[4,24,16,256]{3,2,1,0:T(8,128)}) fusion(f32[4,30,16,262]{3,2,1,0:T(8,128)S(1)} %copy-done, f32[24,16,256]{2,1,0:T(8,128)S(1)} %copy-done.3, f32[24,16,256]{2,1,0:T(8,128)S(1)} %copy-done.2, f32[4,26,16,258]{3,2,1,0:T(8,128)S(1)} %fusion.41, ...), kind=kLoop, calls=%fused_computation.105 | loop fusion | flops 10907648 | bytes 15549952 | tf_op jit(solution)/shard_map/reduce_sum | solution.py:212
  62.9 0.7 broadcast_in_dim.17
  63.5 8.1 %all-to-all-start = ((f32[8,16,256]{2,1,0:T(8,128)}), f32[8,16,256]{2,1,0:T(8,128)S(1)}, u32[]{:S(2)}, u32[]{:S(2)}) async-start(f32[8,16,256]{2,1,0:T(8,128)} %broadcast_in_dim.17), calls=%async_computation | async-start | bytes 262144 | tf_op jit(solution)/shard_map/all_to_all | solution.py:213
  71.6 6.6 %all-to-all-done = f32[8,16,256]{2,1,0:T(8,128)S(1)} async-done(((f32[8,16,256]{2,1,0:T(8,128)}), f32[8,16,256]{2,1,0:T(8,128)S(1)}, u32[]{:S(2)}, u32[]{:S(2)}) %all-to-all-start) | async-done | bytes 131104 | tf_op jit(solution)/shard_map/all_to_all | solution.py:213
  78.3 0.8 %fusion.62 = f32[24,16,256]{2,1,0:T(8,128)} fusion(f32[24,16,256]{2,1,0:T(8,128)S(1)} %get-tuple-element.27, f32[16,256]{1,0:T(8,128)S(1)} %multiply_reduce_fusion), kind=kOutput, calls=%fused_computation.96 | output fusion | flops 2457600 | bytes 802816 | tf_op jit(solution)/shard_map/jit(cumsum)/reduce_window_sum | solution.py:218
  (49 shorter events, 0.9 us)
Async XLA Ops:
  0.6 19.2 %copy-start.1 = (f32[24,16,256]{2,1,0:T(8,128)S(1)}, f32[24,16,256]{2,1,0:T(8,128)}, u32[]{:S(2)}) copy-start(f32[24,16,256]{2,1,0:T(8,128)} %param.15) | copy-start | bytes 1179652
  0.6 19.2 %copy-start.2 = (f32[24,16,256]{2,1,0:T(8,128)S(1)}, f32[24,16,256]{2,1,0:T(8,128)}, u32[]{:S(2)}) copy-start(f32[24,16,256]{2,1,0:T(8,128)} %param.14) | copy-start | bytes 1179652
  0.7 12.3 %copy-start.11 = (s32[4]{0:T(128)S(1)}, s32[4]{0:T(128)}, u32[]{:S(2)}) copy-start(s32[4]{0:T(128)} %param.12) | copy-start | bytes 52
  0.7 13.3 %copy-start.5 = (s32[24]{0:T(128)S(1)}, s32[24]{0:T(128)}, u32[]{:S(2)}) copy-start(s32[24]{0:T(128)} %param.13) | copy-start | bytes 292
  4.7 9.3 %collective-permute-start.1 = (f32[60,16,3]{0,1,2:T(8,128)S(1)}, f32[60,16,3]{0,1,2:T(8,128)S(1)}, u32[]{:S(2)}, u32[]{:S(2)}) collective-permute-start(f32[60,16,3]{0,1,2:T(8,128)S(1)} %pad_maximum_fusion.6), channel_id=1, source_target_pairs={{1,0},{2,1},{3,2},{4,3},{5,4},{6,5},{7,6},{8,7},{9,8},{10,9},{11,1... | collective-permute-start | bytes 34568 | tf_op jit(solution)/shard_map/ppermute | solution.py:25
  10.7 15.8 %copy-start.4 = (f32[4,3,16,256]{3,2,1,0:T(8,128)S(1)}, f32[4,3,16,256]{3,2,1,0:T(8,128)}, u32[]{:S(2)}) copy-start(f32[4,3,16,256]{3,2,1,0:T(8,128)} %param.11) | copy-start | bytes 589828
  11.0 8.1 %collective-permute-start = (f32[60,16,3]{0,1,2:T(8,128)S(1)}, f32[60,16,3]{0,1,2:T(8,128)S(1)}, u32[]{:S(2)}, u32[]{:S(2)}) collective-permute-start(f32[60,16,3]{0,1,2:T(8,128)S(1)} %pad_maximum_fusion.5), channel_id=1, source_target_pairs={{0,1},{1,2},{2,3},{3,4},{4,5},{5,6},{6,7},{7,8},{8,9},{9,10},{10,1... | collective-permute-start | bytes 34568 | tf_op jit(solution)/shard_map/ppermute | solution.py:25
  19.9 9.3 %copy-start.9 = (f32[4]{0:T(128)S(1)}, f32[4]{0:T(128)}, u32[]{:S(2)}) copy-start(f32[4]{0:T(128)} %constant.138.clone) | copy-start | bytes 52
  19.9 9.3 %copy-start.10 = (f32[4]{0:T(128)S(1)}, f32[4]{0:T(128)}, u32[]{:S(2)}) copy-start(f32[4]{0:T(128)} %constant.139.clone) | copy-start | bytes 52
  20.0 7.4 %collective-permute-start.3 = (f32[7,16,262]{2,1,0:T(8,128)S(1)}, f32[7,16,262]{2,1,0:T(8,128)S(1)}, u32[]{:S(2)}, u32[]{:S(2)}) collective-permute-start(f32[7,16,262]{2,1,0:T(8,128)S(1)} %select_maximum_fusion.3), channel_id=1, source_target_pairs={{64,0},{128,64},{192,128},{256,192},{320,256},{384,320},{448,384},... | collective-permute-start | bytes 352136 | tf_op jit(solution)/shard_map/ppermute | solution.py:25
  21.4 7.7 %collective-permute-start.2 = (f32[8,16,262]{2,1,0:T(8,128)S(1)}, f32[8,16,262]{2,1,0:T(8,128)S(1)}, u32[]{:S(2)}, u32[]{:S(2)}) collective-permute-start(f32[8,16,262]{2,1,0:T(8,128)S(1)} %select_maximum_fusion), channel_id=1, source_target_pairs={{0,64},{64,128},{128,192},{192,256},{256,320},{320,384},{384,448},... | collective-permute-start | bytes 402440 | tf_op jit(solution)/shard_map/ppermute | solution.py:25
  49.1 8.7 %copy-start = (f32[4,30,16,262]{3,2,1,0:T(8,128)S(1)}, f32[4,30,16,262]{3,2,1,0:T(8,128)}, u32[]{:S(2)}) copy-start(f32[4,30,16,262]{3,2,1,0:T(8,128)} %get-tuple-element.46) | copy-start | bytes 6036484
  49.1 8.7 %copy-start.3 = (f32[24,16,256]{2,1,0:T(8,128)S(1)}, f32[24,16,256]{2,1,0:T(8,128)}, u32[]{:S(2)}) copy-start(f32[24,16,256]{2,1,0:T(8,128)} %get-tuple-element.44) | copy-start | bytes 1179652
  49.1 8.7 %copy-start.6 = (f32[24]{0:T(128)S(1)}, f32[24]{0:T(128)}, u32[]{:S(2)}) copy-start(f32[24]{0:T(128)} %get-tuple-element.72) | copy-start | bytes 292
  49.2 8.7 %copy-start.7 = (f32[24]{0:T(128)S(1)}, f32[24]{0:T(128)}, u32[]{:S(2)}) copy-start(f32[24]{0:T(128)} %get-tuple-element.74) | copy-start | bytes 292
  49.2 8.7 %copy-start.8 = (f32[24]{0:T(128)S(1)}, f32[24]{0:T(128)}, u32[]{:S(2)}) copy-start(f32[24]{0:T(128)} %get-tuple-element.83) | copy-start | bytes 292
  63.5 14.6 %all-to-all-start = ((f32[8,16,256]{2,1,0:T(8,128)}), f32[8,16,256]{2,1,0:T(8,128)S(1)}, u32[]{:S(2)}, u32[]{:S(2)}) async-start(f32[8,16,256]{2,1,0:T(8,128)} %broadcast_in_dim.17), calls=%async_computation | async-start | bytes 262144 | tf_op jit(solution)/shard_map/all_to_all | solution.py:213

commit v10 on v9

--- a/solution.py
+++ b/solution.py
@@ -193,20 +193,28 @@
 
     diagonal_sum = 2.0 * cond_rows + 2.0 * cond_cols + up_e + down_e + stiff_e
     adjoint = relaxation * source_e / diagonal_sum * inside
-    for iteration in range(1, ITERS):
-        by = iteration
+    for iteration in range(1, ITERS - 1):
         adjoint = sweep(
-            adjoint,
-            trim(source_e, by, 1, 3),
-            trim(stiff_e, by, 0, 2),
-            trim(up_e, by, 0, 2),
-            trim(down_e, by, 0, 2),
-            cond_rows[by : cond_rows.shape[0] - by],
-            cond_cols[by : cond_cols.shape[0] - by],
-            cond_cross[by : cond_cross.shape[0] - by],
+            jnp.pad(adjoint, ((0, 0), (1, 1), (0, 0), (1, 1))),
+            source_e,
+            stiff_e,
+            up_e,
+            down_e,
+            cond_rows,
+            cond_cols,
+            cond_cross,
         )
-        if iteration < ITERS - 1:
-            adjoint = adjoint * trim(inside, by, 0, 2)
+        adjoint = adjoint * inside
+    adjoint = sweep(
+        trim(adjoint, halo - 1, 1, 3),
+        trim(source_e, halo, 1, 3),
+        trim(stiff_e, halo, 0, 2),
+        trim(up_e, halo, 0, 2),
+        trim(down_e, halo, 0, 2),
+        cond_rows[halo : cond_rows.shape[0] - halo],
+        cond_cols[halo : cond_cols.shape[0] - halo],
+        cond_cross[halo : cond_cross.shape[0] - halo],
+    )
     source = trim(source_e, halo, 1, 3)
     product = adjoint * source
     total = jnp.sum(product, axis=(0, 1))

time: 79.7 us -> 90.7 us (1.14)
  other arithmetic: 35.4 us -> 42.9 us
  local copies, waits for them, and re-layouts: 8.01 us -> 13.2 us
  starting transfers between devices: 21.4 us -> 19.4 us
    mul x2 -> x3, other arithmetic: 17.2 us -> 28.6 us  [the longest x2 28.5 us: body(): adjoint = adjoint * inside]
    slice x3 -> x0, other arithmetic: 4.73 us -> none  [trim(): return lax.slice_in_dim(array, by, array.shape[col_dim] - by, axis=col_dim)]
    pad x0 -> x2, local copies, waits for them, and re-layouts: none -> 3.29 us  [body(): jnp.pad(adjoint, ((0, 0), (1, 1), (0, 0), (1, 1)))]
    slice x0 -> x1, local copies, waits for them, and re-layouts: none -> 2.6 us  [trim(): return lax.slice_in_dim(array, by, array.shape[col_dim] - by, axis=col_dim)]
    all_to_all x1, starting transfers between devices: 8.06 us -> 6.14 us  [body(): lax.all_to_all(jnp.broadcast_to(total[None], (ply_count,) + total.shape),...]
    mul x3 -> x1, other arithmetic: 1.93 us -> 0.77 us  [sweep(): cond_rows * (2.0 * centre - along_rows)]
    add x0 -> x1, other arithmetic: none -> 1.08 us  [sweep(): 2.0 * cond_rows + 2.0 * cond_cols + coupling_up + coupling_down + stiffening]
  transfers between devices with their start and end apart: 5 -> 5, of which waited for: 3 -> 3; matrix products, arithmetic and copies ran while one was open for 4% -> 3% of each run, Pallas kernels for 0% -> 0%
where the time goes in v10:
time: 90.7 us; the launch traced here: 90 us
  other arithmetic  42.9 us (47%)
  starting transfers between devices  19.4 us (21%)
  waiting for transfers between devices  13.3 us (15%)
  local copies, waits for them, and re-layouts  13.2 us (15%)
  between operations  1.25 us (1%)
    mul x2, other arithmetic, body(): adjoint = adjoint * inside  28.5 us
    ppermute x4, starting transfers between devices, passed_along(): return lax.ppermute(array, axis, pairs)  13.3 us
    ppermute x4, waiting for transfers between devices, passed_along(): return lax.ppermute(array, axis, pairs)  6.73 us
    all_to_all x1, waiting for transfers between devices, body(): lax.all_to_all(jnp.broadcast_to(total[None], (ply_count,) + total.shape),...  6.57 us
    all_to_all x1, starting transfers between devices, body(): lax.all_to_all(jnp.broadcast_to(total[None], (ply_count,) + total.shape),...  6.14 us
    reduce_sum x1, other arithmetic, body(): total = jnp.sum(product, axis=(0, 1))  5.41 us
    mul x1, other arithmetic, body(): adjoint = relaxation * source_e / diagonal_sum * inside  3.9 us
    pad x2, local copies, waits for them, and re-layouts, body(): jnp.pad(adjoint, ((0, 0), (1, 1), (0, 0), (1, 1)))  3.29 us
  transfers between devices with their start and end apart: 5, of which 3 were waited for; matrix products, arithmetic and copies ran while one was open for 3% of the time, Pallas kernels for 0%

profile of v10, /device:TPU:448, one launch (start us, length us, event | category | flops | bytes accessed | tf_op | source)
XLA Modules:
  0.0 90.0 jit_solution(16927049046519984508)
XLA Ops:
  0.7 1.2 %fusion.73 = (f32[24,16,3]{2,1,0:T(8,128)S(1)}, f32[24,16,3]{2,1,0:T(8,128)S(1)}) fusion(f32[24,16,256]{2,1,0:T(8,128)} %param.14), kind=kLoop, calls=%fused_computation.162 | loop fusion | bytes 18432 | tf_op jit(solution)/shard_map/slice | solution.py:116
  1.9 0.2 copy.57
  2.1 1.1 %fusion.74 = (f32[24,16,3]{2,1,0:T(8,128)S(1)}, f32[24,16,3]{2,1,0:T(8,128)S(1)}) fusion(f32[24,16,256]{2,1,0:T(8,128)} %param.15), kind=kLoop, calls=%fused_computation.163 | loop fusion | bytes 18432 | tf_op jit(solution)/shard_map/slice | solution.py:117
  3.2 0.2 copy.58
  3.4 1.0 %fusion.75 = (f32[4,3,16,3]{3,2,1,0:T(8,128)S(1)}, f32[4,3,16,3]{3,2,1,0:T(8,128)S(1)}) fusion(f32[4,3,16,256]{3,2,1,0:T(8,128)} %param.11), kind=kLoop, calls=%fused_computation.164 | loop fusion | bytes 9216 | tf_op jit(solution)/shard_map/slice | solution.py:115
  4.4 0.2 copy.40
  4.7 0.1 pad_maximum_fusion.8
  4.7 1.9 %collective-permute-start = (f32[60,16,3]{0,1,2:T(8,128)S(1)}, f32[60,16,3]{0,1,2:T(8,128)S(1)}, u32[]{:S(2)}, u32[]{:S(2)}) collective-permute-start(f32[60,16,3]{0,1,2:T(8,128)S(1)} %pad_maximum_fusion.8), channel_id=1, source_target_pairs={{0,1},{1,2},{2,3},{3,4},{4,5},{5,6},{6,7},{7,8},{8,9},{9,10},{10,1... | collective-permute-start | bytes 34568 | tf_op jit(solution)/shard_map/ppermute | solution.py:25
  6.7 0.2 copy.59
  6.8 0.2 copy.60
  7.0 0.2 copy.44
  7.2 0.1 pad_maximum_fusion.9
  7.3 6.6 %collective-permute-start.1 = (f32[60,16,3]{0,1,2:T(8,128)S(1)}, f32[60,16,3]{0,1,2:T(8,128)S(1)}, u32[]{:S(2)}, u32[]{:S(2)}) collective-permute-start(f32[60,16,3]{0,1,2:T(8,128)S(1)} %pad_maximum_fusion.9), channel_id=1, source_target_pairs={{1,0},{2,1},{3,2},{4,3},{5,4},{6,5},{7,6},{8,7},{9,8},{10,9},{11,1... | collective-permute-start | bytes 34568 | tf_op jit(solution)/shard_map/ppermute | solution.py:25
  14.3 0.2 copy.47
  14.5 1.0 %collective-permute-done.1 = f32[60,16,3]{0,1,2:T(8,128)S(1)} collective-permute-done((f32[60,16,3]{0,1,2:T(8,128)S(1)}, f32[60,16,3]{0,1,2:T(8,128)S(1)}, u32[]{:S(2)}, u32[]{:S(2)}) %collective-permute-start.1) | collective-permute-done | bytes 11552 | tf_op jit(solution)/shard_map/ppermute | solution.py:25
  15.5 0.2 copy.48
  15.8 0.2 copy.45
  15.9 0.2 copy.46
  16.2 0.1 select_maximum_fusion
  16.3 3.4 %collective-permute-start.2 = (f32[8,16,262]{2,1,0:T(8,128)S(1)}, f32[8,16,262]{2,1,0:T(8,128)S(1)}, u32[]{:S(2)}, u32[]{:S(2)}) collective-permute-start(f32[8,16,262]{2,1,0:T(8,128)S(1)} %select_maximum_fusion), channel_id=1, source_target_pairs={{0,64},{64,128},{128,192},{192,256},{256,320},{320,384},{384,448},... | collective-permute-start | bytes 402440 | tf_op jit(solution)/shard_map/ppermute | solution.py:25
  19.7 0.1 select_maximum_fusion.3
  19.8 1.3 %collective-permute-start.3 = (f32[7,16,262]{2,1,0:T(8,128)S(1)}, f32[7,16,262]{2,1,0:T(8,128)S(1)}, u32[]{:S(2)}, u32[]{:S(2)}) collective-permute-start(f32[7,16,262]{2,1,0:T(8,128)S(1)} %select_maximum_fusion.3), channel_id=1, source_target_pairs={{64,0},{128,64},{192,128},{256,192},{320,256},{384,320},{448,384},... | collective-permute-start | bytes 352136 | tf_op jit(solution)/shard_map/ppermute | solution.py:25
  21.1 0.1 copy.49
  21.2 0.1 copy.51
  21.4 0.1 copy.50
  21.5 0.1 copy.52
  21.6 0.2 pad_maximum_fusion.5
  21.8 0.6 gather_fusion
  22.4 0.1 broadcast_select_fusion
  22.6 5.7 %collective-permute-done.3 = f32[7,16,262]{2,1,0:T(8,128)S(1)} collective-permute-done((f32[7,16,262]{2,1,0:T(8,128)S(1)}, f32[7,16,262]{2,1,0:T(8,128)S(1)}, u32[]{:S(2)}, u32[]{:S(2)}) %collective-permute-start.3) | collective-permute-done | bytes 117408 | tf_op jit(solution)/shard_map/ppermute | solution.py:25
  28.5 0.1 select_reduce_fusion
  28.6 0.6 bitcast_multiply_fusion
  29.2 0.3 pad_maximum_fusion
  29.5 0.4 add_add_fusion
  30.0 3.9 %divide_multiply_fusion = (f32[4,30,16,262]{3,2,1,0:T(8,128)S(1)}, f32[4,30,16,262]{3,2,1,0:T(8,128)}) fusion(f32[30,262]{1,0:T(8,128)S(1)} %and_convert_fusion, f32[30,16,262]{2,1,0:T(8,128)S(1)} %get-tuple-element.35, f32[30]{0:T(128)S(1)} %get-tuple-element.65, f32[4,16,262]{2,1,0:T(8,128)S(1)} %get-tuple-element.49, f32[30]{0:T(128)S(1)} %get-tuple-element.69, ...), kind=kLoop, calls=%fused_computation.53 | loop fusion | flops 12072960 | bytes 4827688 | tf_op jit(solution)/shard_map/mul | solution.py:195
  33.9 0.8 pad.26
  34.8 7.6 %fusion.33 = f32[4,30,16,262]{3,2,1,0:T(8,128)S(1)} fusion(f32[4,32,16,264]{3,2,1,0:T(8,128)S(1)} %pad.26, f32[30,16,262]{2,1,0:T(8,128)S(1)} %get-tuple-element.36, f32[30,16,262]{2,1,0:T(8,128)S(1)} %get-tuple-element.41, f32[30,16,262]{2,1,0:T(8,128)S(1)} %get-tuple-element.40, f32[30]{0:T(128)S(1)} %get-tuple-element.63, f32[30]{0:T(128)S(1)} %get-tuple-element.67, ...), kind=kLoop, calls=%fused_computation.56 | loop fusion | flops 25152000 | bytes 20349952 | tf_op jit(solution)/shard_map/mul | solution.py:207
  42.4 2.5 %pad.28 = f32[4,32,16,264]{3,2,1,0:T(8,128)} pad(f32[4,30,16,262]{3,2,1,0:T(8,128)S(1)} %fusion.33, f32[]{:T(128)} %constant.107.clone.1), padding=0_0x1_1x0_0x1_1 | pad | bytes 4174852 | tf_op jit(solution)/shard_map/jit(_pad)/pad | solution.py:198
  44.9 20.9 %fusion.32 = f32[4,30,16,262]{3,2,1,0:T(8,128)} fusion(f32[4,32,16,264]{3,2,1,0:T(8,128)} %pad.28, f32[30,16,262]{2,1,0:T(8,128)} %copy-done.6, f32[30,16,262]{2,1,0:T(8,128)} %copy-done.8, f32[30,16,262]{2,1,0:T(8,128)} %copy-done.7, f32[30]{0:T(128)} %copy-done.20, f32[30]{0:T(128)} %copy-done.21, f32[30]{0:T(128)} %copy-done.22, f32[30,262]{1,0:T(8,128)} %copy-done.16, ...), kind=kLoop, calls=%fused_computation.55 | loop fusion | flops 38231040 | bytes 35292160 | tf_op jit(solution)/shard_map/mul | solution.py:207
  65.9 2.6 %slice.370 = f32[4,26,16,258]{3,2,1,0:T(8,128)S(1)} slice(f32[4,30,16,262]{3,2,1,0:T(8,128)} %fusion.32), slice={[0:4], [2:28], [0:16], [2:260]} | slice | bytes 3434496 | tf_op jit(solution)/shard_map/slice | solution.py:99
  68.5 0.8 slice_bitcast_fusion.4
  69.2 1.1 %add_add_fusion.1 = (f32[24,16,256]{2,1,0:T(8,128)S(1)}, f32[24,16,256]{2,1,0:T(8,128)S(1)}) fusion(f32[24,16,256]{2,1,0:T(8,128)S(1)} %copy-done.3, f32[24,16,256]{2,1,0:T(8,128)S(1)} %copy-done.1, f32[24]{0:T(128)S(1)} %get-tuple-element.73, f32[24,16,3]{2,1,0:T(8,128)} %copy-done.10, f32[24,16,3]{2,1,0:T(8,128)} %copy-done.9, f32[4,16,262]{2,1,0:T(8,128)} %copy-done.15), kind=kLoop, calls=%fused_computation.91 | loop fusion | flops 589824 | bytes 1649248 | tf_op jit(solution)/shard_map/add | solution.py:91
  70.3 5.4 %fusion.55 = (f32[16,256]{1,0:T(8,128)S(1)}, f32[24,16,256]{2,1,0:T(8,128)S(1)}, f32[4,24,16,256]{3,2,1,0:T(8,128)}) fusion(f32[4,30,16,262]{3,2,1,0:T(8,128)S(1)} %copy-done.5, f32[24,16,256]{2,1,0:T(8,128)S(1)} %get-tuple-element.31, f32[24,16,256]{2,1,0:T(8,128)S(1)} %copy-done.3, f32[4,30,16,262]{3,2,1,0:T(8,128)S(1)} %copy-done, ...), kind=kLoop, calls=%fused_computation.86 | loop fusion | flops 10907648 | bytes 14710048 | tf_op jit(solution)/shard_map/reduce_sum | solution.py:220
  75.7 0.7 broadcast_in_dim.17
  76.4 6.1 %all-to-all-start = ((f32[8,16,256]{2,1,0:T(8,128)}), f32[8,16,256]{2,1,0:T(8,128)S(1)}, u32[]{:S(2)}, u32[]{:S(2)}) async-start(f32[8,16,256]{2,1,0:T(8,128)} %broadcast_in_dim.17), calls=%async_computation | async-start | bytes 262144 | tf_op jit(solution)/shard_map/all_to_all | solution.py:221
  82.6 6.6 %all-to-all-done = f32[8,16,256]{2,1,0:T(8,128)S(1)} async-done(((f32[8,16,256]{2,1,0:T(8,128)}), f32[8,16,256]{2,1,0:T(8,128)S(1)}, u32[]{:S(2)}, u32[]{:S(2)}) %all-to-all-start) | async-done | bytes 131104 | tf_op jit(solution)/shard_map/all_to_all | solution.py:221
  89.1 0.1 multiply_reduce_fusion
  89.2 0.8 fusion.54
  (74 shorter events, 0.6 us)
Async XLA Ops:
  0.6 15.5 %copy-start.2 = (f32[24,16,256]{2,1,0:T(8,128)S(1)}, f32[24,16,256]{2,1,0:T(8,128)}, u32[]{:S(2)}) copy-start(f32[24,16,256]{2,1,0:T(8,128)} %param.14) | copy-start | bytes 1179652
  0.6 15.5 %copy-start.1 = (f32[24,16,256]{2,1,0:T(8,128)S(1)}, f32[24,16,256]{2,1,0:T(8,128)}, u32[]{:S(2)}) copy-start(f32[24,16,256]{2,1,0:T(8,128)} %param.15) | copy-start | bytes 1179652
  0.7 13.3 %copy-start.26 = (s32[4]{0:T(128)S(1)}, s32[4]{0:T(128)}, u32[]{:S(2)}) copy-start(s32[4]{0:T(128)} %param.12) | copy-start | bytes 52
  0.7 13.4 %copy-start.23 = (s32[24]{0:T(128)S(1)}, s32[24]{0:T(128)}, u32[]{:S(2)}) copy-start(s32[24]{0:T(128)} %param.13) | copy-start | bytes 292
  4.4 17.2 %copy-start.18 = (f32[4,3,16,256]{3,2,1,0:T(8,128)S(1)}, f32[4,3,16,256]{3,2,1,0:T(8,128)}, u32[]{:S(2)}) copy-start(f32[4,3,16,256]{3,2,1,0:T(8,128)} %param.11) | copy-start | bytes 589828
  4.7 9.5 %collective-permute-start = (f32[60,16,3]{0,1,2:T(8,128)S(1)}, f32[60,16,3]{0,1,2:T(8,128)S(1)}, u32[]{:S(2)}, u32[]{:S(2)}) collective-permute-start(f32[60,16,3]{0,1,2:T(8,128)S(1)} %pad_maximum_fusion.8), channel_id=1, source_target_pairs={{0,1},{1,2},{2,3},{3,4},{4,5},{5,6},{6,7},{7,8},{8,9},{9,10},{10,1... | collective-permute-start | bytes 34568 | tf_op jit(solution)/shard_map/ppermute | solution.py:25
  7.3 8.2 %collective-permute-start.1 = (f32[60,16,3]{0,1,2:T(8,128)S(1)}, f32[60,16,3]{0,1,2:T(8,128)S(1)}, u32[]{:S(2)}, u32[]{:S(2)}) collective-permute-start(f32[60,16,3]{0,1,2:T(8,128)S(1)} %pad_maximum_fusion.9), channel_id=1, source_target_pairs={{1,0},{2,1},{3,2},{4,3},{5,4},{6,5},{7,6},{8,7},{9,8},{10,9},{11,1... | collective-permute-start | bytes 34568 | tf_op jit(solution)/shard_map/ppermute | solution.py:25
  14.2 15.8 %copy-start.16 = (f32[30,262]{1,0:T(8,128)}, f32[30,262]{1,0:T(8,128)S(1)}, u32[]{:S(2)}) copy-start(f32[30,262]{1,0:T(8,128)S(1)} %and_convert_fusion) | copy-start | bytes 94324
  14.5 14.7 %copy-start.9 = (f32[24,16,3]{2,1,0:T(8,128)}, f32[24,16,3]{2,1,0:T(8,128)S(1)}, u32[]{:S(2)}) copy-start(f32[24,16,3]{2,1,0:T(8,128)S(1)} %copy.47) | copy-start | bytes 13828
  15.7 13.5 %copy-start.10 = (f32[24,16,3]{2,1,0:T(8,128)}, f32[24,16,3]{2,1,0:T(8,128)S(1)}, u32[]{:S(2)}) copy-start(f32[24,16,3]{2,1,0:T(8,128)S(1)} %copy.48) | copy-start | bytes 13828
  16.2 12.3 %copy-start.24 = (f32[4]{0:T(128)S(1)}, f32[4]{0:T(128)}, u32[]{:S(2)}) copy-start(f32[4]{0:T(128)} %constant.131.clone) | copy-start | bytes 52
  16.2 12.3 %copy-start.25 = (f32[4]{0:T(128)S(1)}, f32[4]{0:T(128)}, u32[]{:S(2)}) copy-start(f32[4]{0:T(128)} %constant.132.clone) | copy-start | bytes 52
  16.3 12.0 %collective-permute-start.2 = (f32[8,16,262]{2,1,0:T(8,128)S(1)}, f32[8,16,262]{2,1,0:T(8,128)S(1)}, u32[]{:S(2)}, u32[]{:S(2)}) collective-permute-start(f32[8,16,262]{2,1,0:T(8,128)S(1)} %select_maximum_fusion), channel_id=1, source_target_pairs={{0,64},{64,128},{128,192},{192,256},{256,320},{320,384},{384,448},... | collective-permute-start | bytes 402440 | tf_op jit(solution)/shard_map/ppermute | solution.py:25
  19.8 8.5 %collective-permute-start.3 = (f32[7,16,262]{2,1,0:T(8,128)S(1)}, f32[7,16,262]{2,1,0:T(8,128)S(1)}, u32[]{:S(2)}, u32[]{:S(2)}) collective-permute-start(f32[7,16,262]{2,1,0:T(8,128)S(1)} %select_maximum_fusion.3), channel_id=1, source_target_pairs={{64,0},{128,64},{192,128},{256,192},{320,256},{384,320},{448,384},... | collective-permute-start | bytes 352136 | tf_op jit(solution)/shard_map/ppermute | solution.py:25
  22.5 12.1 %copy-start.11 = (f32[4,16,262]{2,1,0:T(8,128)}, f32[4,16,262]{2,1,0:T(8,128)S(1)}, u32[]{:S(2)}) copy-start(f32[4,16,262]{2,1,0:T(8,128)S(1)} %get-tuple-element.48) | copy-start | bytes 201220
  22.5 12.1 %copy-start.12 = (f32[4,16,262]{2,1,0:T(8,128)}, f32[4,16,262]{2,1,0:T(8,128)S(1)}, u32[]{:S(2)}) copy-start(f32[4,16,262]{2,1,0:T(8,128)S(1)} %get-tuple-element.49) | copy-start | bytes 201220
  22.6 12.1 %copy-start.13 = (f32[4,16,262]{2,1,0:T(8,128)}, f32[4,16,262]{2,1,0:T(8,128)S(1)}, u32[]{:S(2)}) copy-start(f32[4,16,262]{2,1,0:T(8,128)S(1)} %get-tuple-element.50) | copy-start | bytes 201220
  22.6 12.1 %copy-start.14 = (f32[4,16,262]{2,1,0:T(8,128)}, f32[4,16,262]{2,1,0:T(8,128)S(1)}, u32[]{:S(2)}) copy-start(f32[4,16,262]{2,1,0:T(8,128)S(1)} %get-tuple-element.51) | copy-start | bytes 201220
  28.6 6.2 %copy-start.19 = (f32[30]{0:T(128)}, f32[30]{0:T(128)S(1)}, u32[]{:S(2)}) copy-start(f32[30]{0:T(128)S(1)} %get-tuple-element.71) | copy-start | bytes 364
  28.6 6.2 %copy-start.20 = (f32[30]{0:T(128)}, f32[30]{0:T(128)S(1)}, u32[]{:S(2)}) copy-start(f32[30]{0:T(128)S(1)} %get-tuple-element.63) | copy-start | bytes 364
  28.6 6.2 %copy-start.21 = (f32[30]{0:T(128)}, f32[30]{0:T(128)S(1)}, u32[]{:S(2)}) copy-start(f32[30]{0:T(128)S(1)} %get-tuple-element.67) | copy-start | bytes 364
  28.6 6.2 %copy-start.22 = (f32[30]{0:T(128)}, f32[30]{0:T(128)S(1)}, u32[]{:S(2)}) copy-start(f32[30]{0:T(128)S(1)} %get-tuple-element.68) | copy-start | bytes 364
  29.2 0.7 copy-start.15
  29.9 4.9 %copy-start.4 = (f32[30,16,262]{2,1,0:T(8,128)}, f32[30,16,262]{2,1,0:T(8,128)S(1)}, u32[]{:S(2)}) copy-start(f32[30,16,262]{2,1,0:T(8,128)S(1)} %get-tuple-element.35) | copy-start | bytes 1509124
  29.9 4.9 %copy-start.6 = (f32[30,16,262]{2,1,0:T(8,128)}, f32[30,16,262]{2,1,0:T(8,128)S(1)}, u32[]{:S(2)}) copy-start(f32[30,16,262]{2,1,0:T(8,128)S(1)} %get-tuple-element.36) | copy-start | bytes 1509124
  29.9 4.9 %copy-start.7 = (f32[30,16,262]{2,1,0:T(8,128)}, f32[30,16,262]{2,1,0:T(8,128)S(1)}, u32[]{:S(2)}) copy-start(f32[30,16,262]{2,1,0:T(8,128)S(1)} %get-tuple-element.40) | copy-start | bytes 1509124
  29.9 4.9 %copy-start.8 = (f32[30,16,262]{2,1,0:T(8,128)}, f32[30,16,262]{2,1,0:T(8,128)S(1)}, u32[]{:S(2)}) copy-start(f32[30,16,262]{2,1,0:T(8,128)S(1)} %get-tuple-element.41) | copy-start | bytes 1509124
  33.9 0.9 %copy-start.17 = (f32[30,262]{1,0:T(8,128)S(1)}, f32[30,262]{1,0:T(8,128)}, u32[]{:S(2)}) copy-start(f32[30,262]{1,0:T(8,128)} %copy-done.16) | copy-start | bytes 94324
  65.8 3.4 %copy-start.3 = (f32[24,16,256]{2,1,0:T(8,128)S(1)}, f32[24,16,256]{2,1,0:T(8,128)}, u32[]{:S(2)}) copy-start(f32[24,16,256]{2,1,0:T(8,128)} %param.14) | copy-start | bytes 1179652
  65.8 4.5 %copy-start = (f32[4,30,16,262]{3,2,1,0:T(8,128)S(1)}, f32[4,30,16,262]{3,2,1,0:T(8,128)}, u32[]{:S(2)}) copy-start(f32[4,30,16,262]{3,2,1,0:T(8,128)} %fusion.32) | copy-start | bytes 6036484
  65.9 4.5 %copy-start.5 = (f32[4,30,16,262]{3,2,1,0:T(8,128)S(1)}, f32[4,30,16,262]{3,2,1,0:T(8,128)}, u32[]{:S(2)}) copy-start(f32[4,30,16,262]{3,2,1,0:T(8,128)} %get-tuple-element.43) | copy-start | bytes 6036484
  76.4 12.7 %all-to-all-start = ((f32[8,16,256]{2,1,0:T(8,128)}), f32[8,16,256]{2,1,0:T(8,128)S(1)}, u32[]{:S(2)}, u32[]{:S(2)}) async-start(f32[8,16,256]{2,1,0:T(8,128)} %broadcast_in_dim.17), calls=%async_computation | async-start | bytes 262144 | tf_op jit(solution)/shard_map/all_to_all | solution.py:221

commit v11 on v8

--- a/solution.py
+++ b/solution.py
@@ -134,7 +134,7 @@
         a_s[p] = forced * (ply_mask[p] * col_mask)
         return carry
 
-    lax.fori_loop(0, planes, first, 0)
+    lax.fori_loop(0, planes, first, 0, unroll=2)
     buffers = (a_s, b_s)
     for iteration in range(1, ITERS):
         previous, following = buffers[(iteration - 1) % 2], buffers[iteration % 2]
@@ -163,20 +163,14 @@
                 + down_s[p] * previous[p - 1]
             )
             if masked:
-                value = value * (ply_mask[p] * col_mask)
-            following[p] = value
+                following[p] = value * (ply_mask[p] * col_mask)
+            else:
+                value = value[:, :own_cols]
+                adj_ref[0, p - halo] = value
+                acc_ref[p - halo] = acc_ref[p - halo] + value * src_s[p][:, :own_cols]
             return carry
 
         lax.fori_loop(iteration, planes - iteration, step, 0, unroll=2)
-    final = buffers[(ITERS - 1) % 2]
-
-    def store(p, carry):
-        value = final[p + halo][:, :own_cols]
-        adj_ref[0, p] = value
-        acc_ref[p] = acc_ref[p] + value * src_s[p + halo][:, :own_cols]
-        return carry
-
-    lax.fori_loop(0, own_planes, store, 0)
 
 
 def trim(array, by, ply_dim, col_dim):
@@ -193,20 +187,31 @@
     ply_count = lax.axis_size("ply")
     tile_count = lax.axis_size("tile")
     cases = case_ids.shape[0]
-    chosen = jnp.take(strain, case_ids, axis=0)
-    rows = chosen.shape[2]
-
+    rows = strain.shape[2]
     lanes = -(-(col_local + 2 * halo) // 128) * 128
-    flat = jnp.concatenate(
-        [chosen.reshape(cases * 3, rows, col_local), stiffening, interface], axis=0
-    )
-    left = passed_along(flat[..., col_local - halo :], "tile", 1)
-    right = passed_along(flat[..., :halo], "tile", -1)
-    gap = jnp.zeros(flat.shape[:2] + (lanes - col_local - 2 * halo,), jnp.float32)
-    packed = jnp.concatenate([flat, right, gap, left], axis=2)
-    strain_e = packed[: cases * 3].reshape(cases, 3, rows, lanes)
-    stiff_c = packed[cases * 3 : cases * 3 + ply_local]
-    inter_c = packed[cases * 3 + ply_local :]
+
+    def edge(start):
+        return jnp.concatenate(
+            [
+                lax.slice_in_dim(strain, start, start + halo, axis=3).reshape(-1, rows, halo),
+                lax.slice_in_dim(stiffening, start, start + halo, axis=2),
+                lax.slice_in_dim(interface, start, start + halo, axis=2),
+            ],
+            axis=0,
+        )
+
+    left = passed_along(edge(col_local - halo), "tile", 1)
+    right = passed_along(edge(0), "tile", -1)
+    states = strain.shape[0] * 3
+
+    def circular(own, first, last):
+        gap = jnp.zeros(own.shape[:-1] + (lanes - col_local - 2 * halo,), jnp.float32)
+        return jnp.concatenate([own, right[first:last].reshape(own.shape[:-1] + (halo,)), gap,
+                                left[first:last].reshape(own.shape[:-1] + (halo,))], axis=-1)
+
+    strain_e = jnp.take(circular(strain, 0, states), case_ids, axis=0)
+    stiff_c = circular(stiffening, states, states + ply_local)
+    inter_c = circular(interface, states + ply_local, states + 2 * ply_local)
     angle_plane = jnp.zeros((1, rows, lanes), jnp.float32)
     below = passed_along(
         jnp.concatenate(

time: 92.9 us -> 88.6 us (0.954)
  waiting for transfers between devices: 24.7 us -> 19 us
  local copies, waits for them, and re-layouts: 3.77 us -> 6.05 us
  Pallas kernels: 33.1 us -> 31.5 us
  starting transfers between devices: 21.6 us -> 22.7 us
    ppermute x4, waiting for transfers between devices: 18.1 us -> 12.5 us  [passed_along(): return lax.ppermute(array, axis, pairs)]
    pallas_call x1, Pallas kernels: 33.1 us -> 31.5 us  [body(): pl.pallas_call(sweeps_kernel, grid=(cases,), in_specs=[pl.BlockSpec(memor...]
    slice x3 -> x7, local copies, waits for them, and re-layouts: 1 us -> 2.5 us  [the longest x1 1.4 us: edge(): lax.slice_in_dim(stiffening, start, start + halo, axis=2)]
    ppermute x4, starting transfers between devices: 13.5 us -> 14.7 us  [passed_along(): return lax.ppermute(array, axis, pairs)]
    concatenate x2 -> x4, other arithmetic: 1.41 us -> 0.4 us  [the longest x2 0.33 us: circular(): jnp.concatenate([own, right[first:last].reshape(own.shape[:-1] + (halo,))...]
  transfers between devices with their start and end apart: 5 -> 5, of which waited for: 5 -> 4; matrix products, arithmetic and copies ran while one was open for 1% -> 4% of each run, Pallas kernels for 0% -> 0%
where the time goes in v11:
time: 88.6 us; the launch traced here: 88.1 us
  Pallas kernels  31.5 us (36%)
  starting transfers between devices  22.7 us (26%)
  waiting for transfers between devices  19 us (21%)
  other arithmetic  7.77 us (9%)
  local copies, waits for them, and re-layouts  6.05 us (7%)
  between operations  0.93 us (1%)
    pallas_call x1, Pallas kernels, body(): pl.pallas_call(sweeps_kernel, grid=(cases,), in_specs=[pl.BlockSpec(memor...  31.5 us
    ppermute x4, starting transfers between devices, passed_along(): return lax.ppermute(array, axis, pairs)  14.7 us
    ppermute x4, waiting for transfers between devices, passed_along(): return lax.ppermute(array, axis, pairs)  12.5 us
    all_to_all x1, starting transfers between devices, body(): lax.all_to_all(jnp.broadcast_to(total[None], (ply_count,) + total.shape),...  8.06 us
    all_to_all x1, waiting for transfers between devices, body(): lax.all_to_all(jnp.broadcast_to(total[None], (ply_count,) + total.shape),...  6.57 us
    another operation x1, other arithmetic, body(): running = jnp.cumsum(summed, axis=0)  1.8 us
  transfers between devices with their start and end apart: 5, of which 4 were waited for; matrix products, arithmetic and copies ran while one was open for 4% of the time, Pallas kernels for 0%

profile of v11, /device:TPU:448, one launch (start us, length us, event | category | flops | bytes accessed | tf_op | source)
XLA Modules:
  0.0 88.1 jit_solution(3389844294869371254)
XLA Ops:
  0.6 1.0 %fusion.19 = (f32[4,3,16,3]{3,2,1,0:T(8,128)S(1)}, f32[4,3,16,3]{3,2,1,0:T(8,128)S(1)}) fusion(f32[4,3,16,256]{3,2,1,0:T(8,128)} %param.11), kind=kLoop, calls=%fused_computation.53 | loop fusion | bytes 9216 | tf_op jit(solution)/shard_map/slice | solution.py:196
  1.7 0.0 copy-start.6
  1.7 0.0 copy-start.3
  1.7 1.4 %fusion.17 = (f32[24,16,3]{2,1,0:T(8,128)S(1)}, f32[24,16,3]{2,1,0:T(8,128)S(1)}, f32[24,16,3]{2,1,0:T(8,128)S(1)}, f32[24,16,3]{2,1,0:T(8,128)S(1)}) fusion(f32[24,16,256]{2,1,0:T(8,128)} %param.14, f32[24,16,256]{2,1,0:T(8,128)} %param.15), kind=kLoop, calls=%fused_computation.51 | loop fusion | bytes 36864 | tf_op jit(solution)/shard_map/slice | solution.py:197
  3.1 0.0 copy-start
  3.1 0.0 copy-start.1
  3.1 2.1 %collective-permute-start.1 = (f32[60,16,3]{2,1,0:T(8,128)S(1)}, f32[60,16,3]{2,1,0:T(8,128)S(1)}, u32[]{:S(2)}, u32[]{:S(2)}) collective-permute-start(f32[60,16,3]{2,1,0:T(8,128)S(1)} %pad_maximum_fusion.5), channel_id=1, source_target_pairs={{0,1},{1,2},{2,3},{3,4},{4,5},{5,6},{6,7},{7,8},{8,9},{9,10},{10,1... | collective-permute-start | bytes 34568 | tf_op jit(solution)/shard_map/ppermute | solution.py:27
  5.3 6.7 %collective-permute-start = (f32[60,16,3]{2,1,0:T(8,128)S(1)}, f32[60,16,3]{2,1,0:T(8,128)S(1)}, u32[]{:S(2)}, u32[]{:S(2)}) collective-permute-start(f32[60,16,3]{2,1,0:T(8,128)S(1)} %pad_maximum_fusion.4), channel_id=1, source_target_pairs={{1,0},{2,1},{3,2},{4,3},{5,4},{6,5},{7,6},{8,7},{9,8},{10,9},{11,1... | collective-permute-start | bytes 34568 | tf_op jit(solution)/shard_map/ppermute | solution.py:27
  11.9 0.0 copy-done.6
  12.0 0.0 copy-done.3
  12.0 0.1 convert_bitcast_fusion.1
  12.1 0.5 and_convert_fusion.ply_mask
  12.6 0.1 pad.22.clone
  12.7 6.5 %collective-permute-done.1 = f32[60,16,3]{2,1,0:T(8,128)S(1)} collective-permute-done((f32[60,16,3]{2,1,0:T(8,128)S(1)}, f32[60,16,3]{2,1,0:T(8,128)S(1)}, u32[]{:S(2)}, u32[]{:S(2)}) %collective-permute-start.1) | collective-permute-done | bytes 11552 | tf_op jit(solution)/shard_map/ppermute | solution.py:27
  19.2 4.3 %collective-permute-done = f32[60,16,3]{2,1,0:T(8,128)S(1)} collective-permute-done((f32[60,16,3]{2,1,0:T(8,128)S(1)}, f32[60,16,3]{2,1,0:T(8,128)S(1)}, u32[]{:S(2)}, u32[]{:S(2)}) %collective-permute-start) | collective-permute-done | bytes 11552 | tf_op jit(solution)/shard_map/ppermute | solution.py:27
  23.6 0.0 copy-done
  23.6 0.0 copy-done.1
  23.6 0.2 fusion.1
  23.8 0.0 copy-start.2
  23.9 0.0 copy-start.4
  23.9 0.0 copy-start.5
  23.9 1.4 %collective-permute-start.3 = (f32[7,16,384]{2,1,0:T(8,128)S(1)}, f32[7,16,384]{2,1,0:T(8,128)}, u32[]{:S(2)}, u32[]{:S(2)}) collective-permute-start(f32[7,16,384]{2,1,0:T(8,128)S(1)} %select_maximum_fusion.1), channel_id=1, source_target_pairs={{64,0},{128,64},{192,128},{256,192},{320,256},{384,320},{448,384},... | collective-permute-start | bytes 516104 | tf_op jit(solution)/shard_map/ppermute | solution.py:27
  25.4 4.6 %collective-permute-start.2 = (f32[8,16,384]{2,1,0:T(8,128)S(1)}, f32[8,16,384]{2,1,0:T(8,128)S(1)}, u32[]{:S(2)}, u32[]{:S(2)}) collective-permute-start(f32[8,16,384]{2,1,0:T(8,128)S(1)} %select_maximum_fusion), channel_id=1, source_target_pairs={{0,64},{64,128},{128,192},{192,256},{256,320},{320,384},{384,448},... | collective-permute-start | bytes 589832 | tf_op jit(solution)/shard_map/ppermute | solution.py:27
  30.0 0.0 copy-done.2
  30.0 0.1 pad_maximum_fusion.6
  30.1 0.6 gather_fusion
  30.7 0.8 broadcast_select_fusion.strain_ref
  31.5 1.7 %collective-permute-done.3 = f32[7,16,384]{2,1,0:T(8,128)} collective-permute-done((f32[7,16,384]{2,1,0:T(8,128)S(1)}, f32[7,16,384]{2,1,0:T(8,128)}, u32[]{:S(2)}, u32[]{:S(2)}) %collective-permute-start.3) | collective-permute-done | bytes 172064 | tf_op jit(solution)/shard_map/ppermute | solution.py:27
  33.2 0.9 %fusion.20 = (f32[3,16,384]{2,1,0:T(8,128)S(1)}, f32[3,16,384]{2,1,0:T(8,128)S(1)}) fusion(f32[7,16,384]{2,1,0:T(8,128)} %collective-permute-done.3), kind=kLoop, calls=%fused_computation.54 | loop fusion | bytes 294912 | tf_op jit(solution)/shard_map/slice | solution.py:248
  34.1 0.7 fusion.12
  34.8 0.0 collective-permute-done.2
  34.8 0.1 pad_add_fusion
  34.9 0.0 copy-done.4
  34.9 0.0 copy-done.5
  34.9 0.1 select_reduce_fusion.1
  35.0 1.1 %pad_maximum_fusion.2.inter_ref = f32[31,16,384]{2,1,0:T(8,128)} fusion(f32[3,16,384]{2,1,0:T(8,128)S(1)} %get-tuple-element.46, f32[24,16,3]{2,1,0:T(8,128)S(1)} %get-tuple-element.37, f32[24,16,122]{2,1,0:T(8,128)S(1)} %broadcast.141, f32[24,16,3]{2,1,0:T(8,128)S(1)} %get-tuple-element.35, f32[24,16,256]{2,1,0:T(8,128)S(1)} %copy-done.1, ...), kind=kLoop, calls=%fused_computation.5 | loop fusion | flops 952320 | bytes 1523712 | tf_op jit(solution)/shard_map/concatenate | solution.py:248
  36.0 1.1 %pad_maximum_fusion.3.stiff_ref = f32[30,16,384]{2,1,0:T(8,128)} fusion(f32[3,16,384]{2,1,0:T(8,128)S(1)} %get-tuple-element.47, f32[24,16,3]{2,1,0:T(8,128)S(1)} %get-tuple-element.36, f32[24,16,122]{2,1,0:T(8,128)S(1)} %broadcast.141, f32[24,16,3]{2,1,0:T(8,128)S(1)} %get-tuple-element.34, f32[24,16,256]{2,1,0:T(8,128)S(1)} %copy-done, ...), kind=kLoop, calls=%fused_computation.6 | loop fusion | flops 921600 | bytes 1474560 | tf_op jit(solution)/shard_map/concatenate | solution.py:247
  37.1 0.6 stack.3.tab
  37.7 0.6 broadcast_in_dim.38.col_mask_ref
  38.3 31.5 %shard_map.86 = (f32[4,24,16,256]{3,2,1,0:T(8,128)}, f32[24,16,256]{2,1,0:T(8,128)}) custom-call(f32[5,30]{1,0:T(8,128)} %stack.3.tab, f32[30]{0:T(128)} %and_convert_fusion.ply_mask, f32[4,3,16,384]{3,2,1,0:T(8,128)} %broadcast_select_fusion.strain_ref, f32[30,16,384]{2,1,0:T(8,128)} %pad_maximum_fusion.3.stiff_ref, ...), custom_call_target="tpu_custom_call" | custom-call | tf_op jit(solution)/shard_map/pallas_call | solution.py:263
  69.8 1.0 %reduce_sum.44 = f32[16,256]{1,0:T(8,128)S(1)} reduce(f32[24,16,256]{2,1,0:T(8,128)} %get-tuple-element.29, f32[]{:T(128)} %constant.94.clone.1), dimensions={0}, to_apply=%region_3.4 | reduce | flops 94208 | bytes 409604 | tf_op jit(solution)/shard_map/reduce_sum | solution.py:285
  70.9 0.7 broadcast_in_dim.39
  71.5 8.1 %all-to-all-start = ((f32[8,16,256]{2,1,0:T(8,128)}), f32[8,16,256]{2,1,0:T(8,128)S(1)}, u32[]{:S(2)}, u32[]{:S(2)}) async-start(f32[8,16,256]{2,1,0:T(8,128)} %broadcast_in_dim.39), calls=%async_computation | async-start | bytes 262144 | tf_op jit(solution)/shard_map/all_to_all | solution.py:286
  79.6 6.6 %all-to-all-done = f32[8,16,256]{2,1,0:T(8,128)S(1)} async-done(((f32[8,16,256]{2,1,0:T(8,128)}), f32[8,16,256]{2,1,0:T(8,128)S(1)}, u32[]{:S(2)}, u32[]{:S(2)}) %all-to-all-start) | async-done | bytes 131104 | tf_op jit(solution)/shard_map/all_to_all | solution.py:286
  86.2 0.1 multiply_reduce_fusion
  86.3 1.8 %fusion = f32[24,16,256]{2,1,0:T(8,128)} fusion(f32[24,16,256]{2,1,0:T(8,128)} %get-tuple-element.29, f32[16,256]{1,0:T(8,128)S(1)} %multiply_reduce_fusion), kind=kOutput, calls=%fused_computation.2 | output fusion | flops 2457600 | bytes 802816 | tf_op jit(solution)/shard_map/jit(cumsum)/reduce_window_sum | solution.py:291
  (22 shorter events, 0.3 us)
Async XLA Ops:
  1.7 10.3 %copy-start.6 = (s32[4]{0:T(128)S(1)}, s32[4]{0:T(128)}, u32[]{:S(2)}) copy-start(s32[4]{0:T(128)} %param.12) | copy-start | bytes 52
  1.7 10.3 %copy-start.3 = (s32[24]{0:T(128)S(1)}, s32[24]{0:T(128)}, u32[]{:S(2)}) copy-start(s32[24]{0:T(128)} %param.13) | copy-start | bytes 292
  3.1 20.4 %copy-start = (f32[24,16,256]{2,1,0:T(8,128)S(1)}, f32[24,16,256]{2,1,0:T(8,128)}, u32[]{:S(2)}) copy-start(f32[24,16,256]{2,1,0:T(8,128)} %param.14) | copy-start | bytes 1179652
  3.1 20.4 %copy-start.1 = (f32[24,16,256]{2,1,0:T(8,128)S(1)}, f32[24,16,256]{2,1,0:T(8,128)}, u32[]{:S(2)}) copy-start(f32[24,16,256]{2,1,0:T(8,128)} %param.15) | copy-start | bytes 1179652
  3.1 16.0 %collective-permute-start.1 = (f32[60,16,3]{2,1,0:T(8,128)S(1)}, f32[60,16,3]{2,1,0:T(8,128)S(1)}, u32[]{:S(2)}, u32[]{:S(2)}) collective-permute-start(f32[60,16,3]{2,1,0:T(8,128)S(1)} %pad_maximum_fusion.5), channel_id=1, source_target_pairs={{0,1},{1,2},{2,3},{3,4},{4,5},{5,6},{6,7},{7,8},{8,9},{9,10},{10,1... | collective-permute-start | bytes 34568 | tf_op jit(solution)/shard_map/ppermute | solution.py:27
  5.3 18.3 %collective-permute-start = (f32[60,16,3]{2,1,0:T(8,128)S(1)}, f32[60,16,3]{2,1,0:T(8,128)S(1)}, u32[]{:S(2)}, u32[]{:S(2)}) collective-permute-start(f32[60,16,3]{2,1,0:T(8,128)S(1)} %pad_maximum_fusion.4), channel_id=1, source_target_pairs={{1,0},{2,1},{3,2},{4,3},{5,4},{6,5},{7,6},{8,7},{9,8},{10,9},{11,1... | collective-permute-start | bytes 34568 | tf_op jit(solution)/shard_map/ppermute | solution.py:27
  23.8 6.2 %copy-start.2 = (f32[4,3,16,256]{3,2,1,0:T(8,128)S(1)}, f32[4,3,16,256]{3,2,1,0:T(8,128)}, u32[]{:S(2)}) copy-start(f32[4,3,16,256]{3,2,1,0:T(8,128)} %param.11) | copy-start | bytes 589828
  23.9 11.0 %copy-start.4 = (f32[4]{0:T(128)S(1)}, f32[4]{0:T(128)}, u32[]{:S(2)}) copy-start(f32[4]{0:T(128)} %constant.114.clone) | copy-start | bytes 52
  23.9 11.0 %copy-start.5 = (f32[4]{0:T(128)S(1)}, f32[4]{0:T(128)}, u32[]{:S(2)}) copy-start(f32[4]{0:T(128)} %constant.113.clone) | copy-start | bytes 52
  23.9 9.2 %collective-permute-start.3 = (f32[7,16,384]{2,1,0:T(8,128)S(1)}, f32[7,16,384]{2,1,0:T(8,128)}, u32[]{:S(2)}, u32[]{:S(2)}) collective-permute-start(f32[7,16,384]{2,1,0:T(8,128)S(1)} %select_maximum_fusion.1), channel_id=1, source_target_pairs={{64,0},{128,64},{192,128},{256,192},{320,256},{384,320},{448,384},... | collective-permute-start | bytes 516104 | tf_op jit(solution)/shard_map/ppermute | solution.py:27
  25.4 9.4 %collective-permute-start.2 = (f32[8,16,384]{2,1,0:T(8,128)S(1)}, f32[8,16,384]{2,1,0:T(8,128)S(1)}, u32[]{:S(2)}, u32[]{:S(2)}) collective-permute-start(f32[8,16,384]{2,1,0:T(8,128)S(1)} %select_maximum_fusion), channel_id=1, source_target_pairs={{0,64},{64,128},{128,192},{192,256},{256,320},{320,384},{384,448},... | collective-permute-start | bytes 589832 | tf_op jit(solution)/shard_map/ppermute | solution.py:27
  71.5 14.6 %all-to-all-start = ((f32[8,16,256]{2,1,0:T(8,128)}), f32[8,16,256]{2,1,0:T(8,128)S(1)}, u32[]{:S(2)}, u32[]{:S(2)}) async-start(f32[8,16,256]{2,1,0:T(8,128)} %broadcast_in_dim.39), calls=%async_computation | async-start | bytes 262144 | tf_op jit(solution)/shard_map/all_to_all | solution.py:286

commit v12 on v5

--- a/solution.py
+++ b/solution.py
@@ -106,23 +106,15 @@
     ply_count = lax.axis_size("ply")
     tile_count = lax.axis_size("tile")
     cases = case_ids.shape[0]
-    chosen = jnp.take(strain, case_ids, axis=0)
-    rows = chosen.shape[2]
-
-    packed = jnp.concatenate(
-        [chosen.reshape(cases * 3, rows, col_local), stiffening, interface], axis=0
-    )
-    packed = with_halos(packed, "tile", 2, halo, halo)
+    rows = strain.shape[2]
     width = col_local + 2 * halo
-    strain_e = packed[: cases * 3].reshape(cases, 3, rows, width)
-    stiff_c = packed[cases * 3 : cases * 3 + ply_local]
-    inter_c = packed[cases * 3 + ply_local :]
-    angle_plane = jnp.zeros((1, rows, width), jnp.float32)
+
+    angle_plane = jnp.zeros((1, rows, col_local), jnp.float32)
     below = passed_along(
         jnp.concatenate(
             [
-                stiff_c[ply_local - halo :],
-                inter_c[ply_local - halo - 1 :],
+                stiffening[ply_local - halo :],
+                interface[ply_local - halo - 1 :],
                 angle_plane.at[0, 0, :halo].set(angle_ids[ply_local - halo :].astype(jnp.float32)),
             ],
             axis=0,
@@ -133,8 +125,8 @@
     above = passed_along(
         jnp.concatenate(
             [
-                stiff_c[:halo],
-                inter_c[:halo],
+                stiffening[:halo],
+                interface[:halo],
                 angle_plane.at[0, 0, :halo].set(angle_ids[:halo].astype(jnp.float32)),
             ],
             axis=0,
@@ -149,10 +141,34 @@
             above[2 * halo, 0, :halo].astype(jnp.int32),
         ]
     )
-    below = below[: 2 * halo + 1]
-    above = above[: 2 * halo]
-    stiff_e = jnp.concatenate([below[:halo], stiff_c, above[:halo]], axis=0)
-    inter_all = jnp.concatenate([below[halo:], inter_c, above[halo:]], axis=0)
+    stiff_p = jnp.concatenate([below[:halo], stiffening, above[:halo]], axis=0)
+    inter_p = jnp.concatenate([below[halo : 2 * halo + 1], interface, above[halo : 2 * halo]], axis=0)
+
+    def edge(start):
+        return jnp.concatenate(
+            [
+                lax.slice_in_dim(strain, start, start + halo, axis=3).reshape(-1, rows, halo),
+                lax.slice_in_dim(stiff_p, start, start + halo, axis=2),
+                lax.slice_in_dim(inter_p, start, start + halo, axis=2),
+            ],
+            axis=0,
+        )
+
+    left = passed_along(edge(col_local - halo), "tile", 1)
+    right = passed_along(edge(0), "tile", -1)
+    states = strain.shape[0] * 3
+    strain_all = jnp.concatenate(
+        [
+            left[:states].reshape(strain.shape[:3] + (halo,)),
+            strain,
+            right[:states].reshape(strain.shape[:3] + (halo,)),
+        ],
+        axis=3,
+    )
+    strain_e = jnp.take(strain_all, case_ids, axis=0)
+    split = states + stiff_p.shape[0]
+    stiff_e = jnp.concatenate([left[states:split], stiff_p, right[states:split]], axis=2)
+    inter_all = jnp.concatenate([left[split:], inter_p, right[split:]], axis=2)
     up_e = inter_all[1:]
     down_e = inter_all[:-1]
 

time: 85.1 us -> 81 us (0.952)
  the two profiles are of different devices: /device:TPU:448 before, /device:TPU:249 now
where the time goes in v12:
time: 81 us; the launch traced here: 80.5 us
  other arithmetic  40.9 us (50%)
  starting transfers between devices  19.6 us (24%)
  waiting for transfers between devices  9.96 us (12%)
  local copies, waits for them, and re-layouts  8.9 us (11%)
  between operations  1.03 us (1%)
    mul x2, other arithmetic, body(): adjoint = adjoint * trim(inside, by, 0, 2)  17.2 us
    ppermute x4, starting transfers between devices, passed_along(): return lax.ppermute(array, axis, pairs)  15.9 us
    ppermute x4, waiting for transfers between devices, passed_along(): return lax.ppermute(array, axis, pairs)  5.59 us
    reduce_sum x1, other arithmetic, body(): total = jnp.sum(product, axis=(0, 1))  5.03 us
    all_to_all x1, waiting for transfers between devices, body(): lax.all_to_all(jnp.broadcast_to(total[None], (ply_count,) + total.shape),...  4.37 us
    mul x1, other arithmetic, body(): adjoint = relaxation * source_e / diagonal_sum * inside  3.89 us
    all_to_all x1, starting transfers between devices, body(): lax.all_to_all(jnp.broadcast_to(total[None], (ply_count,) + total.shape),...  3.77 us
    slice x2, other arithmetic, trim(): return lax.slice_in_dim(array, by, array.shape[col_dim] - by, axis=col_dim)  3.77 us
  transfers between devices with their start and end apart: 5, of which 2 were waited for; matrix products, arithmetic and copies ran while one was open for 9% of the time, Pallas kernels for 0%

profile of v12, /device:TPU:249, one launch (start us, length us, event | category | flops | bytes accessed | tf_op | source)
XLA Modules:
  0.0 80.5 jit_solution(217609922214192760)
XLA Ops:
  0.6 0.9 %fusion.82 = (f32[3,16,256]{2,1,0:T(8,128)S(1)}, f32[3,16,256]{2,1,0:T(8,128)S(1)}) fusion(f32[24,16,256]{2,1,0:T(8,128)} %param.14), kind=kLoop, calls=%fused_computation.178 | loop fusion | bytes 196608 | tf_op jit(solution)/shard_map/slice | solution.py:116
  1.5 0.8 convert_bitcast_fusion.1
  2.3 0.8 %slice.349 = f32[4,16,256]{2,1,0:T(8,128)S(1)} slice(f32[24,16,256]{2,1,0:T(8,128)} %param.15), slice={[20:24], [0:16], [0:256]} | slice | bytes 131072 | tf_op jit(solution)/shard_map/slice | solution.py:117
  3.2 3.1 %collective-permute-start = (f32[8,16,256]{2,1,0:T(8,128)S(1)}, f32[8,16,256]{2,1,0:T(8,128)S(1)}, u32[]{:S(2)}, u32[]{:S(2)}) collective-permute-start(f32[8,16,256]{2,1,0:T(8,128)S(1)} %select_maximum_fusion), channel_id=1, source_target_pairs={{0,64},{64,128},{128,192},{192,256},{256,320},{320,384},{384,448},... | collective-permute-start | bytes 393224 | tf_op jit(solution)/shard_map/ppermute | solution.py:25
  6.3 0.8 %slice.353 = f32[3,16,256]{2,1,0:T(8,128)S(1)} slice(f32[24,16,256]{2,1,0:T(8,128)} %param.15), slice={[0:3], [0:16], [0:256]} | slice | bytes 98304 | tf_op jit(solution)/shard_map/slice | solution.py:129
  7.1 4.3 %collective-permute-start.1 = (f32[7,16,256]{2,1,0:T(8,128)S(1)}, f32[7,16,256]{2,1,0:T(8,128)S(1)}, u32[]{:S(2)}, u32[]{:S(2)}) collective-permute-start(f32[7,16,256]{2,1,0:T(8,128)S(1)} %select_maximum_fusion.1), channel_id=1, source_target_pairs={{64,0},{128,64},{192,128},{256,192},{320,256},{384,320},{448,384},... | collective-permute-start | bytes 344072 | tf_op jit(solution)/shard_map/ppermute | solution.py:25
  11.4 0.7 and_convert_fusion.1
  12.3 0.7 slice_bitcast_fusion.3
  13.0 1.0 %fusion.83 = (f32[4,3,16,3]{3,2,1,0:T(8,128)S(1)}, f32[4,3,16,3]{3,2,1,0:T(8,128)S(1)}) fusion(f32[4,3,16,256]{3,2,1,0:T(8,128)} %param.11), kind=kLoop, calls=%fused_computation.179 | loop fusion | bytes 9216 | tf_op jit(solution)/shard_map/slice | solution.py:150
  14.0 0.7 compare_select_fusion
  14.7 0.7 compare_and_fusion.1
  15.3 0.2 copy.74
  15.6 0.2 copy.79
  15.8 0.7 pad_add_fusion
  16.6 0.8 select_reduce_fusion.1
  17.3 0.6 fusion.76
  17.9 0.7 slice_bitcast_fusion.10
  18.6 0.7 slice_bitcast_fusion.6
  19.3 1.1 %pad_maximum_fusion.2 = f32[31,16,256]{2,1,0:T(8,128)S(1)} fusion(f32[3,16,256]{2,1,0:T(8,128)S(1)} %get-tuple-element.60, f32[24,16,256]{2,1,0:T(8,128)} %param.15, f32[4,16,256]{2,1,0:T(8,128)S(1)} %slice.438), kind=kLoop, calls=%fused_computation.106 | loop fusion | flops 253952 | bytes 1015808 | tf_op jit(solution)/shard_map/concatenate | solution.py:145
  20.5 0.2 copy.76
  20.9 0.2 copy.75
  21.2 6.5 %collective-permute-start.2 = (f32[73,16,3]{0,1,2:T(8,128)S(1)}, f32[73,16,3]{0,1,2:T(8,128)S(1)}, u32[]{:S(2)}, u32[]{:S(2)}) collective-permute-start(f32[73,16,3]{0,1,2:T(8,128)S(1)} %pad_maximum_fusion.6), channel_id=1, source_target_pairs={{0,1},{1,2},{2,3},{3,4},{4,5},{5,6},{6,7},{7,8},{8,9},{9,10},{10,1... | collective-permute-start | bytes 42056 | tf_op jit(solution)/shard_map/ppermute | solution.py:25
  27.8 0.2 copy.81
  28.0 0.2 copy.80
  28.3 1.9 %collective-permute-start.3 = (f32[73,16,3]{0,1,2:T(8,128)S(1)}, f32[73,16,3]{0,1,2:T(8,128)S(1)}, u32[]{:S(2)}, u32[]{:S(2)}) collective-permute-start(f32[73,16,3]{0,1,2:T(8,128)S(1)} %pad_maximum_fusion.7), channel_id=1, source_target_pairs={{1,0},{2,1},{3,2},{4,3},{5,4},{6,5},{7,6},{8,7},{9,8},{10,9},{11,1... | collective-permute-start | bytes 42056 | tf_op jit(solution)/shard_map/ppermute | solution.py:25
  30.2 0.9 %pad_maximum_fusion.4 = (f32[24,16,256]{2,1,0:T(8,128)S(1)}, f32[24,16,256]{2,1,0:T(8,128)}) fusion(f32[24,16,256]{2,1,0:T(8,128)S(1)} %copy-done.1, f32[4,16,256]{2,1,0:T(8,128)S(1)} %slice.438, f32[24,16,256]{2,1,0:T(8,128)S(1)} %copy-done.2, f32[24]{0:T(128)S(1)} %get-tuple-element.71), kind=kLoop, calls=%fused_computation.108 | loop fusion | flops 393216 | bytes 1638496 | tf_op jit(solution)/shard_map/concatenate | solution.py:145
  31.1 0.7 slice_bitcast_fusion.8
  31.8 0.2 copy.85
  32.0 5.6 %collective-permute-done.3 = f32[73,16,3]{0,1,2:T(8,128)S(1)} collective-permute-done((f32[73,16,3]{0,1,2:T(8,128)S(1)}, f32[73,16,3]{0,1,2:T(8,128)S(1)}, u32[]{:S(2)}, u32[]{:S(2)}) %collective-permute-start.3) | collective-permute-done | bytes 14048 | tf_op jit(solution)/shard_map/ppermute | solution.py:25
  37.7 0.2 copy.86
  38.0 0.2 copy.87
  38.3 0.2 copy.88
  38.7 0.1 copy.83
  38.9 0.1 copy.84
  39.1 0.2 pad_maximum_fusion.5
  39.2 0.6 gather_fusion
  40.0 0.3 pad_maximum_fusion
  40.3 0.4 fusion.63
  40.7 1.7 %fusion.79 = (f32[28,16,260]{2,1,0:T(8,128)S(1)}, f32[28,16,260]{2,1,0:T(8,128)S(1)}, f32[28,16,260]{2,1,0:T(8,128)}, f32[28,16,260]{2,1,0:T(8,128)}) fusion(f32[31,16,262]{2,1,0:T(8,128)S(1)} %pad_maximum_fusion, f32[30,16,262]{2,1,0:T(8,128)S(1)} %get-tuple-element.34, f32[28]{0:T(128)S(1)} %copy-done.9), kind=kLoop, calls=%fused_computation.175 | loop fusion | flops 349440 | bytes 3261552 | tf_op jit(solution)/shard_map/slice | solution.py:99
  42.5 2.1 %fusion.78 = (f32[26,16,258]{2,1,0:T(8,128)}, f32[26,16,258]{2,1,0:T(8,128)}, f32[26,16,258]{2,1,0:T(8,128)}, f32[26,16,258]{2,1,0:T(8,128)}) fusion(f32[31,16,262]{2,1,0:T(8,128)S(1)} %pad_maximum_fusion, f32[30,16,262]{2,1,0:T(8,128)S(1)} %get-tuple-element.34, f32[26]{0:T(128)S(1)} %copy-done.10), kind=kLoop, calls=%fused_computation.174 | loop fusion | flops 321984 | bytes 3005288 | tf_op jit(solution)/shard_map/slice | solution.py:99
  44.6 3.9 %divide_multiply_fusion = (f32[4,30,16,262]{3,2,1,0:T(8,128)S(1)}, f32[4,30,16,262]{3,2,1,0:T(8,128)}) fusion(f32[30,262]{1,0:T(8,128)S(1)} %copy-done.5, f32[30,16,262]{2,1,0:T(8,128)S(1)} %get-tuple-element.33, f32[30]{0:T(128)S(1)} %copy-done.12, f32[4,16,262]{2,1,0:T(8,128)S(1)} %get-tuple-element.54, f32[30]{0:T(128)S(1)} %copy-done.13, ...), kind=kLoop, calls=%fused_computation.21 | loop fusion | flops 12072960 | bytes 4827688 | tf_op jit(solution)/shard_map/mul | solution.py:191
  48.5 8.6 %fusion.20 = f32[4,28,16,260]{3,2,1,0:T(8,128)S(1)} fusion(f32[4,30,16,262]{3,2,1,0:T(8,128)S(1)} %get-tuple-element.49, f32[4,30,16,262]{3,2,1,0:T(8,128)} %get-tuple-element.50, f32[28,260]{1,0:T(8,128)S(1)} %slice_bitcast_fusion.4, f32[28,16,260]{2,1,0:T(8,128)S(1)} %get-tuple-element.39, f32[28,16,260]{2,1,0:T(8,128)} %get-tuple-element.41, ...), kind=kLoop, calls=%fused_computation.46 | loop fusion | flops 12113920 | bytes 22797424 | tf_op jit(solution)/shard_map/mul | solution.py:205
  57.1 8.6 %fusion.41 = f32[4,26,16,258]{3,2,1,0:T(8,128)S(1)} fusion(f32[4,28,16,260]{3,2,1,0:T(8,128)S(1)} %fusion.20, f32[4,30,16,262]{3,2,1,0:T(8,128)} %get-tuple-element.50, f32[26,258]{1,0:T(8,128)} %slice_bitcast_fusion.3, f32[26,16,258]{2,1,0:T(8,128)} %get-tuple-element.36, f32[26,16,258]{2,1,0:T(8,128)} %get-tuple-element.42, ...), kind=kLoop, calls=%fused_computation.70 | loop fusion | flops 11162112 | bytes 20710920 | tf_op jit(solution)/shard_map/mul | solution.py:205
  65.7 5.0 %fusion.64 = (f32[16,256]{1,0:T(8,128)S(1)}, f32[24,16,256]{2,1,0:T(8,128)S(1)}, f32[4,24,16,256]{3,2,1,0:T(8,128)}) fusion(f32[4,30,16,262]{3,2,1,0:T(8,128)S(1)} %copy-done, f32[24,16,256]{2,1,0:T(8,128)S(1)} %copy-done.3, f32[24,16,256]{2,1,0:T(8,128)S(1)} %copy-done.2, f32[4,26,16,258]{3,2,1,0:T(8,128)S(1)} %fusion.41, ...), kind=kLoop, calls=%fused_computation.104 | loop fusion | flops 10907648 | bytes 15549952 | tf_op jit(solution)/shard_map/reduce_sum | solution.py:208
  70.8 0.7 broadcast_in_dim.17
  71.4 3.8 %all-to-all-start = ((f32[8,16,256]{2,1,0:T(8,128)}), f32[8,16,256]{2,1,0:T(8,128)S(1)}, u32[]{:S(2)}, u32[]{:S(2)}) async-start(f32[8,16,256]{2,1,0:T(8,128)} %broadcast_in_dim.17), calls=%async_computation | async-start | bytes 262144 | tf_op jit(solution)/shard_map/all_to_all | solution.py:209
  75.2 4.4 %all-to-all-done = f32[8,16,256]{2,1,0:T(8,128)S(1)} async-done(((f32[8,16,256]{2,1,0:T(8,128)}), f32[8,16,256]{2,1,0:T(8,128)S(1)}, u32[]{:S(2)}, u32[]{:S(2)}) %all-to-all-start) | async-done | bytes 131104 | tf_op jit(solution)/shard_map/all_to_all | solution.py:209
  79.7 0.8 fusion.62
  (63 shorter events, 1.4 us)
Async XLA Ops:
  0.6 20.1 %copy-start.2 = (f32[24,16,256]{2,1,0:T(8,128)S(1)}, f32[24,16,256]{2,1,0:T(8,128)}, u32[]{:S(2)}) copy-start(f32[24,16,256]{2,1,0:T(8,128)} %param.14) | copy-start | bytes 1179652
  3.2 12.6 %collective-permute-start = (f32[8,16,256]{2,1,0:T(8,128)S(1)}, f32[8,16,256]{2,1,0:T(8,128)S(1)}, u32[]{:S(2)}, u32[]{:S(2)}) collective-permute-start(f32[8,16,256]{2,1,0:T(8,128)S(1)} %select_maximum_fusion), channel_id=1, source_target_pairs={{0,64},{64,128},{128,192},{192,256},{256,320},{320,384},{384,448},... | collective-permute-start | bytes 393224 | tf_op jit(solution)/shard_map/ppermute | solution.py:25
  7.1 8.7 %collective-permute-start.1 = (f32[7,16,256]{2,1,0:T(8,128)S(1)}, f32[7,16,256]{2,1,0:T(8,128)S(1)}, u32[]{:S(2)}, u32[]{:S(2)}) collective-permute-start(f32[7,16,256]{2,1,0:T(8,128)S(1)} %select_maximum_fusion.1), channel_id=1, source_target_pairs={{64,0},{128,64},{192,128},{256,192},{320,256},{384,320},{448,384},... | collective-permute-start | bytes 344072 | tf_op jit(solution)/shard_map/ppermute | solution.py:25
  19.3 10.9 %copy-start.1 = (f32[24,16,256]{2,1,0:T(8,128)S(1)}, f32[24,16,256]{2,1,0:T(8,128)}, u32[]{:S(2)}) copy-start(f32[24,16,256]{2,1,0:T(8,128)} %param.15) | copy-start | bytes 1179652
  20.8 18.3 %copy-start.4 = (f32[4,3,16,256]{3,2,1,0:T(8,128)S(1)}, f32[4,3,16,256]{3,2,1,0:T(8,128)}, u32[]{:S(2)}) copy-start(f32[4,3,16,256]{3,2,1,0:T(8,128)} %param.11) | copy-start | bytes 589828
  21.2 10.5 %collective-permute-start.2 = (f32[73,16,3]{0,1,2:T(8,128)S(1)}, f32[73,16,3]{0,1,2:T(8,128)S(1)}, u32[]{:S(2)}, u32[]{:S(2)}) collective-permute-start(f32[73,16,3]{0,1,2:T(8,128)S(1)} %pad_maximum_fusion.6), channel_id=1, source_target_pairs={{0,1},{1,2},{2,3},{3,4},{4,5},{5,6},{6,7},{7,8},{8,9},{9,10},{10,1... | collective-permute-start | bytes 42056 | tf_op jit(solution)/shard_map/ppermute | solution.py:25
  28.3 9.4 %collective-permute-start.3 = (f32[73,16,3]{0,1,2:T(8,128)S(1)}, f32[73,16,3]{0,1,2:T(8,128)S(1)}, u32[]{:S(2)}, u32[]{:S(2)}) collective-permute-start(f32[73,16,3]{0,1,2:T(8,128)S(1)} %pad_maximum_fusion.7), channel_id=1, source_target_pairs={{1,0},{2,1},{3,2},{4,3},{5,4},{6,5},{7,6},{8,7},{9,8},{10,9},{11,1... | collective-permute-start | bytes 42056 | tf_op jit(solution)/shard_map/ppermute | solution.py:25
  40.0 0.8 copy-start.9
  40.7 1.8 %copy-start.10 = (f32[26]{0:T(128)S(1)}, f32[26]{0:T(128)}, u32[]{:S(2)}) copy-start(f32[26]{0:T(128)} %get-tuple-element.74) | copy-start | bytes 316
  42.4 2.1 %copy-start.5 = (f32[30,262]{1,0:T(8,128)S(1)}, f32[30,262]{1,0:T(8,128)}, u32[]{:S(2)}) copy-start(f32[30,262]{1,0:T(8,128)} %and_convert_fusion.1) | copy-start | bytes 94324
  42.4 2.1 %copy-start.11 = (f32[30]{0:T(128)S(1)}, f32[30]{0:T(128)}, u32[]{:S(2)}) copy-start(f32[30]{0:T(128)} %get-tuple-element.65) | copy-start | bytes 364
  42.4 2.1 %copy-start.12 = (f32[30]{0:T(128)S(1)}, f32[30]{0:T(128)}, u32[]{:S(2)}) copy-start(f32[30]{0:T(128)} %get-tuple-element.66) | copy-start | bytes 364
  42.4 2.1 %copy-start.13 = (f32[30]{0:T(128)S(1)}, f32[30]{0:T(128)}, u32[]{:S(2)}) copy-start(f32[30]{0:T(128)} %get-tuple-element.67) | copy-start | bytes 364
  42.4 2.1 %copy-start.14 = (f32[30]{0:T(128)S(1)}, f32[30]{0:T(128)}, u32[]{:S(2)}) copy-start(f32[30]{0:T(128)} %get-tuple-element.68) | copy-start | bytes 364
  42.4 2.1 %copy-start.15 = (f32[30]{0:T(128)S(1)}, f32[30]{0:T(128)}, u32[]{:S(2)}) copy-start(f32[30]{0:T(128)} %get-tuple-element.69) | copy-start | bytes 364
  57.0 8.7 %copy-start = (f32[4,30,16,262]{3,2,1,0:T(8,128)S(1)}, f32[4,30,16,262]{3,2,1,0:T(8,128)}, u32[]{:S(2)}) copy-start(f32[4,30,16,262]{3,2,1,0:T(8,128)} %get-tuple-element.50) | copy-start | bytes 6036484
  57.0 8.7 %copy-start.3 = (f32[24,16,256]{2,1,0:T(8,128)S(1)}, f32[24,16,256]{2,1,0:T(8,128)}, u32[]{:S(2)}) copy-start(f32[24,16,256]{2,1,0:T(8,128)} %get-tuple-element.48) | copy-start | bytes 1179652
  57.1 8.7 %copy-start.6 = (f32[24]{0:T(128)S(1)}, f32[24]{0:T(128)}, u32[]{:S(2)}) copy-start(f32[24]{0:T(128)} %get-tuple-element.70) | copy-start | bytes 292
  57.1 8.7 %copy-start.7 = (f32[24]{0:T(128)S(1)}, f32[24]{0:T(128)}, u32[]{:S(2)}) copy-start(f32[24]{0:T(128)} %get-tuple-element.72) | copy-start | bytes 292
  57.1 8.7 %copy-start.8 = (f32[24]{0:T(128)S(1)}, f32[24]{0:T(128)}, u32[]{:S(2)}) copy-start(f32[24]{0:T(128)} %get-tuple-element.81) | copy-start | bytes 292
  71.4 8.1 %all-to-all-start = ((f32[8,16,256]{2,1,0:T(8,128)}), f32[8,16,256]{2,1,0:T(8,128)S(1)}, u32[]{:S(2)}, u32[]{:S(2)}) async-start(f32[8,16,256]{2,1,0:T(8,128)} %broadcast_in_dim.17), calls=%async_computation | async-start | bytes 262144 | tf_op jit(solution)/shard_map/all_to_all | solution.py:209
